TPU v7x, 256 devices: a whole 4x4x8 slice. The times are simulated.
256 devices in a mesh: ctx: 32 (over y, x, core), head: 8 (over z).
Axes of the slice: x: 4, y: 4, z: 8, core: 2. Of those that a mesh axis runs over, the one named last changes fastest.
Arguments:
- query_vectors: bfloat16 [4096, 4096], P('ctx', 'head'), may hold values from -6 to 6
- key_vectors: bfloat16 [4096, 4096], P('ctx', 'head'), may hold values from -1.5 to 1.5
- value_vectors: bfloat16 [4096, 4096], P('ctx', 'head'), may hold values from -6 to 6
- log_decay: float32 [32, 4096], P('head', 'ctx'), may hold values from -2 to 0, as said below
- residual: bfloat16 [4096, 3072], P('ctx'), may hold values from -6 to 6
- out_weight: bfloat16 [4096, 3072], P('head', 'ctx'), may hold values from -0.09375 to 0.09375
- attn_gain: float32 [4096], P('head'), may hold values from 0.1 to 1.9
- moe_gain: float32 [3072], replicated, may hold values from 0.1 to 1.9
- router: float32 [3072, 32], replicated, may hold values from -0.109375 to 0.109375
- w_gate: bfloat16 [32, 3072, 4608], P('ctx', None, 'head'), may hold values from -0.109375 to 0.109375
- w_up: bfloat16 [32, 3072, 4608], P('ctx', None, 'head'), may hold values from -0.109375 to 0.109375
- w_down: bfloat16 [32, 4608, 3072], P('ctx', 'head'), may hold values from -0.09375 to 0.09375
- expert_ids: int32 [4096, 2], P('ctx'), may hold values from 0 to 31, all different within a row; in each aligned block of 128 rows (0 to 127, 128 to 255, ...) at most 16 rows name the same one
Outputs:
- final_out: bfloat16 [4096, 3072], P('ctx', 'head')
Inputs may be any that keep to these rules, and one draw needn't show every extreme that they name: `expert_ids`: each row names 2 different experts. In each aligned block of 128 rows no expert is named by more than 16 rows, and in every draw some expert is named by exactly 16 rows of some block. `log_decay`: every entry is negative.
All inputs are finite; a program needn't handle non-finite values.
Results may differ from a plain program's by a relative error of at most 0.022.
Values may be sent and summed in bfloat16 or wider, within the bound.
No kernel may reach another device: no remote copies, remote signals or barrier semaphores. Data moves between devices by JAX's collectives and lax.ppermute only.
A program may use at most 128 MiB of HBM per device.

v0:
```python
import jax
import jax.numpy as jnp
from jax import lax
from jax.sharding import PartitionSpec as P

TOP = 2


PRECISE = lax.Precision.HIGHEST


def entering(value, axis, combine, identity):
    peers, index = (lax.axis_size(axis), lax.axis_index(axis))
    everything = jax.tree.map(
        lambda part, kind: lax.all_gather(part.astype(kind), axis),
        value,
        (jnp.bfloat16, jnp.bfloat16),
    )
    start = jax.tree.map(
        lambda part, zero: jnp.broadcast_to(jnp.asarray(zero, part.dtype), part.shape),
        value,
        identity,
    )

    def step(k, before):
        reached = k < index
        new = combine(
            before, jax.tree.map(lambda part, own: part[k].astype(own.dtype), everything, value)
        )
        return jax.tree.map(lambda a, b: jnp.where(reached, a, b), new, before)

    return lax.fori_loop(0, peers, step, start)


def local_attention(query_block, key_block, value_block, decay_block):
    running = jnp.cumsum(decay_block, axis=1)
    length_here = decay_block.shape[1]
    row_index = lax.broadcasted_iota(jnp.int32, (length_here, length_here), 0)
    col_index = lax.broadcasted_iota(jnp.int32, (length_here, length_here), 1)
    causal = (col_index <= row_index)[None]
    spread = jnp.where(causal, running[:, :, None] - running[:, None, :], 0.0)
    decay_weights = jnp.where(causal, jnp.exp(spread), 0.0)
    scores = jnp.einsum("htd,hsd->hts", query_block, key_block, precision=PRECISE) * decay_weights
    inside_part = jnp.einsum("hts,hse->hte", scores, value_block, precision=PRECISE)
    final_log = running[:, -1]
    tail_decay = jnp.exp(final_log[:, None] - running)
    local_state = jnp.einsum(
        "hsd,hse->hde", key_block * tail_decay[:, :, None], value_block, precision=PRECISE
    )
    return (inside_part, running, local_state, final_log)


def route_tokens(logits, expert_ids, experts_total):
    onehot = expert_ids[:, :, None] == lax.broadcasted_iota(jnp.int32, (1, 1, experts_total), 2)
    chosen = jnp.sum(jnp.where(onehot, logits[:, None, :], 0.0), axis=2)
    leading = jax.nn.sigmoid(chosen[:, 0] - chosen[:, 1])
    gate_weights = jnp.stack([leading, 1.0 - leading], axis=1)
    marked = onehot.reshape(-1, experts_total).astype(jnp.int32)
    earlier = jnp.cumsum(marked, axis=0) - marked
    slot_index = jnp.sum(earlier * marked, axis=1).reshape(expert_ids.shape)
    return (gate_weights, slot_index)


def link_states(earlier, later):
    return (earlier[0] + later[0], jnp.exp(later[0])[:, None, None] * earlier[1] + later[1])


def body(
    query_vectors,
    key_vectors,
    value_vectors,
    log_decay,
    residual,
    out_weight,
    attn_gain,
    moe_gain,
    router,
    w_gate,
    w_up,
    w_down,
    expert_ids,
):
    token_count = query_vectors.shape[0]
    heads_here = log_decay.shape[0]
    head_size = query_vectors.shape[1] // heads_here

    def split_heads(matrix_in):
        return (
            matrix_in.astype(jnp.float32)
            .reshape(token_count, heads_here, head_size)
            .transpose(1, 0, 2)
        )

    query_heads = split_heads(query_vectors)
    inside_part, running, local_state, final_log = local_attention(
        query_heads, split_heads(key_vectors), split_heads(value_vectors), log_decay
    )
    identity = (jnp.zeros_like(final_log), jnp.zeros_like(local_state))
    _, prior_state = entering((final_log, local_state), "ctx", link_states, identity)
    outside_part = jnp.exp(running)[:, :, None] * jnp.einsum(
        "htd,hde->hte", query_heads, prior_state, precision=PRECISE
    )
    attended = inside_part + outside_part
    square_mean = jnp.mean(attended * attended, axis=2, keepdims=True)
    heads_normed = (
        attended * lax.rsqrt(square_mean + 1e-05) * attn_gain.reshape(heads_here, 1, head_size)
    )
    heads_normed = (
        heads_normed.astype(jnp.bfloat16)
        .transpose(1, 0, 2)
        .reshape(token_count, heads_here * head_size)
    )
    partial_out = jnp.dot(
        heads_normed,
        lax.all_gather(out_weight, "ctx", axis=1, tiled=True),
        preferred_element_type=jnp.float32,
    )
    model_width = residual.shape[1]
    experts_total = router.shape[1]
    capacity = 2 * token_count * TOP // experts_total
    slice_width = model_width // lax.axis_size("head")
    slice_start = lax.axis_index("head") * slice_width
    projected = lax.psum(partial_out.astype(jnp.bfloat16), "head").astype(jnp.float32)
    mixed_rows = (residual.astype(jnp.float32) + projected).astype(jnp.bfloat16)
    mixed_wide = mixed_rows.astype(jnp.float32)
    inv_rms = lax.rsqrt(jnp.mean(mixed_wide * mixed_wide, axis=1, keepdims=True) + 1e-06)
    scaled = mixed_wide * moe_gain[None, :]
    moe_in = (scaled * inv_rms).astype(jnp.bfloat16)
    logits = inv_rms * jnp.dot(scaled, router, precision=PRECISE)
    base_slice = lax.dynamic_slice_in_dim(mixed_wide, slice_start, slice_width, 1)
    gate_weights, slot_index = route_tokens(logits, expert_ids, experts_total)
    target = (expert_ids * capacity + slot_index).reshape(-1)
    width_here = moe_in.shape[1]
    source = jnp.repeat(moe_in, TOP, axis=0)
    packed = jnp.zeros((experts_total * capacity, width_here), jnp.bfloat16).at[target].set(source)
    arrived = lax.all_to_all(
        packed.reshape(experts_total, capacity, width_here),
        "ctx",
        split_axis=0,
        concat_axis=0,
        tiled=True,
    )
    flat_rows = arrived.reshape(-1, model_width)
    gate_part = jnp.dot(flat_rows, w_gate[0], preferred_element_type=jnp.float32)
    up_part = jnp.dot(flat_rows, w_up[0], preferred_element_type=jnp.float32)
    hidden = (jax.nn.silu(gate_part) * up_part).astype(jnp.bfloat16)
    partial_down = jnp.dot(hidden, w_down[0], preferred_element_type=jnp.float32).reshape(
        arrived.shape
    )
    returned = lax.all_to_all(
        lax.all_to_all(
            partial_down.astype(jnp.bfloat16)[None], "ctx", split_axis=1, concat_axis=1, tiled=True
        ),
        "head",
        split_axis=3,
        concat_axis=0,
        tiled=True,
    )
    expert_out = jnp.sum(returned.astype(jnp.float32), axis=0).astype(jnp.bfloat16)
    lookup = expert_out.reshape(experts_total * capacity, slice_width)
    picked = lookup[target].reshape(token_count, TOP, slice_width).astype(jnp.float32)
    final_out = (
        base_slice + gate_weights[:, 0:1] * picked[:, 0] + gate_weights[:, 1:2] * picked[:, 1]
    )
    return final_out.astype(jnp.bfloat16)


def solution(mesh):
    in_specs = (
        P("ctx", "head"),
        P("ctx", "head"),
        P("ctx", "head"),
        P("head", "ctx"),
        P("ctx", None),
        P("head", "ctx"),
        P("head"),
        P(),
        P(),
        P("ctx", None, "head"),
        P("ctx", None, "head"),
        P("ctx", "head", None),
        P("ctx", None),
    )
    out_specs = P("ctx", "head")
    return jax.shard_map(body, mesh=mesh, in_specs=in_specs, out_specs=out_specs, check_vma=False)
```

profile of v0, /device:TPU:1, one launch (start us, length us, event | category | flops | bytes accessed | tf_op | source)
XLA Modules:
  0.0 512.6 jit_solution(2315523512978640934)
XLA Ops:
  9.6 1.9 convolution_convert_fusion.2
  16.8 65.8 %all-reduce = bf16[128]{0:T(256)(128)(2,1)S(1)} all-reduce(bf16[128]{0:T(256)(128)(2,1)} %dynamic-update-slice), channel_id=2, replica_groups=mesh['ctx'=32,'head'=8] {'ctx'}, use_global_device_ids=true, to_apply=%add | all-reduce | flops 128 | bytes 512
  86.3 1.8 convolution_multiply_fusion
  88.1 78.5 %while.14 = (s32[]{:T(128)}, f32[4,128,128]{2,1,0:T(8,128)}, s32[]{:T(128)}, bf16[32,4]{1,0:T(8,128)(2,1)}, bf16[32,4,128,128]{3,2,1,0:T(8,128)(2,1)}, /*index=5*/s32[]{:T(128)}, s32[]{:T(128)}) while((s32[]{:T(128)}, f32[4,128,128]{2,1,0:T(8,128)}, s32[]{:T(128)}, bf16[32,4]{1,0:T(8,128)(2,1)}, ...), condition=%wide.region_2.3_spmd.clone, body=%wide.region_1.2_spmd.clone.sunk | while | flops 327688 | bytes 655513 | solution.py:32
  91.2 1.8 fusion.63
  96.2 1.8 fusion.63
  98.6 1.8 fusion.63
  101.1 1.8 fusion.63
  103.6 1.8 fusion.63
  106.1 1.8 fusion.63
  108.5 1.8 fusion.63
  111.0 1.8 fusion.63
  113.5 1.8 fusion.63
  116.0 1.8 fusion.63
  123.3 1.8 fusion.63
  125.8 1.8 fusion.63
  128.3 1.8 fusion.63
  133.2 1.8 fusion.63
  135.6 1.8 fusion.63
  138.1 1.8 fusion.63
  143.0 1.8 fusion.63
  145.5 1.8 fusion.63
  150.3 1.8 fusion.63
  152.7 1.8 fusion.63
  157.6 1.8 fusion.63
  160.0 1.8 fusion.63
  170.9 4.0 convolution_convert_fusion.1
  177.8 1.9 reduce-window.6
  192.9 53.1 %all-reduce.3.cloned.1.call-done = bf16[128,3072]{1,0:T(8,128)(2,1)} async-done(((bf16[128,3072]{1,0:T(8,128)(2,1)}), bf16[128,3072]{1,0:T(8,128)(2,1)}) %all-reduce.3.cloned.1.call-update) | async-done | bytes 786448 | tf_op jit(solution)/shard_map/psum | solution.py:123
  246.0 2.8 fusion.47
  250.5 2.0 broadcast_in_dim.60
  252.4 4.6 reshape.182
  257.0 5.8 %scatter_custom_fusion = bf16[512,3072]{1,0:T(8,128)(2,1)} fusion(s32[256]{0:T(256)} %bitcast.159, bf16[256,3072]{1,0:T(8,128)(2,1)} %reshape.182, bf16[]{:T(256)} %constant.66.clone.1), kind=kCustom, calls=%fused_computation.14 | custom fusion | bytes 3146240 | tf_op jit(solution)/shard_map/scatter | solution.py:135
  262.8 51.8 %all_to_all.22 = bf16[32,16,3072]{2,1,0:T(8,128)(2,1)S(1)} all-to-all(bf16[32,16,3072]{2,1,0:T(8,128)(2,1)} %bitcast.150), channel_id=1, replica_groups=mesh['ctx'=32,'head'=8] {'ctx'}, dimensions={0} | all-to-all | bytes 6291456 | tf_op jit(solution)/shard_map/all_to_all | solution.py:136
  314.6 2.0 fusion.5
  316.6 3.0 fusion.14
  319.6 2.1 copy.104
  321.7 3.9 fusion.1
  325.7 43.1 %all_to_all.23 = bf16[1,32,16,3072]{3,2,0,1:T(8,128)(2,1)S(1)} all-to-all(bf16[1,32,16,3072]{3,2,0,1:T(8,128)(2,1)S(1)} %fusion.1), channel_id=1, replica_groups=mesh['ctx'=32,'head'=8] {'ctx'}, dimensions={1} | all-to-all | bytes 6291456 | tf_op jit(solution)/shard_map/all_to_all | solution.py:151
  368.8 13.4 %copy.106 = bf16[1,32,16,3072]{1,2,0,3:T(8,128)(2,1)} copy(bf16[1,32,16,3072]{3,2,0,1:T(8,128)(2,1)S(1)} %all_to_all.23) | data formatting | bytes 6291456 | tf_op jit(solution)/shard_map/all_to_all | solution.py:151
  382.1 14.5 %reshape.201 = bf16[8,2,98304]{2,1,0:T(2,128)(2,1)} reshape(bf16[3072,1,16,32]{3,2,1,0:T(8,128)(2,1)} %bitcast.149) | data formatting | bytes 6291456
  396.7 4.8 all-to-all-start.2
  403.7 72.0 %all-to-all-done.2 = bf16[8,2,98304]{2,1,0:T(2,128)(2,1)} async-done(((bf16[8,2,98304]{2,1,0:T(2,128)(2,1)}), bf16[8,2,98304]{2,1,0:T(2,128)(2,1)}, u32[]{:S(2)}, u32[]{:S(2)}) %all-to-all-start.2) | async-done | bytes 3145760 | tf_op jit(solution)/shard_map/all_to_all | solution.py:150
  475.7 10.6 %reshape.202 = bf16[3072,1,16,32]{3,2,1,0:T(8,128)(2,1)} reshape(bf16[8,2,98304]{2,1,0:T(2,128)(2,1)} %all-to-all-done.2) | data formatting | bytes 6291456
  486.3 8.9 %reduce_sum.52 = bf16[32,16,384]{0,1,2:T(8,128)(2,1)} reduce(bf16[32,16,8,384]{0,1,3,2:T(8,128)(2,1)} %bitcast.148, bf16[]{:T(256)} %constant.66.clone.1), dimensions={2}, to_apply=%region_11.12 | reduce | flops 1376256 | bytes 3538946 | tf_op jit(solution)/shard_map/reduce_sum | solution.py:159
  495.2 2.9 copy.108
  498.1 3.0 gather_fusion
  501.1 1.9 reshape.169
  (112 shorter events, 77.9 us)
Async XLA Ops:
  6.5 315.2 %copy-start = (bf16[1,576,3072]{2,1,0:T(8,128)(2,1)S(1)}, bf16[1,576,3072]{2,1,0:T(8,128)(2,1)}, u32[]{:S(2)}) copy-start(bf16[1,576,3072]{2,1,0:T(8,128)(2,1)} %param.26) | copy-start | bytes 10616836
  6.5 81.6 %all-gather.7.cloned.1.call-start = ((), (), s32[]{:S(2)}) async-start(), calls=%async_computation.5 | async-start | bytes 4325376 | tf_op jit(solution)/shard_map/all_gather | solution.py:15
  11.5 159.4 %all-gather.5.cloned.1.call-start = ((), (), s32[]{:S(2)}) async-start(), calls=%async_computation.3 | async-start | bytes 3244032 | tf_op jit(solution)/shard_map/all_gather | solution.py:115
  12.2 233.8 %all-reduce.3.cloned.1.call-start = ((), (), s32[]{:S(2)}) async-start(), calls=%async_computation.4 | async-start | bytes 1572864 | tf_op jit(solution)/shard_map/psum | solution.py:123
  169.4 18.0 %copy-start.6 = (s32[128,2]{0,1:T(2,128)S(1)}, s32[128,2]{0,1:T(2,128)}, u32[]{:S(2)}) copy-start(s32[128,2]{0,1:T(2,128)} %param.27) | copy-start | bytes 3076
  174.9 75.3 %copy-start.5 = (f32[3072]{0:T(1024)S(1)}, f32[3072]{0:T(1024)}, u32[]{:S(2)}) copy-start(f32[3072]{0:T(1024)} %param.22) | copy-start | bytes 36868
  248.8 0.9 copy-start.2
  249.6 0.6 copy-start.8
  262.8 51.8 %copy-start.10 = (bf16[1,3072,576]{1,2,0:T(8,128)(2,1)S(1)}, bf16[1,3072,576]{1,2,0:T(8,128)(2,1)}, u32[]{:S(2)}) copy-start(bf16[1,3072,576]{1,2,0:T(8,128)(2,1)} %param.24) | copy-start | bytes 10616836
  314.6 2.0 copy-start.11
  396.6 4.9 copy-start.7
  396.6 5.5 %copy-start.3 = (bf16[128,3072]{1,0:T(8,128)(2,1)S(1)}, bf16[128,3072]{1,0:T(8,128)(2,1)}, u32[]{:S(2)}) copy-start(bf16[128,3072]{1,0:T(8,128)(2,1)} %copy-done.2) | copy-start | bytes 2359300
  396.6 5.5 %copy-start.4 = (f32[3072,32]{0,1:T(8,128)S(1)}, f32[3072,32]{0,1:T(8,128)}, u32[]{:S(2)}) copy-start(f32[3072,32]{0,1:T(8,128)} %param.23) | copy-start | bytes 1179652
  396.6 5.5 %copy-start.9 = (f32[128]{0:T(128)S(1)}, f32[128]{0:T(128)}, u32[]{:S(2)}) copy-start(f32[128]{0:T(128)} %copy-done.8) | copy-start | bytes 1540
  396.7 79.0 %all-to-all-start.2 = ((bf16[8,2,98304]{2,1,0:T(2,128)(2,1)}), bf16[8,2,98304]{2,1,0:T(2,128)(2,1)}, u32[]{:S(2)}, u32[]{:S(2)}) async-start(bf16[8,2,98304]{2,1,0:T(2,128)(2,1)} %reshape.201), calls=%async_computation.2 | async-start | bytes 6291456 | tf_op jit(solution)/shard_map/all_to_all | solution.py:150
  486.3 19.8 %copy-start.1 = (bf16[1,576,3072]{2,1,0:T(8,128)(2,1)S(1)}, bf16[1,576,3072]{2,1,0:T(8,128)(2,1)}, u32[]{:S(2)}) copy-start(bf16[1,576,3072]{2,1,0:T(8,128)(2,1)} %param.26) | copy-start | bytes 10616836
Sparse Core Ops, SparseCore 0:
  11.6 55.2 all-gather.6
  69.4 49.3 all-gather.4
  175.1 70.9 all-reduce.2
where the time goes:
time: 516 us; the launch traced here: 513 us
  blocking collectives  161 us (31%)
  waiting for transfers between devices  126 us (24%)
  other arithmetic  104 us (20%)
  local copies, waits for them, and re-layouts  81.8 us (16%)
  matrix products  21 us (4%)
  between operations  13.9 us (3%)
    all_to_all x1, waiting for transfers between devices, body(): lax.all_to_all(lax.all_to_all(partial_down.astype(jnp.bfloat16)[None], 'c...  72 us
    unnamed x1, blocking collectives  65.8 us
    select_n x32, other arithmetic, step(): return jax.tree.map(lambda a, b: jnp.where(reached, a, b), new, before)  56.9 us
    psum x1, waiting for transfers between devices, body(): lax.psum(partial_out.astype(jnp.bfloat16), 'head').astype(jnp.float32)  53.1 us
    all_to_all x1, blocking collectives, body(): lax.all_to_all(packed.reshape(experts_total, capacity, width_here), 'ctx'...  51.8 us
    all_to_all x1, blocking collectives, body(): lax.all_to_all(partial_down.astype(jnp.bfloat16)[None], 'ctx', split_axis...  43.1 us
    unnamed x30, local copies, waits for them, and re-layouts  30.8 us
    exp x32, other arithmetic, link_states(): jnp.exp(later[0])[:, None, None] * earlier[1] + later[1]  21.5 us
  transfers between devices with their start and end apart: 4, of which 2 were waited for; matrix products, arithmetic and copies ran while one was open for 22% of the time, Pallas kernels for 0%

commit v1 on v0

--- a/solution.py
+++ b/solution.py
@@ -9,27 +9,19 @@
 PRECISE = lax.Precision.HIGHEST
 
 
-def entering(value, axis, combine, identity):
-    peers, index = (lax.axis_size(axis), lax.axis_index(axis))
-    everything = jax.tree.map(
-        lambda part, kind: lax.all_gather(part.astype(kind), axis),
-        value,
-        (jnp.bfloat16, jnp.bfloat16),
+def prior_states(final_log, local_state, axis):
+    index = lax.axis_index(axis)
+    totals = lax.all_gather(final_log, axis)
+    states = lax.all_gather(local_state.astype(jnp.bfloat16), axis)
+    peers = totals.shape[0]
+    source = lax.broadcasted_iota(jnp.int32, (peers, peers), 0)
+    between = lax.broadcasted_iota(jnp.int32, (peers, peers), 1)
+    inside = (between > source) & (between < index)
+    spans = jnp.sum(jnp.where(inside[:, :, None], totals[None, :, :], 0.0), axis=1)
+    weights = jnp.where(jnp.arange(peers)[:, None] < index, jnp.exp(spans), 0.0)
+    return jnp.einsum(
+        "jh,jhde->hde", weights, states.astype(jnp.float32), precision=PRECISE
     )
-    start = jax.tree.map(
-        lambda part, zero: jnp.broadcast_to(jnp.asarray(zero, part.dtype), part.shape),
-        value,
-        identity,
-    )
-
-    def step(k, before):
-        reached = k < index
-        new = combine(
-            before, jax.tree.map(lambda part, own: part[k].astype(own.dtype), everything, value)
-        )
-        return jax.tree.map(lambda a, b: jnp.where(reached, a, b), new, before)
-
-    return lax.fori_loop(0, peers, step, start)
 
 
 def local_attention(query_block, key_block, value_block, decay_block):
@@ -59,10 +51,6 @@
     earlier = jnp.cumsum(marked, axis=0) - marked
     slot_index = jnp.sum(earlier * marked, axis=1).reshape(expert_ids.shape)
     return (gate_weights, slot_index)
-
-
-def link_states(earlier, later):
-    return (earlier[0] + later[0], jnp.exp(later[0])[:, None, None] * earlier[1] + later[1])
 
 
 def body(
@@ -95,8 +83,7 @@
     inside_part, running, local_state, final_log = local_attention(
         query_heads, split_heads(key_vectors), split_heads(value_vectors), log_decay
     )
-    identity = (jnp.zeros_like(final_log), jnp.zeros_like(local_state))
-    _, prior_state = entering((final_log, local_state), "ctx", link_states, identity)
+    prior_state = prior_states(final_log, local_state, "ctx")
     outside_part = jnp.exp(running)[:, :, None] * jnp.einsum(
         "htd,hde->hte", query_heads, prior_state, precision=PRECISE
     )
@@ -144,20 +131,18 @@
     gate_part = jnp.dot(flat_rows, w_gate[0], preferred_element_type=jnp.float32)
     up_part = jnp.dot(flat_rows, w_up[0], preferred_element_type=jnp.float32)
     hidden = (jax.nn.silu(gate_part) * up_part).astype(jnp.bfloat16)
-    partial_down = jnp.dot(hidden, w_down[0], preferred_element_type=jnp.float32).reshape(
-        arrived.shape
+    partial_down = jnp.dot(hidden, w_down[0], preferred_element_type=jnp.float32)
+    summed = lax.psum_scatter(
+        partial_down.astype(jnp.bfloat16), "head", scatter_dimension=1, tiled=True
     )
     returned = lax.all_to_all(
-        lax.all_to_all(
-            partial_down.astype(jnp.bfloat16)[None], "ctx", split_axis=1, concat_axis=1, tiled=True
-        ),
-        "head",
-        split_axis=3,
+        summed.reshape(experts_total, capacity, slice_width),
+        "ctx",
+        split_axis=0,
         concat_axis=0,
         tiled=True,
     )
-    expert_out = jnp.sum(returned.astype(jnp.float32), axis=0).astype(jnp.bfloat16)
-    lookup = expert_out.reshape(experts_total * capacity, slice_width)
+    lookup = returned.reshape(experts_total * capacity, slice_width)
     picked = lookup[target].reshape(token_count, TOP, slice_width).astype(jnp.float32)
     final_out = (
         base_slice + gate_weights[:, 0:1] * picked[:, 0] + gate_weights[:, 1:2] * picked[:, 1]

time: 516 us -> 358 us (0.69)
  other arithmetic: 104 us -> 17.7 us
  blocking collectives: 161 us -> 118 us
  local copies, waits for them, and re-layouts: 81.8 us -> 45.6 us
  matrix products: 21 us -> 29.8 us
  starting transfers between devices: 4.92 us -> 11.3 us
    all_to_all x1, waiting for transfers between devices: 72 us -> 7.36 us  [body(): lax.all_to_all(summed.reshape(experts_total, capacity, slice_width), 'ctx...]
    select_n x32 -> x1, other arithmetic: 56.9 us -> 0.01 us  [prior_states(): weights = jnp.where(jnp.arange(peers)[:, None] < index, jnp.exp(spans), 0.0)]
    all_to_all x1 -> x0, blocking collectives: 43.1 us -> none  [body(): lax.all_to_all(partial_down.astype(jnp.bfloat16)[None], 'ctx', split_axis...]
    unnamed x3 -> x5, waiting for transfers between devices: 0.73 us -> 38.2 us
    all_gather x1, waiting for transfers between devices: 0.01 us -> 23.6 us  [body(): lax.all_gather(out_weight, 'ctx', axis=1, tiled=True)]
    exp x32 -> x0, other arithmetic: 21.5 us -> none  [link_states(): jnp.exp(later[0])[:, None, None] * earlier[1] + later[1]]
    unnamed x30 -> x34, local copies, waits for them, and re-layouts: 30.8 us -> 12.5 us
    all_to_all x1 -> x0, local copies, waits for them, and re-layouts: 13.4 us -> none  [body(): lax.all_to_all(partial_down.astype(jnp.bfloat16)[None], 'ctx', split_axis...]
  transfers between devices with their start and end apart: 4 -> 5, of which waited for: 2 -> 4; matrix products, arithmetic and copies ran while one was open for 22% -> 11% of each run, Pallas kernels for 0% -> 0%
where the time goes in v1:
time: 358 us; the launch traced here: 357 us
  waiting for transfers between devices  121 us (34%)
  blocking collectives  118 us (33%)
  local copies, waits for them, and re-layouts  45.6 us (13%)
  matrix products  29.8 us (8%)
  other arithmetic  17.7 us (5%)
  between operations  14 us (4%)
  starting transfers between devices  11.3 us (3%)
    unnamed x1, blocking collectives  66 us
    all_to_all x1, blocking collectives, body(): lax.all_to_all(packed.reshape(experts_total, capacity, width_here), 'ctx'...  51.8 us
    psum x1, waiting for transfers between devices, body(): lax.psum(partial_out.astype(jnp.bfloat16), 'head').astype(jnp.float32)  51.4 us
    unnamed x5, waiting for transfers between devices  38.2 us
    all_gather x1, waiting for transfers between devices, body(): lax.all_gather(out_weight, 'ctx', axis=1, tiled=True)  23.6 us
    unnamed x34, local copies, waits for them, and re-layouts  12.5 us
    all_to_all x1, starting transfers between devices, body(): lax.all_to_all(summed.reshape(experts_total, capacity, slice_width), 'ctx...  11 us
    dot_general x1, matrix products, body(): jnp.dot(hidden, w_down[0], preferred_element_type=jnp.float32)  9.52 us
  transfers between devices with their start and end apart: 5, of which 4 were waited for; matrix products, arithmetic and copies ran while one was open for 11% of the time, Pallas kernels for 0%

profile of v1, /device:TPU:1, one launch (start us, length us, event | category | flops | bytes accessed | tf_op | source)
XLA Modules:
  0.0 356.7 jit_solution(9251623039175811909)
XLA Ops:
  6.5 1.1 reduce_window_sum.26
  8.5 1.7 copy.78
  10.1 1.9 convolution_convert_fusion.2
  12.1 0.7 all-gather.5.cloned.1.call-update
  12.8 1.3 dynamic-slice
  15.0 66.0 %all-reduce = f32[128]{0:T(128)} all-reduce(f32[128]{0:T(128)S(1)} %dynamic-update-slice), channel_id=2, replica_groups=mesh['ctx'=32,'head'=8] {'ctx'}, use_global_device_ids=true, to_apply=%add | all-reduce | flops 128 | bytes 1024
  81.0 0.7 reshape.188
  81.8 0.7 copy.65
  82.4 1.4 copy.66
  83.8 1.6 eq.39
  85.4 0.8 select_reduce_fusion
  86.2 1.9 convolution_multiply_fusion
  88.1 5.7 %fusion = f32[4,1,128,128]{3,1,2,0:T(1,128)S(1)} fusion(f32[32,4,1,1]{0,2,3,1:T(1,128)S(1)} %bitcast.151, bf16[32,4,128,128]{3,2,1,0:T(8,128)(2,1)} %bitcast.142), kind=kOutput, calls=%fused_computation.3 | convolution fusion | flops 25165824 | bytes 4456960 | tf_op jit(solution)/shard_map/jh,jhde->hde/dot_general | solution.py:22
  94.8 0.8 fusion.30
  95.6 23.6 %all-gather.5.cloned.1.call-done = bf16[512,3072]{0,1:T(8,128)(2,1)} async-done(((bf16[512,96]{0,1:T(8,128)(2,1)}), bf16[512,3072]{0,1:T(8,128)(2,1)}) %all-gather.5.cloned.1.call-update) | async-done | bytes 3145744 | tf_op jit(solution)/shard_map/all_gather | solution.py:102
  119.2 4.0 %convolution_convert_fusion.1 = bf16[128,3072]{1,0:T(8,128)(2,1)} fusion(bf16[128,512]{0,1:T(8,128)(2,1)} %bitcast.147, bf16[512,3072]{0,1:T(8,128)(2,1)} %all-gather.5.cloned.1.call-done), kind=kOutput, calls=%fused_computation.5 | convolution fusion | flops 403046400 | bytes 4063232 | tf_op jit(solution)/shard_map/dot_general | solution.py:100
  123.5 1.3 fusion.48
  124.8 1.5 eq.35
  126.3 1.9 reduce-window.6
  128.2 1.5 slice_reduce_fusion
  129.7 1.3 reduce-window.9
  131.6 1.4 fusion.47
  133.1 1.4 reshape.164
  134.5 1.5 copy.69
  136.0 1.2 multiply_add_fusion
  137.2 1.4 copy.70
  138.6 1.5 reshape.165
  140.1 1.2 compare_select_fusion
  141.3 51.4 %all-reduce.3.cloned.1.call-done = bf16[128,3072]{1,0:T(8,128)(2,1)} async-done(((bf16[128,3072]{1,0:T(8,128)(2,1)}), bf16[128,3072]{1,0:T(8,128)(2,1)}) %all-reduce.3.cloned.1.call-update) | async-done | bytes 786448 | tf_op jit(solution)/shard_map/psum | solution.py:110
  192.7 2.7 fusion.51
  197.1 2.0 broadcast_in_dim.93
  199.1 4.6 %reshape.184 = bf16[256,3072]{1,0:T(8,128)(2,1)} reshape(bf16[128,2,3072]{2,1,0:T(2,128)(2,1)} %broadcast_in_dim.93) | data formatting | bytes 3145728 | tf_op jit(solution)/shard_map/reshape | solution.py:121
  203.7 5.8 %scatter_custom_fusion = bf16[512,3072]{1,0:T(8,128)(2,1)} fusion(s32[256]{0:T(256)} %bitcast.152, bf16[256,3072]{1,0:T(8,128)(2,1)} %reshape.184, bf16[]{:T(256)} %constant.42.clone.1), kind=kCustom, calls=%fused_computation.12 | custom fusion | bytes 3146240 | tf_op jit(solution)/shard_map/scatter | solution.py:122
  209.4 51.8 %all_to_all.10 = bf16[32,16,3072]{2,1,0:T(8,128)(2,1)S(1)} all-to-all(bf16[32,16,3072]{2,1,0:T(8,128)(2,1)} %bitcast.141), channel_id=1, replica_groups=mesh['ctx'=32,'head'=8] {'ctx'}, dimensions={0} | all-to-all | bytes 6291456 | tf_op jit(solution)/shard_map/all_to_all | solution.py:123
  261.2 1.7 copy-done.2
  262.9 3.1 fusion.5
  266.1 9.5 %convolution_convert_fusion = bf16[512,3072]{1,0:T(8,128)(2,1)} fusion(bf16[1,576,3072]{2,1,0:T(8,128)(2,1)S(1)} %copy-done, bf16[512,3072]{1,0:T(8,128)(2,1)} %bitcast.144, bf16[1,3072,576]{1,2,0:T(8,128)(2,1)} %param.23, f32[512,576]{0,1:T(8,128)} %fusion.5), kind=kOutput, calls=%fused_computation.2 | convolution fusion | flops 3627220992 | bytes 14548992 | tf_op jit(solution)/shard_map/dot_general | solution.py:134
  275.6 4.7 %copy.81 = bf16[512,3072]{0,1:T(8,128)(2,1)} copy(bf16[512,3072]{1,0:T(8,128)(2,1)} %convolution_convert_fusion) | data formatting | bytes 6291456
  280.3 1.2 pad_clamp_fusion
  281.5 37.5 %reduce-scatter.4.cloned.1.call-done = bf16[384,512]{1,0:T(8,128)(2,1)} async-done(((bf16[3072,512]{1,0:T(8,128)(2,1)}), bf16[384,512]{1,0:T(8,128)(2,1)}) %reduce-scatter.4.cloned.1.call-update) | async-done | bytes 393232
  319.0 2.0 copy.82
  321.0 11.0 %all-to-all-start.1 = ((bf16[32,16,384]{2,1,0:T(8,128)(2,1)}), bf16[32,16,384]{2,1,0:T(8,128)(2,1)}, u32[]{:S(2)}, u32[]{:S(2)}) async-start(bf16[32,16,384]{2,1,0:T(8,128)(2,1)} %bitcast.145), calls=%async_computation.1 | async-start | bytes 786432 | tf_op jit(solution)/shard_map/all_to_all | solution.py:138
  332.0 2.8 fusion.18
  334.8 7.4 %all-to-all-done.1 = bf16[32,16,384]{2,1,0:T(8,128)(2,1)} async-done(((bf16[32,16,384]{2,1,0:T(8,128)(2,1)}), bf16[32,16,384]{2,1,0:T(8,128)(2,1)}, u32[]{:S(2)}, u32[]{:S(2)}) %all-to-all-start.1) | async-done | bytes 393248 | tf_op jit(solution)/shard_map/all_to_all | solution.py:138
  342.2 3.0 gather_fusion
  345.2 1.9 reshape.171
  347.0 1.5 fusion.52
  348.5 1.7 fusion.35
  (52 shorter events, 4.7 us)
Async XLA Ops:
  6.5 259.6 %copy-start = (bf16[1,576,3072]{2,1,0:T(8,128)(2,1)S(1)}, bf16[1,576,3072]{2,1,0:T(8,128)(2,1)}, u32[]{:S(2)}) copy-start(bf16[1,576,3072]{2,1,0:T(8,128)(2,1)} %param.24) | copy-start | bytes 10616836
  6.5 81.6 %all-gather.7.cloned.1.call-start = ((), (), s32[]{:S(2)}) async-start(), calls=%async_computation.5 | async-start | bytes 4325376 | tf_op jit(solution)/shard_map/all_gather | solution.py:15
  7.7 7.3 %copy-start.7 = (f32[4,128]{1,0:T(4,128)}, f32[4,128]{1,0:T(4,128)S(1)}, u32[]{:S(2)}) copy-start(f32[4,128]{1,0:T(4,128)S(1)} %reduce_window_sum.26) | copy-start | bytes 6148
  12.0 107.2 %all-gather.5.cloned.1.call-start = ((), (), s32[]{:S(2)}) async-start(), calls=%async_computation.3 | async-start | bytes 3244032 | tf_op jit(solution)/shard_map/all_gather | solution.py:102
  12.8 179.9 %all-reduce.3.cloned.1.call-start = ((), (), s32[]{:S(2)}) async-start(), calls=%async_computation.4 | async-start | bytes 1572864 | tf_op jit(solution)/shard_map/psum | solution.py:110
  82.4 11.8 %copy-start.10 = (f32[4,128]{1,0:T(4,128)S(1)}, f32[4,128]{1,0:T(4,128)}, u32[]{:S(2)}) copy-start(f32[4,128]{1,0:T(4,128)} %get-tuple-element.12) | copy-start | bytes 6148
  88.1 6.7 %copy-start.9 = (f32[128,4]{0,1:T(4,128)S(1)}, f32[128,4]{0,1:T(4,128)}, u32[]{:S(2)}) copy-start(f32[128,4]{0,1:T(4,128)} %get-tuple-element.11) | copy-start | bytes 6148
  88.1 5.8 %copy-start.5 = (bf16[128,512]{1,0:T(8,128)(2,1)S(1)}, bf16[128,512]{1,0:T(8,128)(2,1)}, u32[]{:S(2)}) copy-start(bf16[128,512]{1,0:T(8,128)(2,1)} %param.13) | copy-start | bytes 393220
  88.1 6.2 %copy-start.3 = (bf16[128,512]{1,0:T(8,128)(2,1)S(1)}, bf16[128,512]{1,0:T(8,128)(2,1)}, u32[]{:S(2)}) copy-start(bf16[128,512]{1,0:T(8,128)(2,1)} %param.15) | copy-start | bytes 393220
  88.1 6.2 %copy-start.4 = (f32[4,128,128]{2,1,0:T(8,128)S(1)}, f32[4,128,128]{2,1,0:T(8,128)}, u32[]{:S(2)}) copy-start(f32[4,128,128]{2,1,0:T(8,128)} %convolution_multiply_fusion) | copy-start | bytes 786436
  88.1 6.7 %copy-start.11 = (f32[512]{0:T(512)S(1)}, f32[512]{0:T(512)}, u32[]{:S(2)}) copy-start(f32[512]{0:T(512)} %param.19) | copy-start | bytes 6148
  94.8 41.2 %copy-start.8 = (s32[128,2]{0,1:T(2,128)S(1)}, s32[128,2]{0,1:T(2,128)}, u32[]{:S(2)}) copy-start(s32[128,2]{0,1:T(2,128)} %param.25) | copy-start | bytes 3076
  123.2 73.6 %copy-start.6 = (f32[3072]{0:T(1024)S(1)}, f32[3072]{0:T(1024)}, u32[]{:S(2)}) copy-start(f32[3072]{0:T(1024)} %param.20) | copy-start | bytes 36868
  123.3 195.8 %reduce-scatter.4.cloned.1.call-start = ((), (), s32[]{:S(2)}) async-start(), calls=%async_computation.6 | async-start | bytes 3538944
  195.4 0.9 copy-start.1
  196.3 0.5 copy-start.12
  209.4 53.5 %copy-start.13 = (bf16[1,3072,576]{1,2,0:T(8,128)(2,1)S(1)}, bf16[1,3072,576]{1,2,0:T(8,128)(2,1)}, u32[]{:S(2)}) copy-start(bf16[1,3072,576]{1,2,0:T(8,128)(2,1)} %param.22) | copy-start | bytes 10616836
  261.2 1.7 copy-start.2
  321.0 21.2 %all-to-all-start.1 = ((bf16[32,16,384]{2,1,0:T(8,128)(2,1)}), bf16[32,16,384]{2,1,0:T(8,128)(2,1)}, u32[]{:S(2)}, u32[]{:S(2)}) async-start(bf16[32,16,384]{2,1,0:T(8,128)(2,1)} %bitcast.145), calls=%async_computation.1 | async-start | bytes 786432 | tf_op jit(solution)/shard_map/all_to_all | solution.py:138
Sparse Core Ops, SparseCore 0:
  12.1 55.2 all-gather.6
  70.0 49.2 all-gather.4
  123.4 69.2 all-reduce.2
  280.4 38.5 reduce-scatter.3

commit v2 on v1

--- a/solution.py
+++ b/solution.py
@@ -11,8 +11,17 @@
 
 def prior_states(final_log, local_state, axis):
     index = lax.axis_index(axis)
-    totals = lax.all_gather(final_log, axis)
-    states = lax.all_gather(local_state.astype(jnp.bfloat16), axis)
+    heads_here, head_size = local_state.shape[0], local_state.shape[2]
+    high = final_log.astype(jnp.bfloat16)
+    rest = final_log - high.astype(jnp.float32)
+    middle = rest.astype(jnp.bfloat16)
+    low = (rest - middle.astype(jnp.float32)).astype(jnp.bfloat16)
+    extra = jnp.zeros((heads_here, 16, head_size), jnp.bfloat16)
+    extra = extra.at[:, 0:3, 0].set(jnp.stack([high, middle, low], axis=1))
+    packed = jnp.concatenate([local_state.astype(jnp.bfloat16), extra], axis=1)
+    gathered = lax.all_gather(packed, axis)
+    states = gathered[:, :, :head_size]
+    totals = jnp.sum(gathered[:, :, head_size : head_size + 3, 0].astype(jnp.float32), axis=2)
     peers = totals.shape[0]
     source = lax.broadcasted_iota(jnp.int32, (peers, peers), 0)
     between = lax.broadcasted_iota(jnp.int32, (peers, peers), 1)
@@ -97,18 +106,41 @@
         .transpose(1, 0, 2)
         .reshape(token_count, heads_here * head_size)
     )
-    partial_out = jnp.dot(
-        heads_normed,
-        lax.all_gather(out_weight, "ctx", axis=1, tiled=True),
-        preferred_element_type=jnp.float32,
+    ctx_size = lax.axis_size("ctx")
+    head_count = lax.axis_size("head")
+    weight_blocks = lax.all_to_all(
+        jnp.broadcast_to(out_weight[None], (ctx_size,) + out_weight.shape),
+        "ctx",
+        split_axis=0,
+        concat_axis=0,
+        tiled=True,
     )
     model_width = residual.shape[1]
     experts_total = router.shape[1]
     capacity = 2 * token_count * TOP // experts_total
-    slice_width = model_width // lax.axis_size("head")
+    slice_width = model_width // head_count
     slice_start = lax.axis_index("head") * slice_width
-    projected = lax.psum(partial_out.astype(jnp.bfloat16), "head").astype(jnp.float32)
-    mixed_rows = (residual.astype(jnp.float32) + projected).astype(jnp.bfloat16)
+    partial_out = jnp.einsum(
+        "tk,ckd->tcd", heads_normed, weight_blocks, preferred_element_type=jnp.float32
+    ).reshape(token_count, head_count, slice_width)
+    pieces = lax.all_to_all(
+        partial_out.astype(jnp.bfloat16).transpose(1, 0, 2),
+        "head",
+        split_axis=0,
+        concat_axis=0,
+        tiled=True,
+    )
+    projected = jnp.sum(pieces.astype(jnp.float32), axis=0)
+    own_residual = lax.dynamic_slice_in_dim(residual, slice_start, slice_width, 1)
+    mixed_slice = (own_residual.astype(jnp.float32) + projected).astype(jnp.bfloat16)
+    mixed_all = lax.all_to_all(
+        jnp.broadcast_to(mixed_slice[None], (head_count,) + mixed_slice.shape),
+        "head",
+        split_axis=0,
+        concat_axis=0,
+        tiled=True,
+    )
+    mixed_rows = mixed_all.transpose(1, 0, 2).reshape(token_count, model_width)
     mixed_wide = mixed_rows.astype(jnp.float32)
     inv_rms = lax.rsqrt(jnp.mean(mixed_wide * mixed_wide, axis=1, keepdims=True) + 1e-06)
     scaled = mixed_wide * moe_gain[None, :]

time: 358 us -> 344 us (0.961)
  blocking collectives: 118 us -> 45.2 us
  starting transfers between devices: 11.3 us -> 30.8 us
  local copies, waits for them, and re-layouts: 45.6 us -> 62.9 us
  waiting for transfers between devices: 121 us -> 136 us
  other arithmetic: 17.7 us -> 24.8 us
    unnamed x1 -> x0, blocking collectives: 66 us -> none
    psum x1 -> x0, waiting for transfers between devices: 51.4 us -> none  [body(): lax.psum(partial_out.astype(jnp.bfloat16), 'head').astype(jnp.float32)]
    all_gather x2 -> x1, waiting for transfers between devices: 23.6 us -> 65.1 us  [prior_states(): gathered = lax.all_gather(packed, axis)]
    all_to_all x0 -> x3, waiting for transfers between devices: none -> 26.7 us  [the longest x1 23.7 us: body(): lax.all_to_all(partial_out.astype(jnp.bfloat16).transpose(1, 0, 2), 'head...]
    all_to_all x0 -> x3, starting transfers between devices: none -> 19.7 us  [the longest x1 8.63 us: body(): lax.all_to_all(jnp.broadcast_to(out_weight[None], (ctx_size,) + out_weigh...]
    all_to_all x1, blocking collectives: 51.8 us -> 45.2 us  [body(): lax.all_to_all(packed.reshape(experts_total, capacity, width_here), 'ctx'...]
    convert_element_type x0 -> x2, local copies, waits for them, and re-layouts: none -> 3.93 us  [the longest x1 2.3 us: body(): moe_in = (scaled * inv_rms).astype(jnp.bfloat16)]
    broadcast_in_dim x0 -> x2, local copies, waits for them, and re-layouts: none -> 3.91 us  [the longest x1 2.93 us: body(): jnp.broadcast_to(out_weight[None], (ctx_size,) + out_weight.shape)]
  transfers between devices with their start and end apart: 5 -> 6, of which waited for: 4 -> 5; matrix products, arithmetic and copies ran while one was open for 11% -> 13% of each run, Pallas kernels for 0% -> 0%
where the time goes in v2:
time: 344 us; the launch traced here: 343 us
  waiting for transfers between devices  136 us (40%)
  local copies, waits for them, and re-layouts  62.9 us (18%)
  blocking collectives  45.2 us (13%)
  starting transfers between devices  30.8 us (9%)
  matrix products  28.9 us (8%)
  other arithmetic  24.8 us (7%)
  between operations  13.6 us (4%)
    all_gather x1, waiting for transfers between devices, prior_states(): gathered = lax.all_gather(packed, axis)  65.1 us
    all_to_all x1, blocking collectives, body(): lax.all_to_all(packed.reshape(experts_total, capacity, width_here), 'ctx'...  45.2 us
    unnamed x3, waiting for transfers between devices  37.1 us
    all_to_all x1, waiting for transfers between devices, body(): lax.all_to_all(partial_out.astype(jnp.bfloat16).transpose(1, 0, 2), 'head...  23.7 us
    unnamed x32, local copies, waits for them, and re-layouts  13.7 us
    all_to_all x1, starting transfers between devices, body(): lax.all_to_all(summed.reshape(experts_total, capacity, slice_width), 'ctx...  10.8 us
    dot_general x1, matrix products, body(): jnp.dot(hidden, w_down[0], preferred_element_type=jnp.float32)  9.51 us
    all_to_all x1, starting transfers between devices, body(): lax.all_to_all(jnp.broadcast_to(out_weight[None], (ctx_size,) + out_weigh...  8.63 us
  transfers between devices with their start and end apart: 6, of which 5 were waited for; matrix products, arithmetic and copies ran while one was open for 13% of the time, Pallas kernels for 0%

profile of v2, /device:TPU:1, one launch (start us, length us, event | category | flops | bytes accessed | tf_op | source)
XLA Modules:
  0.0 342.5 jit_solution(15549293287636633367)
XLA Ops:
  8.6 1.7 copy.135
  12.2 2.9 broadcast_in_dim.103
  15.1 8.6 %all-to-all-start = ((bf16[32,512,96]{1,2,0:T(8,128)(2,1)}), bf16[32,512,96]{1,2,0:T(8,128)(2,1)}, u32[]{:S(2)}, u32[]{:S(2)}) async-start(bf16[32,512,96]{1,2,0:T(8,128)(2,1)} %broadcast_in_dim.103), calls=%async_computation | async-start | bytes 6291456 | tf_op jit(solution)/shard_map/all_to_all | solution.py:111
  25.0 1.9 convolution_multiply_fusion
  26.8 65.1 %all-gather.3.cloned.1.call-done = bf16[128,144,128]{2,1,0:T(8,128)(2,1)} async-done(((bf16[4,144,128]{2,1,0:T(8,128)(2,1)}), bf16[128,144,128]{2,1,0:T(8,128)(2,1)}) %all-gather.3.cloned.1.call-update) | async-done | bytes 4718608 | tf_op jit(solution)/shard_map/all_gather | solution.py:22
  91.9 4.8 %slice.65 = bf16[32,4,128,128]{3,2,1,0:T(8,128)(2,1)} slice(bf16[32,4,144,128]{3,2,1,0:T(8,128)(2,1)} %bitcast.152), slice={[0:32], [0:4], [0:128], [0:128]} | slice | bytes 8388608 | tf_op jit(solution)/shard_map/slice | solution.py:23
  100.2 5.7 %fusion = f32[4,1,128,128]{3,1,2,0:T(1,128)S(1)} fusion(f32[32,4,1,1]{0,2,3,1:T(1,128)S(1)} %bitcast.162, bf16[32,4,128,128]{3,2,1,0:T(8,128)(2,1)} %slice.65), kind=kOutput, calls=%fused_computation.3 | convolution fusion | flops 25165824 | bytes 4456960 | tf_op jit(solution)/shard_map/jh,jhde->hde/dot_general | solution.py:31
  107.6 4.0 %fusion.17 = bf16[8,128,384]{2,1,0:T(8,128)(2,1)} fusion(bf16[128,512,1]{0,1,2:T(8,128)(2,1)} %bitcast.158, bf16[8,384,512]{2,1,0:T(8,128)(2,1)} %bitcast.22), kind=kOutput, calls=%fused_computation.20 | convolution fusion | flops 403046400 | bytes 4063232 | tf_op jit(solution)/shard_map/tk,ckd->tcd/dot_general | solution.py:123
  111.6 6.9 %all-to-all-start.1 = ((bf16[8,128,384]{2,1,0:T(8,128)(2,1)}), bf16[8,128,384]{2,1,0:T(8,128)(2,1)}, u32[]{:S(2)}, u32[]{:S(2)}) async-start(bf16[8,128,384]{2,1,0:T(8,128)(2,1)} %fusion.17), calls=%async_computation.1 | async-start | bytes 1572864 | tf_op jit(solution)/shard_map/all_to_all | solution.py:126
  118.5 23.7 %all-to-all-done.1 = bf16[8,128,384]{2,1,0:T(8,128)(2,1)} async-done(((bf16[8,128,384]{2,1,0:T(8,128)(2,1)}), bf16[8,128,384]{2,1,0:T(8,128)(2,1)}, u32[]{:S(2)}, u32[]{:S(2)}) %all-to-all-start.1) | async-done | bytes 786464 | tf_op jit(solution)/shard_map/all_to_all | solution.py:126
  145.3 4.2 %all-to-all-start.2 = ((bf16[8,128,384]{2,1,0:T(8,128)(2,1)}), bf16[8,128,384]{2,1,0:T(8,128)(2,1)}, u32[]{:S(2)}, u32[]{:S(2)}) async-start(bf16[8,128,384]{2,1,0:T(8,128)(2,1)} %broadcast_in_dim.104), calls=%async_computation.2 | async-start | bytes 1572864 | tf_op jit(solution)/shard_map/all_to_all | solution.py:136
  150.5 1.6 eq.39
  152.1 1.5 eq.35
  153.6 1.3 fusion.48
  154.9 1.9 reduce-window.6
  156.8 1.5 slice_reduce_fusion
  160.2 1.4 fusion.47
  161.7 1.4 reshape.211
  163.1 1.5 copy.123
  165.8 1.4 copy.124
  167.2 1.6 reshape.212
  168.8 1.3 compare_select_fusion
  170.1 3.0 all-to-all-done.2
  173.1 2.3 copy.119
  175.4 1.6 multiply_reduce_fusion
  177.5 2.9 multiply_convert_fusion
  180.4 2.3 copy.125
  182.7 3.1 broadcast_in_dim.108
  185.8 4.6 %reshape.232 = bf16[256,3072]{1,0:T(8,128)(2,1)} reshape(bf16[128,2,3072]{2,1,0:T(2,128)(2,1)} %broadcast_in_dim.108) | data formatting | bytes 3145728 | tf_op jit(solution)/shard_map/reshape | solution.py:153
  190.4 5.8 %scatter_custom_fusion = bf16[512,3072]{1,0:T(8,128)(2,1)} fusion(s32[256]{0:T(256)} %bitcast.164, bf16[256,3072]{1,0:T(8,128)(2,1)} %reshape.232, bf16[]{:T(256)} %constant.66.clone.1), kind=kCustom, calls=%fused_computation.11 | custom fusion | bytes 3146240 | tf_op jit(solution)/shard_map/scatter | solution.py:154
  196.2 45.2 %all_to_all.25 = bf16[32,16,3072]{2,1,0:T(8,128)(2,1)S(1)} all-to-all(bf16[32,16,3072]{2,1,0:T(8,128)(2,1)} %bitcast.149), channel_id=1, replica_groups=mesh['ctx'=32,'head'=8] {'ctx'}, dimensions={0} | all-to-all | bytes 6291456 | tf_op jit(solution)/shard_map/all_to_all | solution.py:155
  241.3 1.7 copy-done.1
  243.1 3.2 fusion.5
  246.2 9.5 %convolution_convert_fusion = bf16[512,3072]{1,0:T(8,128)(2,1)} fusion(bf16[1,576,3072]{2,1,0:T(8,128)(2,1)S(1)} %copy-done, bf16[512,3072]{1,0:T(8,128)(2,1)} %bitcast.155, bf16[1,3072,576]{1,2,0:T(8,128)(2,1)} %param.25, f32[512,576]{0,1:T(8,128)} %fusion.5), kind=kOutput, calls=%fused_computation.2 | convolution fusion | flops 3627220992 | bytes 14548992 | tf_op jit(solution)/shard_map/dot_general | solution.py:166
  255.7 4.7 %copy.141 = bf16[512,3072]{0,1:T(8,128)(2,1)} copy(bf16[512,3072]{1,0:T(8,128)(2,1)} %convolution_convert_fusion) | data formatting | bytes 6291456
  260.4 1.3 pad_clamp_fusion
  261.7 37.1 %reduce-scatter.4.cloned.1.call-done = bf16[384,512]{1,0:T(8,128)(2,1)} async-done(((bf16[3072,512]{1,0:T(8,128)(2,1)}), bf16[384,512]{1,0:T(8,128)(2,1)}) %reduce-scatter.4.cloned.1.call-update) | async-done | bytes 393232
  298.8 1.9 copy.142
  300.7 10.8 %all-to-all-start.4 = ((bf16[32,16,384]{2,1,0:T(8,128)(2,1)}), bf16[32,16,384]{2,1,0:T(8,128)(2,1)}, u32[]{:S(2)}, u32[]{:S(2)}) async-start(bf16[32,16,384]{2,1,0:T(8,128)(2,1)} %bitcast.156), calls=%async_computation.4 | async-start | bytes 786432 | tf_op jit(solution)/shard_map/all_to_all | solution.py:170
  311.6 2.7 fusion.18
  314.3 7.5 %all-to-all-done.4 = bf16[32,16,384]{2,1,0:T(8,128)(2,1)} async-done(((bf16[32,16,384]{2,1,0:T(8,128)(2,1)}), bf16[32,16,384]{2,1,0:T(8,128)(2,1)}, u32[]{:S(2)}, u32[]{:S(2)}) %all-to-all-start.4) | async-done | bytes 393248 | tf_op jit(solution)/shard_map/all_to_all | solution.py:170
  321.8 3.0 gather_fusion
  324.8 1.9 reshape.219
  326.6 2.2 fusion.52
  328.8 1.7 copy.144
  330.5 1.7 copy.145
  332.3 1.8 fusion.35
  334.1 1.6 copy.128
  (60 shorter events, 18.1 us)
Async XLA Ops:
  6.5 239.7 %copy-start = (bf16[1,576,3072]{2,1,0:T(8,128)(2,1)S(1)}, bf16[1,576,3072]{2,1,0:T(8,128)(2,1)}, u32[]{:S(2)}) copy-start(bf16[1,576,3072]{2,1,0:T(8,128)(2,1)} %param.26) | copy-start | bytes 10616836
  6.5 85.4 %all-gather.3.cloned.1.call-start = ((), (), s32[]{:S(2)}) async-start(), calls=%async_computation.6 | async-start | bytes 4866048 | tf_op jit(solution)/shard_map/all_gather | solution.py:22
  15.1 92.5 %all-to-all-start = ((bf16[32,512,96]{1,2,0:T(8,128)(2,1)}), bf16[32,512,96]{1,2,0:T(8,128)(2,1)}, u32[]{:S(2)}, u32[]{:S(2)}) async-start(bf16[32,512,96]{1,2,0:T(8,128)(2,1)} %broadcast_in_dim.103), calls=%async_computation | async-start | bytes 6291456 | tf_op jit(solution)/shard_map/all_to_all | solution.py:111
  23.8 0.6 copy-start.10
  98.6 7.3 %copy-start.4 = (bf16[128,512]{1,0:T(8,128)(2,1)S(1)}, bf16[128,512]{1,0:T(8,128)(2,1)}, u32[]{:S(2)}) copy-start(bf16[128,512]{1,0:T(8,128)(2,1)} %param.15) | copy-start | bytes 393220
  98.6 7.7 %copy-start.2 = (bf16[128,512]{1,0:T(8,128)(2,1)S(1)}, bf16[128,512]{1,0:T(8,128)(2,1)}, u32[]{:S(2)}) copy-start(bf16[128,512]{1,0:T(8,128)(2,1)} %param.17) | copy-start | bytes 393220
  98.7 7.7 %copy-start.3 = (f32[4,128,128]{2,1,0:T(8,128)S(1)}, f32[4,128,128]{2,1,0:T(8,128)}, u32[]{:S(2)}) copy-start(f32[4,128,128]{2,1,0:T(8,128)} %convolution_multiply_fusion) | copy-start | bytes 786436
  98.7 7.7 %copy-start.8 = (f32[4,128]{1,0:T(4,128)S(1)}, f32[4,128]{1,0:T(4,128)}, u32[]{:S(2)}) copy-start(f32[4,128]{1,0:T(4,128)} %get-tuple-element.24) | copy-start | bytes 6148
  98.7 8.1 %copy-start.7 = (f32[128,4]{0,1:T(4,128)S(1)}, f32[128,4]{0,1:T(4,128)}, u32[]{:S(2)}) copy-start(f32[128,4]{0,1:T(4,128)} %get-tuple-element.23) | copy-start | bytes 6148
  98.7 8.1 %copy-start.9 = (f32[512]{0:T(512)S(1)}, f32[512]{0:T(512)}, u32[]{:S(2)}) copy-start(f32[512]{0:T(512)} %param.21) | copy-start | bytes 6148
  111.6 38.2 %copy-start.6 = (s32[128,2]{0,1:T(2,128)S(1)}, s32[128,2]{0,1:T(2,128)}, u32[]{:S(2)}) copy-start(s32[128,2]{0,1:T(2,128)} %param.27) | copy-start | bytes 3076
  111.6 30.5 %all-to-all-start.1 = ((bf16[8,128,384]{2,1,0:T(8,128)(2,1)}), bf16[8,128,384]{2,1,0:T(8,128)(2,1)}, u32[]{:S(2)}, u32[]{:S(2)}) async-start(bf16[8,128,384]{2,1,0:T(8,128)(2,1)} %fusion.17), calls=%async_computation.1 | async-start | bytes 1572864 | tf_op jit(solution)/shard_map/all_to_all | solution.py:126
  143.4 34.1 %copy-start.5 = (f32[3072]{0:T(1024)S(1)}, f32[3072]{0:T(1024)}, u32[]{:S(2)}) copy-start(f32[3072]{0:T(1024)} %param.22) | copy-start | bytes 36868
  145.3 27.8 %all-to-all-start.2 = ((bf16[8,128,384]{2,1,0:T(8,128)(2,1)}), bf16[8,128,384]{2,1,0:T(8,128)(2,1)}, u32[]{:S(2)}, u32[]{:S(2)}) async-start(bf16[8,128,384]{2,1,0:T(8,128)(2,1)} %broadcast_in_dim.104), calls=%async_computation.2 | async-start | bytes 1572864 | tf_op jit(solution)/shard_map/all_to_all | solution.py:136
  149.5 149.3 %reduce-scatter.4.cloned.1.call-start = ((), (), s32[]{:S(2)}) async-start(), calls=%async_computation.7 | async-start | bytes 3538944
  177.0 0.5 copy-start.11
  196.2 46.9 %copy-start.12 = (bf16[1,3072,576]{1,2,0:T(8,128)(2,1)S(1)}, bf16[1,3072,576]{1,2,0:T(8,128)(2,1)}, u32[]{:S(2)}) copy-start(bf16[1,3072,576]{1,2,0:T(8,128)(2,1)} %param.24) | copy-start | bytes 10616836
  241.3 1.7 copy-start.1
  300.7 21.1 %all-to-all-start.4 = ((bf16[32,16,384]{2,1,0:T(8,128)(2,1)}), bf16[32,16,384]{2,1,0:T(8,128)(2,1)}, u32[]{:S(2)}, u32[]{:S(2)}) async-start(bf16[32,16,384]{2,1,0:T(8,128)(2,1)} %bitcast.156), calls=%async_computation.4 | async-start | bytes 786432 | tf_op jit(solution)/shard_map/all_to_all | solution.py:170
Sparse Core Ops, SparseCore 0:
  12.3 79.5 all-gather.2
  260.6 38.2 reduce-scatter.3

commit v3 on v2

--- a/solution.py
+++ b/solution.py
@@ -10,27 +10,26 @@
 
 
 def prior_states(final_log, local_state, axis):
-    index = lax.axis_index(axis)
+    peers = lax.axis_size(axis)
     heads_here, head_size = local_state.shape[0], local_state.shape[2]
-    high = final_log.astype(jnp.bfloat16)
-    rest = final_log - high.astype(jnp.float32)
-    middle = rest.astype(jnp.bfloat16)
-    low = (rest - middle.astype(jnp.float32)).astype(jnp.bfloat16)
-    extra = jnp.zeros((heads_here, 16, head_size), jnp.bfloat16)
-    extra = extra.at[:, 0:3, 0].set(jnp.stack([high, middle, low], axis=1))
-    packed = jnp.concatenate([local_state.astype(jnp.bfloat16), extra], axis=1)
-    gathered = lax.all_gather(packed, axis)
-    states = gathered[:, :, :head_size]
-    totals = jnp.sum(gathered[:, :, head_size : head_size + 3, 0].astype(jnp.float32), axis=2)
-    peers = totals.shape[0]
-    source = lax.broadcasted_iota(jnp.int32, (peers, peers), 0)
-    between = lax.broadcasted_iota(jnp.int32, (peers, peers), 1)
-    inside = (between > source) & (between < index)
-    spans = jnp.sum(jnp.where(inside[:, :, None], totals[None, :, :], 0.0), axis=1)
-    weights = jnp.where(jnp.arange(peers)[:, None] < index, jnp.exp(spans), 0.0)
-    return jnp.einsum(
-        "jh,jhde->hde", weights, states.astype(jnp.float32), precision=PRECISE
-    )
+    totals = jnp.broadcast_to(final_log[:, None, None], (heads_here, 8, head_size))
+    packed = jnp.concatenate([local_state, totals], axis=1)
+    row = lax.broadcasted_iota(jnp.int32, packed.shape, 1)
+
+    def combine(earlier, later):
+        scale = jnp.exp(later[:, head_size : head_size + 1, 0:1])
+        return later + jnp.where(row < head_size, scale, 1.0) * earlier
+
+    def shifted(value, distance):
+        pairs = [(k, k + distance) for k in range(peers - distance)]
+        return lax.ppermute(value, axis, pairs)
+
+    before = combine(shifted(packed, 2), shifted(packed, 1))
+    distance = 2
+    while distance < peers:
+        before = combine(shifted(before, distance), before)
+        distance *= 2
+    return before[:, :head_size]
 
 
 def local_attention(query_block, key_block, value_block, decay_block):
@@ -108,13 +107,7 @@
     )
     ctx_size = lax.axis_size("ctx")
     head_count = lax.axis_size("head")
-    weight_blocks = lax.all_to_all(
-        jnp.broadcast_to(out_weight[None], (ctx_size,) + out_weight.shape),
-        "ctx",
-        split_axis=0,
-        concat_axis=0,
-        tiled=True,
-    )
+    weight_blocks = lax.all_gather(out_weight, "ctx")
     model_width = residual.shape[1]
     experts_total = router.shape[1]
     capacity = 2 * token_count * TOP // experts_total

time: 344 us -> 317 us (0.922)
  waiting for transfers between devices: 136 us -> 97.3 us
  starting transfers between devices: 30.8 us -> 58.8 us
  matrix products: 28.9 us -> 19.7 us
  local copies, waits for them, and re-layouts: 62.9 us -> 57.1 us
  other arithmetic: 24.8 us -> 20.5 us
    all_gather x1, waiting for transfers between devices: 65.1 us -> 0.01 us  [body(): weight_blocks = lax.all_gather(out_weight, 'ctx')]
    ppermute x0 -> x6, starting transfers between devices: none -> 32.2 us  [shifted(): return lax.ppermute(value, axis, pairs)]
    ppermute x0 -> x6, waiting for transfers between devices: none -> 28 us  [shifted(): return lax.ppermute(value, axis, pairs)]
    all_to_all x1 -> x0, starting transfers between devices: 8.63 us -> none  [body(): lax.all_to_all(jnp.broadcast_to(out_weight[None], (ctx_size,) + out_weigh...]
    dot_general x1 -> x0, matrix products: 5.69 us -> none  [prior_states(): jnp.einsum('jh,jhde->hde', weights, states.astype(jnp.float32), precision...]
    all_to_all x1, starting transfers between devices: 6.87 us -> 11.6 us  [body(): lax.all_to_all(partial_out.astype(jnp.bfloat16).transpose(1, 0, 2), 'head...]
    unnamed x32 -> x27, local copies, waits for them, and re-layouts: 13.7 us -> 13.1 us
  transfers between devices with their start and end apart: 6 -> 11, of which waited for: 5 -> 10; matrix products, arithmetic and copies ran while one was open for 13% -> 10% of each run, Pallas kernels for 0% -> 0%
where the time goes in v3:
time: 317 us; the launch traced here: 316 us
  waiting for transfers between devices  97.3 us (31%)
  starting transfers between devices  58.8 us (19%)
  local copies, waits for them, and re-layouts  57.1 us (18%)
  blocking collectives  48.6 us (15%)
  other arithmetic  20.5 us (6%)
  matrix products  19.7 us (6%)
  between operations  13.7 us (4%)
    all_to_all x1, blocking collectives, body(): lax.all_to_all(packed.reshape(experts_total, capacity, width_here), 'ctx'...  48.6 us
    unnamed x3, waiting for transfers between devices  40.3 us
    ppermute x6, starting transfers between devices, shifted(): return lax.ppermute(value, axis, pairs)  32.2 us
    ppermute x6, waiting for transfers between devices, shifted(): return lax.ppermute(value, axis, pairs)  28 us
    all_to_all x1, waiting for transfers between devices, body(): lax.all_to_all(partial_out.astype(jnp.bfloat16).transpose(1, 0, 2), 'head...  21.1 us
    unnamed x27, local copies, waits for them, and re-layouts  13.1 us
    all_to_all x1, starting transfers between devices, body(): lax.all_to_all(partial_out.astype(jnp.bfloat16).transpose(1, 0, 2), 'head...  11.6 us
    all_to_all x1, starting transfers between devices, body(): lax.all_to_all(summed.reshape(experts_total, capacity, slice_width), 'ctx...  10.7 us
  transfers between devices with their start and end apart: 11, of which 10 were waited for; matrix products, arithmetic and copies ran while one was open for 10% of the time, Pallas kernels for 0%

profile of v3, /device:TPU:1, one launch (start us, length us, event | category | flops | bytes accessed | tf_op | source)
XLA Modules:
  0.0 315.7 jit_solution(10796881605360934397)
XLA Ops:
  7.3 2.0 copy.118
  11.8 4.5 %collective-permute-start = (f32[4,136,128]{2,1,0:T(8,128)S(1)}, f32[4,136,128]{2,1,0:T(8,128)S(1)}, u32[]{:S(2)}, u32[]{:S(2)}) collective-permute-start(f32[4,136,128]{2,1,0:T(8,128)S(1)} %pad_maximum_fusion), channel_id=1, source_target_pairs={{0,8},{8,16},{16,24},{24,32},{32,40},{40,48},{48,56},{56,64},{64,7... | collective-permute-start | bytes 835592 | tf_op jit(solution)/shard_map/ppermute | solution.py:25
  16.3 3.1 collective-permute-start.1
  20.4 5.4 %collective-permute-done.1 = f32[4,136,128]{2,1,0:T(8,128)S(1)} collective-permute-done((f32[4,136,128]{2,1,0:T(8,128)S(1)}, f32[4,136,128]{2,1,0:T(8,128)S(1)}, u32[]{:S(2)}, u32[]{:S(2)}) %collective-permute-start.1) | collective-permute-done | bytes 278560 | tf_op jit(solution)/shard_map/ppermute | solution.py:25
  25.9 3.8 %collective-permute-start.2 = (f32[4,136,128]{2,1,0:T(8,128)S(1)}, f32[4,136,128]{2,1,0:T(8,128)S(1)}, u32[]{:S(2)}, u32[]{:S(2)}) collective-permute-start(f32[4,136,128]{2,1,0:T(8,128)S(1)} %multiply_add_fusion.3), channel_id=1, source_target_pairs={{0,16},{8,24},{16,32},{24,40},{32,48},{40,56},{48,64},{56,72},{64,... | collective-permute-start | bytes 835592 | tf_op jit(solution)/shard_map/ppermute | solution.py:25
  29.9 6.7 %collective-permute-done.2 = f32[4,136,128]{2,1,0:T(8,128)S(1)} collective-permute-done((f32[4,136,128]{2,1,0:T(8,128)S(1)}, f32[4,136,128]{2,1,0:T(8,128)S(1)}, u32[]{:S(2)}, u32[]{:S(2)}) %collective-permute-start.2) | collective-permute-done | bytes 278560 | tf_op jit(solution)/shard_map/ppermute | solution.py:25
  36.7 5.7 %collective-permute-start.3 = (f32[4,136,128]{2,1,0:T(8,128)S(1)}, f32[4,136,128]{2,1,0:T(8,128)S(1)}, u32[]{:S(2)}, u32[]{:S(2)}) collective-permute-start(f32[4,136,128]{2,1,0:T(8,128)S(1)} %multiply_add_fusion.2), channel_id=1, source_target_pairs={{0,32},{8,40},{16,48},{24,56},{32,64},{40,72},{48,80},{56,88},{64,... | collective-permute-start | bytes 835592 | tf_op jit(solution)/shard_map/ppermute | solution.py:25
  42.5 5.1 %collective-permute-done.3 = f32[4,136,128]{2,1,0:T(8,128)S(1)} collective-permute-done((f32[4,136,128]{2,1,0:T(8,128)S(1)}, f32[4,136,128]{2,1,0:T(8,128)S(1)}, u32[]{:S(2)}, u32[]{:S(2)}) %collective-permute-start.3) | collective-permute-done | bytes 278560 | tf_op jit(solution)/shard_map/ppermute | solution.py:25
  47.7 8.4 %collective-permute-start.4 = (f32[4,136,128]{2,1,0:T(8,128)S(1)}, f32[4,136,128]{2,1,0:T(8,128)S(1)}, u32[]{:S(2)}, u32[]{:S(2)}) collective-permute-start(f32[4,136,128]{2,1,0:T(8,128)S(1)} %multiply_add_fusion.1), channel_id=1, source_target_pairs={{0,64},{8,72},{16,80},{24,88},{32,96},{40,104},{48,112},{56,120},{... | collective-permute-start | bytes 835592 | tf_op jit(solution)/shard_map/ppermute | solution.py:25
  56.2 6.9 %collective-permute-done.4 = f32[4,136,128]{2,1,0:T(8,128)S(1)} collective-permute-done((f32[4,136,128]{2,1,0:T(8,128)S(1)}, f32[4,136,128]{2,1,0:T(8,128)S(1)}, u32[]{:S(2)}, u32[]{:S(2)}) %collective-permute-start.4) | collective-permute-done | bytes 278560 | tf_op jit(solution)/shard_map/ppermute | solution.py:25
  63.2 6.7 %collective-permute-start.5 = (f32[4,136,128]{2,1,0:T(8,128)S(1)}, f32[4,136,128]{2,1,0:T(8,128)S(1)}, u32[]{:S(2)}, u32[]{:S(2)}) collective-permute-start(f32[4,136,128]{2,1,0:T(8,128)S(1)} %multiply_add_fusion), channel_id=1, source_target_pairs={{0,128},{8,136},{16,144},{24,152},{32,160},{40,168},{48,176},{56,1... | collective-permute-start | bytes 835592 | tf_op jit(solution)/shard_map/ppermute | solution.py:25
  70.3 3.1 collective-permute-done.5
  75.2 2.3 copy.150
  77.5 2.1 fusion.15
  79.6 11.6 %all-to-all-start = ((bf16[8,128,384]{2,1,0:T(8,128)(2,1)}), bf16[8,128,384]{2,1,0:T(8,128)(2,1)}, u32[]{:S(2)}, u32[]{:S(2)}) async-start(bf16[8,128,384]{2,1,0:T(8,128)(2,1)} %fusion.15), calls=%async_computation | async-start | bytes 1572864 | tf_op jit(solution)/shard_map/all_to_all | solution.py:119
  91.2 21.1 %all-to-all-done = bf16[8,128,384]{2,1,0:T(8,128)(2,1)} async-done(((bf16[8,128,384]{2,1,0:T(8,128)(2,1)}), bf16[8,128,384]{2,1,0:T(8,128)(2,1)}, u32[]{:S(2)}, u32[]{:S(2)}) %all-to-all-start) | async-done | bytes 786464 | tf_op jit(solution)/shard_map/all_to_all | solution.py:119
  115.5 4.2 %all-to-all-start.1 = ((bf16[8,128,384]{2,1,0:T(8,128)(2,1)}), bf16[8,128,384]{2,1,0:T(8,128)(2,1)}, u32[]{:S(2)}, u32[]{:S(2)}) async-start(bf16[8,128,384]{2,1,0:T(8,128)(2,1)} %broadcast_in_dim.119), calls=%async_computation.1 | async-start | bytes 1572864 | tf_op jit(solution)/shard_map/all_to_all | solution.py:129
  120.5 1.6 eq.39
  122.0 1.5 eq.35
  124.9 1.9 reduce-window.6
  126.8 1.5 slice_reduce_fusion
  131.6 1.4 reshape.146
  133.1 1.5 copy.108
  137.2 1.6 reshape.147
  140.4 2.3 copy.104
  142.7 1.6 multiply_reduce_fusion
  144.8 2.9 multiply_convert_fusion
  147.8 2.3 copy.110
  150.1 3.1 broadcast_in_dim.123
  153.1 4.6 %reshape.167 = bf16[256,3072]{1,0:T(8,128)(2,1)} reshape(bf16[128,2,3072]{2,1,0:T(2,128)(2,1)} %broadcast_in_dim.123) | data formatting | bytes 3145728 | tf_op jit(solution)/shard_map/reshape | solution.py:146
  157.8 5.8 %scatter_custom_fusion = bf16[512,3072]{1,0:T(8,128)(2,1)} fusion(s32[256]{0:T(256)} %bitcast.156, bf16[256,3072]{1,0:T(8,128)(2,1)} %reshape.167, bf16[]{:T(256)} %constant.40.clone.1), kind=kCustom, calls=%fused_computation.10 | custom fusion | bytes 3146240 | tf_op jit(solution)/shard_map/scatter | solution.py:147
  163.5 48.6 %all_to_all.20 = bf16[32,16,3072]{2,1,0:T(8,128)(2,1)S(1)} all-to-all(bf16[32,16,3072]{2,1,0:T(8,128)(2,1)} %bitcast.143), channel_id=1, replica_groups=mesh['ctx'=32,'head'=8] {'ctx'}, dimensions={0} | all-to-all | bytes 6291456 | tf_op jit(solution)/shard_map/all_to_all | solution.py:148
  212.1 1.7 copy-done.1
  213.8 3.2 fusion.3
  216.9 9.5 %convolution_convert_fusion = bf16[512,3072]{1,0:T(8,128)(2,1)} fusion(bf16[1,576,3072]{2,1,0:T(8,128)(2,1)S(1)} %copy-done, bf16[512,3072]{1,0:T(8,128)(2,1)} %bitcast.149, bf16[1,3072,576]{1,2,0:T(8,128)(2,1)} %param.23, f32[512,576]{0,1:T(8,128)} %fusion.3), kind=kOutput, calls=%fused_computation.2 | convolution fusion | flops 3627220992 | bytes 14548992 | tf_op jit(solution)/shard_map/dot_general | solution.py:159
  226.5 4.7 %copy.122 = bf16[512,3072]{0,1:T(8,128)(2,1)} copy(bf16[512,3072]{1,0:T(8,128)(2,1)} %convolution_convert_fusion) | data formatting | bytes 6291456
  232.5 39.6 %reduce-scatter.4.cloned.1.call-done = bf16[384,512]{1,0:T(8,128)(2,1)} async-done(((bf16[3072,512]{1,0:T(8,128)(2,1)}), bf16[384,512]{1,0:T(8,128)(2,1)}) %reduce-scatter.4.cloned.1.call-update) | async-done | bytes 393232
  272.1 1.9 copy.123
  274.0 10.7 %all-to-all-start.3 = ((bf16[32,16,384]{2,1,0:T(8,128)(2,1)}), bf16[32,16,384]{2,1,0:T(8,128)(2,1)}, u32[]{:S(2)}, u32[]{:S(2)}) async-start(bf16[32,16,384]{2,1,0:T(8,128)(2,1)} %bitcast.150), calls=%async_computation.3 | async-start | bytes 786432 | tf_op jit(solution)/shard_map/all_to_all | solution.py:163
  284.7 2.7 fusion.16
  287.4 7.5 %all-to-all-done.3 = bf16[32,16,384]{2,1,0:T(8,128)(2,1)} async-done(((bf16[32,16,384]{2,1,0:T(8,128)(2,1)}), bf16[32,16,384]{2,1,0:T(8,128)(2,1)}, u32[]{:S(2)}, u32[]{:S(2)}) %all-to-all-start.3) | async-done | bytes 393248 | tf_op jit(solution)/shard_map/all_to_all | solution.py:163
  294.9 3.0 gather_fusion
  297.9 1.9 reshape.154
  299.7 2.2 fusion.57
  301.9 1.7 copy.124
  303.7 1.7 copy.125
  305.4 1.8 fusion.35
  307.2 1.6 copy.113
  (65 shorter events, 21.8 us)
Async XLA Ops:
  6.5 210.4 %copy-start = (bf16[1,576,3072]{2,1,0:T(8,128)(2,1)S(1)}, bf16[1,576,3072]{2,1,0:T(8,128)(2,1)}, u32[]{:S(2)}) copy-start(bf16[1,576,3072]{2,1,0:T(8,128)(2,1)} %param.24) | copy-start | bytes 10616836
  6.5 68.6 %all-gather.3.cloned.1.call-start = ((), (), s32[]{:S(2)}) async-start(), calls=%async_computation.5 | async-start | bytes 3244032 | tf_op jit(solution)/shard_map/all_gather | solution.py:110
  10.2 59.7 %copy-start.4 = (bf16[128,512]{0,1:T(8,128)(2,1)S(1)}, bf16[128,512]{0,1:T(8,128)(2,1)}, u32[]{:S(2)}) copy-start(bf16[128,512]{0,1:T(8,128)(2,1)} %copy.118) | copy-start | bytes 393220
  10.2 59.7 %copy-start.5 = (bf16[128,512]{1,0:T(8,128)(2,1)S(1)}, bf16[128,512]{1,0:T(8,128)(2,1)}, u32[]{:S(2)}) copy-start(bf16[128,512]{1,0:T(8,128)(2,1)} %param.13) | copy-start | bytes 393220
  10.2 63.7 %copy-start.3 = (bf16[128,512]{1,0:T(8,128)(2,1)S(1)}, bf16[128,512]{1,0:T(8,128)(2,1)}, u32[]{:S(2)}) copy-start(bf16[128,512]{1,0:T(8,128)(2,1)} %param.15) | copy-start | bytes 393220
  11.8 62.5 %copy-start.8 = (f32[512]{0:T(512)S(1)}, f32[512]{0:T(512)}, u32[]{:S(2)}) copy-start(f32[512]{0:T(512)} %param.19) | copy-start | bytes 6148
  11.8 8.5 %collective-permute-start = (f32[4,136,128]{2,1,0:T(8,128)S(1)}, f32[4,136,128]{2,1,0:T(8,128)S(1)}, u32[]{:S(2)}, u32[]{:S(2)}) collective-permute-start(f32[4,136,128]{2,1,0:T(8,128)S(1)} %pad_maximum_fusion), channel_id=1, source_target_pairs={{0,8},{8,16},{16,24},{24,32},{32,40},{40,48},{48,56},{56,64},{64,7... | collective-permute-start | bytes 835592 | tf_op jit(solution)/shard_map/ppermute | solution.py:25
  16.3 9.4 %collective-permute-start.1 = (f32[4,136,128]{2,1,0:T(8,128)S(1)}, f32[4,136,128]{2,1,0:T(8,128)S(1)}, u32[]{:S(2)}, u32[]{:S(2)}) collective-permute-start(f32[4,136,128]{2,1,0:T(8,128)S(1)} %pad_maximum_fusion), channel_id=1, source_target_pairs={{0,16},{8,24},{16,32},{24,40},{32,48},{40,56},{48,64},{56,72},{64,... | collective-permute-start | bytes 835592 | tf_op jit(solution)/shard_map/ppermute | solution.py:25
  25.9 10.7 %collective-permute-start.2 = (f32[4,136,128]{2,1,0:T(8,128)S(1)}, f32[4,136,128]{2,1,0:T(8,128)S(1)}, u32[]{:S(2)}, u32[]{:S(2)}) collective-permute-start(f32[4,136,128]{2,1,0:T(8,128)S(1)} %multiply_add_fusion.3), channel_id=1, source_target_pairs={{0,16},{8,24},{16,32},{24,40},{32,48},{40,56},{48,64},{56,72},{64,... | collective-permute-start | bytes 835592 | tf_op jit(solution)/shard_map/ppermute | solution.py:25
  36.7 10.8 %collective-permute-start.3 = (f32[4,136,128]{2,1,0:T(8,128)S(1)}, f32[4,136,128]{2,1,0:T(8,128)S(1)}, u32[]{:S(2)}, u32[]{:S(2)}) collective-permute-start(f32[4,136,128]{2,1,0:T(8,128)S(1)} %multiply_add_fusion.2), channel_id=1, source_target_pairs={{0,32},{8,40},{16,48},{24,56},{32,64},{40,72},{48,80},{56,88},{64,... | collective-permute-start | bytes 835592 | tf_op jit(solution)/shard_map/ppermute | solution.py:25
  47.7 15.4 %collective-permute-start.4 = (f32[4,136,128]{2,1,0:T(8,128)S(1)}, f32[4,136,128]{2,1,0:T(8,128)S(1)}, u32[]{:S(2)}, u32[]{:S(2)}) collective-permute-start(f32[4,136,128]{2,1,0:T(8,128)S(1)} %multiply_add_fusion.1), channel_id=1, source_target_pairs={{0,64},{8,72},{16,80},{24,88},{32,96},{40,104},{48,112},{56,120},{... | collective-permute-start | bytes 835592 | tf_op jit(solution)/shard_map/ppermute | solution.py:25
  63.2 10.2 %collective-permute-start.5 = (f32[4,136,128]{2,1,0:T(8,128)S(1)}, f32[4,136,128]{2,1,0:T(8,128)S(1)}, u32[]{:S(2)}, u32[]{:S(2)}) collective-permute-start(f32[4,136,128]{2,1,0:T(8,128)S(1)} %multiply_add_fusion), channel_id=1, source_target_pairs={{0,128},{8,136},{16,144},{24,152},{32,160},{40,168},{48,176},{56,1... | collective-permute-start | bytes 835592 | tf_op jit(solution)/shard_map/ppermute | solution.py:25
  75.2 2.3 copy-start.2
  79.6 40.2 %copy-start.7 = (s32[128,2]{0,1:T(2,128)S(1)}, s32[128,2]{0,1:T(2,128)}, u32[]{:S(2)}) copy-start(s32[128,2]{0,1:T(2,128)} %param.25) | copy-start | bytes 3076
  79.6 32.7 %all-to-all-start = ((bf16[8,128,384]{2,1,0:T(8,128)(2,1)}), bf16[8,128,384]{2,1,0:T(8,128)(2,1)}, u32[]{:S(2)}, u32[]{:S(2)}) async-start(bf16[8,128,384]{2,1,0:T(8,128)(2,1)} %fusion.15), calls=%async_computation | async-start | bytes 1572864 | tf_op jit(solution)/shard_map/all_to_all | solution.py:119
  113.6 31.2 %copy-start.6 = (f32[3072]{0:T(1024)S(1)}, f32[3072]{0:T(1024)}, u32[]{:S(2)}) copy-start(f32[3072]{0:T(1024)} %param.20) | copy-start | bytes 36868
  115.5 24.9 %all-to-all-start.1 = ((bf16[8,128,384]{2,1,0:T(8,128)(2,1)}), bf16[8,128,384]{2,1,0:T(8,128)(2,1)}, u32[]{:S(2)}, u32[]{:S(2)}) async-start(bf16[8,128,384]{2,1,0:T(8,128)(2,1)} %broadcast_in_dim.119), calls=%async_computation.1 | async-start | bytes 1572864 | tf_op jit(solution)/shard_map/all_to_all | solution.py:129
  119.7 152.4 %reduce-scatter.4.cloned.1.call-start = ((), (), s32[]{:S(2)}) async-start(), calls=%async_computation.6 | async-start | bytes 3538944
  144.3 0.5 copy-start.9
  163.5 50.3 %copy-start.10 = (bf16[1,3072,576]{1,2,0:T(8,128)(2,1)S(1)}, bf16[1,3072,576]{1,2,0:T(8,128)(2,1)}, u32[]{:S(2)}) copy-start(bf16[1,3072,576]{1,2,0:T(8,128)(2,1)} %param.22) | copy-start | bytes 10616836
  212.1 1.7 copy-start.1
  274.0 20.9 %all-to-all-start.3 = ((bf16[32,16,384]{2,1,0:T(8,128)(2,1)}), bf16[32,16,384]{2,1,0:T(8,128)(2,1)}, u32[]{:S(2)}, u32[]{:S(2)}) async-start(bf16[32,16,384]{2,1,0:T(8,128)(2,1)} %bitcast.150), calls=%async_computation.3 | async-start | bytes 786432 | tf_op jit(solution)/shard_map/all_to_all | solution.py:163
Sparse Core Ops, SparseCore 0:
  9.8 60.5 all-gather.2
  231.3 40.7 reduce-scatter.3

commit v4 on v3

--- a/solution.py
+++ b/solution.py
@@ -24,11 +24,18 @@
         pairs = [(k, k + distance) for k in range(peers - distance)]
         return lax.ppermute(value, axis, pairs)
 
-    before = combine(shifted(packed, 2), shifted(packed, 1))
-    distance = 2
-    while distance < peers:
-        before = combine(shifted(before, distance), before)
-        distance *= 2
+    radix = 4
+    before = shifted(packed, 1)
+    for distance in range(2, radix + 1):
+        before = combine(shifted(packed, distance), before)
+    covered = radix
+    while covered < peers:
+        reached = before
+        for times in range(1, radix):
+            if covered * times < peers:
+                reached = combine(shifted(before, covered * times), reached)
+        before = reached
+        covered *= radix
     return before[:, :head_size]
 
 
@@ -115,15 +122,10 @@
     slice_start = lax.axis_index("head") * slice_width
     partial_out = jnp.einsum(
         "tk,ckd->tcd", heads_normed, weight_blocks, preferred_element_type=jnp.float32
-    ).reshape(token_count, head_count, slice_width)
-    pieces = lax.all_to_all(
-        partial_out.astype(jnp.bfloat16).transpose(1, 0, 2),
-        "head",
-        split_axis=0,
-        concat_axis=0,
-        tiled=True,
-    )
-    projected = jnp.sum(pieces.astype(jnp.float32), axis=0)
+    ).reshape(token_count, model_width)
+    projected = lax.psum_scatter(
+        partial_out.astype(jnp.bfloat16), "head", scatter_dimension=1, tiled=True
+    ).astype(jnp.float32)
     own_residual = lax.dynamic_slice_in_dim(residual, slice_start, slice_width, 1)
     mixed_slice = (own_residual.astype(jnp.float32) + projected).astype(jnp.bfloat16)
     mixed_all = lax.all_to_all(

time: 317 us -> 338 us (1.066)
  waiting for transfers between devices: 97.3 us -> 119 us
  starting transfers between devices: 58.8 us -> 48.7 us
  local copies, waits for them, and re-layouts: 57.1 us -> 63.8 us
  blocking collectives: 48.6 us -> 52.2 us
    unnamed x3 -> x5, waiting for transfers between devices: 40.3 us -> 76.9 us
    all_to_all x1 -> x0, waiting for transfers between devices: 21.1 us -> none  [body(): lax.all_to_all(partial_out.astype(jnp.bfloat16).transpose(1, 0, 2), 'head...]
    all_to_all x1 -> x0, starting transfers between devices: 11.6 us -> none  [body(): lax.all_to_all(partial_out.astype(jnp.bfloat16).transpose(1, 0, 2), 'head...]
    unnamed x27 -> x30, local copies, waits for them, and re-layouts: 13.1 us -> 20.1 us
    ppermute x6 -> x8, waiting for transfers between devices: 28 us -> 34.7 us  [shifted(): return lax.ppermute(value, axis, pairs)]
    all_to_all x1, blocking collectives: 48.6 us -> 52.2 us  [body(): lax.all_to_all(packed.reshape(experts_total, capacity, width_here), 'ctx'...]
    ppermute x6 -> x8, starting transfers between devices: 32.2 us -> 33.3 us  [shifted(): return lax.ppermute(value, axis, pairs)]
  transfers between devices with their start and end apart: 11 -> 13, of which waited for: 10 -> 7; matrix products, arithmetic and copies ran while one was open for 10% -> 10% of each run, Pallas kernels for 0% -> 0%
where the time goes in v4:
time: 338 us; the launch traced here: 336 us
  waiting for transfers between devices  119 us (35%)
  local copies, waits for them, and re-layouts  63.8 us (19%)
  blocking collectives  52.2 us (15%)
  starting transfers between devices  48.7 us (14%)
  matrix products  19.7 us (6%)
  other arithmetic  19.5 us (6%)
  between operations  13.4 us (4%)
    unnamed x5, waiting for transfers between devices  76.9 us
    all_to_all x1, blocking collectives, body(): lax.all_to_all(packed.reshape(experts_total, capacity, width_here), 'ctx'...  52.2 us
    ppermute x8, waiting for transfers between devices, shifted(): return lax.ppermute(value, axis, pairs)  34.7 us
    ppermute x8, starting transfers between devices, shifted(): return lax.ppermute(value, axis, pairs)  33.3 us
    unnamed x30, local copies, waits for them, and re-layouts  20.1 us
    all_to_all x1, starting transfers between devices, body(): lax.all_to_all(summed.reshape(experts_total, capacity, slice_width), 'ctx...  10.7 us
    dot_general x1, matrix products, body(): jnp.dot(hidden, w_down[0], preferred_element_type=jnp.float32)  9.52 us
    all_to_all x1, waiting for transfers between devices, body(): lax.all_to_all(summed.reshape(experts_total, capacity, slice_width), 'ctx...  7.49 us
  transfers between devices with their start and end apart: 13, of which 7 were waited for; matrix products, arithmetic and copies ran while one was open for 10% of the time, Pallas kernels for 0%

profile of v4, /device:TPU:1, one launch (start us, length us, event | category | flops | bytes accessed | tf_op | source)
XLA Modules:
  0.0 336.4 jit_solution(10608454783317532350)
XLA Ops:
  7.3 1.9 copy.125
  11.8 4.5 %collective-permute-start = (f32[4,136,128]{2,1,0:T(8,128)S(1)}, f32[4,136,128]{2,1,0:T(8,128)S(1)}, u32[]{:S(2)}, u32[]{:S(2)}) collective-permute-start(f32[4,136,128]{2,1,0:T(8,128)S(1)} %pad_maximum_fusion), channel_id=1, source_target_pairs={{0,8},{8,16},{16,24},{24,32},{32,40},{40,48},{48,56},{56,64},{64,7... | collective-permute-start | bytes 835592 | tf_op jit(solution)/shard_map/ppermute | solution.py:25
  16.3 3.1 collective-permute-start.1
  19.5 3.4 %collective-permute-start.2 = (f32[4,136,128]{2,1,0:T(8,128)S(1)}, f32[4,136,128]{2,1,0:T(8,128)S(1)}, u32[]{:S(2)}, u32[]{:S(2)}) collective-permute-start(f32[4,136,128]{2,1,0:T(8,128)S(1)} %pad_maximum_fusion), channel_id=1, source_target_pairs={{0,24},{8,32},{16,40},{24,48},{32,56},{40,64},{48,72},{56,80},{64,... | collective-permute-start | bytes 835592 | tf_op jit(solution)/shard_map/ppermute | solution.py:25
  22.9 3.4 %collective-permute-start.3 = (f32[4,136,128]{2,1,0:T(8,128)S(1)}, f32[4,136,128]{2,1,0:T(8,128)S(1)}, u32[]{:S(2)}, u32[]{:S(2)}) collective-permute-start(f32[4,136,128]{2,1,0:T(8,128)S(1)} %pad_maximum_fusion), channel_id=1, source_target_pairs={{0,32},{8,40},{16,48},{24,56},{32,64},{40,72},{48,80},{56,88},{64,... | collective-permute-start | bytes 835592 | tf_op jit(solution)/shard_map/ppermute | solution.py:25
  26.8 6.5 %collective-permute-done.2 = f32[4,136,128]{2,1,0:T(8,128)S(1)} collective-permute-done((f32[4,136,128]{2,1,0:T(8,128)S(1)}, f32[4,136,128]{2,1,0:T(8,128)S(1)}, u32[]{:S(2)}, u32[]{:S(2)}) %collective-permute-start.2) | collective-permute-done | bytes 278560 | tf_op jit(solution)/shard_map/ppermute | solution.py:25
  33.5 5.8 %collective-permute-done.3 = f32[4,136,128]{2,1,0:T(8,128)S(1)} collective-permute-done((f32[4,136,128]{2,1,0:T(8,128)S(1)}, f32[4,136,128]{2,1,0:T(8,128)S(1)}, u32[]{:S(2)}, u32[]{:S(2)}) %collective-permute-start.3) | collective-permute-done | bytes 278560 | tf_op jit(solution)/shard_map/ppermute | solution.py:25
  39.4 5.4 %collective-permute-start.4 = (f32[4,136,128]{2,1,0:T(8,128)S(1)}, f32[4,136,128]{2,1,0:T(8,128)S(1)}, u32[]{:S(2)}, u32[]{:S(2)}) collective-permute-start(f32[4,136,128]{2,1,0:T(8,128)S(1)} %multiply_add_fusion.3), channel_id=1, source_target_pairs={{0,32},{8,40},{16,48},{24,56},{32,64},{40,72},{48,80},{56,88},{64,... | collective-permute-start | bytes 835592 | tf_op jit(solution)/shard_map/ppermute | solution.py:25
  44.8 3.2 collective-permute-start.5
  48.1 6.2 %collective-permute-start.6 = (f32[4,136,128]{2,1,0:T(8,128)S(1)}, f32[4,136,128]{2,1,0:T(8,128)S(1)}, u32[]{:S(2)}, u32[]{:S(2)}) collective-permute-start(f32[4,136,128]{2,1,0:T(8,128)S(1)} %multiply_add_fusion.3), channel_id=1, source_target_pairs={{0,96},{8,104},{16,112},{24,120},{32,128},{40,136},{48,144},{56,15... | collective-permute-start | bytes 835592 | tf_op jit(solution)/shard_map/ppermute | solution.py:25
  54.6 17.2 %collective-permute-done.5 = f32[4,136,128]{2,1,0:T(8,128)S(1)} collective-permute-done((f32[4,136,128]{2,1,0:T(8,128)S(1)}, f32[4,136,128]{2,1,0:T(8,128)S(1)}, u32[]{:S(2)}, u32[]{:S(2)}) %collective-permute-start.5) | collective-permute-done | bytes 278560 | tf_op jit(solution)/shard_map/ppermute | solution.py:25
  72.2 4.0 %collective-permute-start.7 = (f32[4,136,128]{2,1,0:T(8,128)S(1)}, f32[4,136,128]{2,1,0:T(8,128)S(1)}, u32[]{:S(2)}, u32[]{:S(2)}) collective-permute-start(f32[4,136,128]{2,1,0:T(8,128)S(1)} %multiply_add_fusion), channel_id=1, source_target_pairs={{0,128},{8,136},{16,144},{24,152},{32,160},{40,168},{48,176},{56,1... | collective-permute-start | bytes 835592 | tf_op jit(solution)/shard_map/ppermute | solution.py:25
  76.6 5.2 %collective-permute-done.7 = f32[4,136,128]{2,1,0:T(8,128)S(1)} collective-permute-done((f32[4,136,128]{2,1,0:T(8,128)S(1)}, f32[4,136,128]{2,1,0:T(8,128)S(1)}, u32[]{:S(2)}, u32[]{:S(2)}) %collective-permute-start.7) | collective-permute-done | bytes 278560 | tf_op jit(solution)/shard_map/ppermute | solution.py:25
  83.5 3.1 copy.137
  86.6 1.8 copy.111
  88.4 2.1 convolution_convert_fusion.1
  90.5 2.3 copy.128
  92.8 35.8 %reduce-scatter.7.cloned.1.call-done = bf16[384,128]{1,0:T(8,128)(2,1)} async-done(((bf16[3072,128]{1,0:T(8,128)(2,1)}), bf16[384,128]{1,0:T(8,128)(2,1)}) %reduce-scatter.7.cloned.1.call-update) | async-done | bytes 98320
  128.6 1.6 copy.129
  132.1 4.4 %all-to-all-start = ((bf16[8,128,384]{2,1,0:T(8,128)(2,1)}), bf16[8,128,384]{2,1,0:T(8,128)(2,1)}, u32[]{:S(2)}, u32[]{:S(2)}) async-start(bf16[8,128,384]{2,1,0:T(8,128)(2,1)} %broadcast_in_dim.139), calls=%async_computation | async-start | bytes 1572864 | tf_op jit(solution)/shard_map/all_to_all | solution.py:131
  137.5 1.6 eq.39
  139.1 1.5 eq.35
  141.9 1.9 reduce-window.6
  154.3 1.6 reshape.147
  157.1 2.3 copy.112
  159.4 1.6 multiply_reduce_fusion
  161.5 2.9 multiply_convert_fusion
  164.4 2.3 copy.118
  166.7 3.1 broadcast_in_dim.143
  169.8 4.6 %reshape.167 = bf16[256,3072]{1,0:T(8,128)(2,1)} reshape(bf16[128,2,3072]{2,1,0:T(2,128)(2,1)} %broadcast_in_dim.143) | data formatting | bytes 3145728 | tf_op jit(solution)/shard_map/reshape | solution.py:148
  174.4 5.8 %scatter_custom_fusion = bf16[512,3072]{1,0:T(8,128)(2,1)} fusion(s32[256]{0:T(256)} %bitcast.157, bf16[256,3072]{1,0:T(8,128)(2,1)} %reshape.167, bf16[]{:T(256)} %constant.40.clone.1), kind=kCustom, calls=%fused_computation.10 | custom fusion | bytes 3146240 | tf_op jit(solution)/shard_map/scatter | solution.py:149
  180.2 52.2 %all_to_all.15 = bf16[32,16,3072]{2,1,0:T(8,128)(2,1)S(1)} all-to-all(bf16[32,16,3072]{2,1,0:T(8,128)(2,1)} %bitcast.141), channel_id=1, replica_groups=mesh['ctx'=32,'head'=8] {'ctx'}, dimensions={0} | all-to-all | bytes 6291456 | tf_op jit(solution)/shard_map/all_to_all | solution.py:150
  232.3 1.7 copy-done.1
  234.0 3.2 fusion.3
  237.2 9.5 %convolution_convert_fusion = bf16[512,3072]{1,0:T(8,128)(2,1)} fusion(bf16[1,576,3072]{2,1,0:T(8,128)(2,1)S(1)} %copy-done, bf16[512,3072]{1,0:T(8,128)(2,1)} %bitcast.148, bf16[1,3072,576]{1,2,0:T(8,128)(2,1)} %param.23, f32[512,576]{0,1:T(8,128)} %fusion.3), kind=kOutput, calls=%fused_computation.2 | convolution fusion | flops 3627220992 | bytes 14548992 | tf_op jit(solution)/shard_map/dot_general | solution.py:161
  246.7 4.7 %copy.130 = bf16[512,3072]{0,1:T(8,128)(2,1)} copy(bf16[512,3072]{1,0:T(8,128)(2,1)} %convolution_convert_fusion) | data formatting | bytes 6291456
  252.7 40.4 %reduce-scatter.9.cloned.1.call-done = bf16[384,512]{1,0:T(8,128)(2,1)} async-done(((bf16[3072,512]{1,0:T(8,128)(2,1)}), bf16[384,512]{1,0:T(8,128)(2,1)}) %reduce-scatter.9.cloned.1.call-update) | async-done | bytes 393232
  293.1 1.9 copy.131
  295.1 10.7 %all-to-all-start.2 = ((bf16[32,16,384]{2,1,0:T(8,128)(2,1)}), bf16[32,16,384]{2,1,0:T(8,128)(2,1)}, u32[]{:S(2)}, u32[]{:S(2)}) async-start(bf16[32,16,384]{2,1,0:T(8,128)(2,1)} %bitcast.150), calls=%async_computation.2 | async-start | bytes 786432 | tf_op jit(solution)/shard_map/all_to_all | solution.py:165
  305.8 2.7 fusion.15
  308.5 7.5 %all-to-all-done.2 = bf16[32,16,384]{2,1,0:T(8,128)(2,1)} async-done(((bf16[32,16,384]{2,1,0:T(8,128)(2,1)}), bf16[32,16,384]{2,1,0:T(8,128)(2,1)}, u32[]{:S(2)}, u32[]{:S(2)}) %all-to-all-start.2) | async-done | bytes 393248 | tf_op jit(solution)/shard_map/all_to_all | solution.py:165
  316.0 3.0 gather_fusion
  318.9 1.9 reshape.154
  320.8 2.2 fusion.58
  323.0 1.7 copy.132
  324.7 1.7 copy.133
  326.5 1.8 fusion.34
  328.2 1.6 copy.121
  (76 shorter events, 24.6 us)
Async XLA Ops:
  6.5 230.7 %copy-start = (bf16[1,576,3072]{2,1,0:T(8,128)(2,1)S(1)}, bf16[1,576,3072]{2,1,0:T(8,128)(2,1)}, u32[]{:S(2)}) copy-start(bf16[1,576,3072]{2,1,0:T(8,128)(2,1)} %param.24) | copy-start | bytes 10616836
  6.5 77.0 %all-gather.3.cloned.1.call-start = ((), (), s32[]{:S(2)}) async-start(), calls=%async_computation.5 | async-start | bytes 3244032 | tf_op jit(solution)/shard_map/all_gather | solution.py:117
  7.3 121.3 %reduce-scatter.7.cloned.1.call-start = ((), (), s32[]{:S(2)}) async-start(), calls=%async_computation.6 | async-start | bytes 884736
  10.2 66.0 %copy-start.4 = (bf16[128,512]{0,1:T(8,128)(2,1)S(1)}, bf16[128,512]{0,1:T(8,128)(2,1)}, u32[]{:S(2)}) copy-start(bf16[128,512]{0,1:T(8,128)(2,1)} %copy.125) | copy-start | bytes 393220
  10.2 66.0 %copy-start.5 = (bf16[128,512]{1,0:T(8,128)(2,1)S(1)}, bf16[128,512]{1,0:T(8,128)(2,1)}, u32[]{:S(2)}) copy-start(bf16[128,512]{1,0:T(8,128)(2,1)} %param.13) | copy-start | bytes 393220
  11.8 14.6 %collective-permute-start = (f32[4,136,128]{2,1,0:T(8,128)S(1)}, f32[4,136,128]{2,1,0:T(8,128)S(1)}, u32[]{:S(2)}, u32[]{:S(2)}) collective-permute-start(f32[4,136,128]{2,1,0:T(8,128)S(1)} %pad_maximum_fusion), channel_id=1, source_target_pairs={{0,8},{8,16},{16,24},{24,32},{32,40},{40,48},{48,56},{56,64},{64,7... | collective-permute-start | bytes 835592 | tf_op jit(solution)/shard_map/ppermute | solution.py:25
  16.3 10.2 %collective-permute-start.1 = (f32[4,136,128]{2,1,0:T(8,128)S(1)}, f32[4,136,128]{2,1,0:T(8,128)S(1)}, u32[]{:S(2)}, u32[]{:S(2)}) collective-permute-start(f32[4,136,128]{2,1,0:T(8,128)S(1)} %pad_maximum_fusion), channel_id=1, source_target_pairs={{0,16},{8,24},{16,32},{24,40},{32,48},{40,56},{48,64},{56,72},{64,... | collective-permute-start | bytes 835592 | tf_op jit(solution)/shard_map/ppermute | solution.py:25
  19.5 13.8 %collective-permute-start.2 = (f32[4,136,128]{2,1,0:T(8,128)S(1)}, f32[4,136,128]{2,1,0:T(8,128)S(1)}, u32[]{:S(2)}, u32[]{:S(2)}) collective-permute-start(f32[4,136,128]{2,1,0:T(8,128)S(1)} %pad_maximum_fusion), channel_id=1, source_target_pairs={{0,24},{8,32},{16,40},{24,48},{32,56},{40,64},{48,72},{56,80},{64,... | collective-permute-start | bytes 835592 | tf_op jit(solution)/shard_map/ppermute | solution.py:25
  22.9 16.4 %collective-permute-start.3 = (f32[4,136,128]{2,1,0:T(8,128)S(1)}, f32[4,136,128]{2,1,0:T(8,128)S(1)}, u32[]{:S(2)}, u32[]{:S(2)}) collective-permute-start(f32[4,136,128]{2,1,0:T(8,128)S(1)} %pad_maximum_fusion), channel_id=1, source_target_pairs={{0,32},{8,40},{16,48},{24,56},{32,64},{40,72},{48,80},{56,88},{64,... | collective-permute-start | bytes 835592 | tf_op jit(solution)/shard_map/ppermute | solution.py:25
  26.7 55.6 %copy-start.3 = (bf16[128,512]{1,0:T(8,128)(2,1)S(1)}, bf16[128,512]{1,0:T(8,128)(2,1)}, u32[]{:S(2)}) copy-start(bf16[128,512]{1,0:T(8,128)(2,1)} %param.15) | copy-start | bytes 393220
  33.4 49.4 %copy-start.8 = (f32[512]{0:T(512)S(1)}, f32[512]{0:T(512)}, u32[]{:S(2)}) copy-start(f32[512]{0:T(512)} %param.19) | copy-start | bytes 6148
  39.4 15.0 %collective-permute-start.4 = (f32[4,136,128]{2,1,0:T(8,128)S(1)}, f32[4,136,128]{2,1,0:T(8,128)S(1)}, u32[]{:S(2)}, u32[]{:S(2)}) collective-permute-start(f32[4,136,128]{2,1,0:T(8,128)S(1)} %multiply_add_fusion.3), channel_id=1, source_target_pairs={{0,32},{8,40},{16,48},{24,56},{32,64},{40,72},{48,80},{56,88},{64,... | collective-permute-start | bytes 835592 | tf_op jit(solution)/shard_map/ppermute | solution.py:25
  44.8 27.0 %collective-permute-start.5 = (f32[4,136,128]{2,1,0:T(8,128)S(1)}, f32[4,136,128]{2,1,0:T(8,128)S(1)}, u32[]{:S(2)}, u32[]{:S(2)}) collective-permute-start(f32[4,136,128]{2,1,0:T(8,128)S(1)} %multiply_add_fusion.3), channel_id=1, source_target_pairs={{0,64},{8,72},{16,80},{24,88},{32,96},{40,104},{48,112},{56,120},{... | collective-permute-start | bytes 835592 | tf_op jit(solution)/shard_map/ppermute | solution.py:25
  48.1 24.1 %collective-permute-start.6 = (f32[4,136,128]{2,1,0:T(8,128)S(1)}, f32[4,136,128]{2,1,0:T(8,128)S(1)}, u32[]{:S(2)}, u32[]{:S(2)}) collective-permute-start(f32[4,136,128]{2,1,0:T(8,128)S(1)} %multiply_add_fusion.3), channel_id=1, source_target_pairs={{0,96},{8,104},{16,112},{24,120},{32,128},{40,136},{48,144},{56,15... | collective-permute-start | bytes 835592 | tf_op jit(solution)/shard_map/ppermute | solution.py:25
  72.2 9.5 %collective-permute-start.7 = (f32[4,136,128]{2,1,0:T(8,128)S(1)}, f32[4,136,128]{2,1,0:T(8,128)S(1)}, u32[]{:S(2)}, u32[]{:S(2)}) collective-permute-start(f32[4,136,128]{2,1,0:T(8,128)S(1)} %multiply_add_fusion), channel_id=1, source_target_pairs={{0,128},{8,136},{16,144},{24,152},{32,160},{40,168},{48,176},{56,1... | collective-permute-start | bytes 835592 | tf_op jit(solution)/shard_map/ppermute | solution.py:25
  86.6 1.8 copy-start.2
  90.5 46.3 %copy-start.7 = (s32[128,2]{0,1:T(2,128)S(1)}, s32[128,2]{0,1:T(2,128)}, u32[]{:S(2)}) copy-start(s32[128,2]{0,1:T(2,128)} %param.25) | copy-start | bytes 3076
  92.8 68.7 %copy-start.6 = (f32[3072]{0:T(1024)S(1)}, f32[3072]{0:T(1024)}, u32[]{:S(2)}) copy-start(f32[3072]{0:T(1024)} %param.20) | copy-start | bytes 36868
  132.1 24.9 %all-to-all-start = ((bf16[8,128,384]{2,1,0:T(8,128)(2,1)}), bf16[8,128,384]{2,1,0:T(8,128)(2,1)}, u32[]{:S(2)}, u32[]{:S(2)}) async-start(bf16[8,128,384]{2,1,0:T(8,128)(2,1)} %broadcast_in_dim.139), calls=%async_computation | async-start | bytes 1572864 | tf_op jit(solution)/shard_map/all_to_all | solution.py:131
  136.6 156.6 %reduce-scatter.9.cloned.1.call-start = ((), (), s32[]{:S(2)}) async-start(), calls=%async_computation.7 | async-start | bytes 3538944
  161.0 0.5 copy-start.9
  180.2 53.9 %copy-start.10 = (bf16[1,3072,576]{1,2,0:T(8,128)(2,1)S(1)}, bf16[1,3072,576]{1,2,0:T(8,128)(2,1)}, u32[]{:S(2)}) copy-start(bf16[1,3072,576]{1,2,0:T(8,128)(2,1)} %param.22) | copy-start | bytes 10616836
  232.3 1.7 copy-start.1
  295.1 20.9 %all-to-all-start.2 = ((bf16[32,16,384]{2,1,0:T(8,128)(2,1)}), bf16[32,16,384]{2,1,0:T(8,128)(2,1)}, u32[]{:S(2)}, u32[]{:S(2)}) async-start(bf16[32,16,384]{2,1,0:T(8,128)(2,1)} %bitcast.150), calls=%async_computation.2 | async-start | bytes 786432 | tf_op jit(solution)/shard_map/all_to_all | solution.py:165
Sparse Core Ops, SparseCore 0:
  9.8 67.8 all-gather.2
  92.9 35.6 reduce-scatter.6
  251.6 41.5 reduce-scatter.8

commit v5 on v3

--- a/solution.py
+++ b/solution.py
@@ -143,8 +143,11 @@
     gate_weights, slot_index = route_tokens(logits, expert_ids, experts_total)
     target = (expert_ids * capacity + slot_index).reshape(-1)
     width_here = moe_in.shape[1]
-    source = jnp.repeat(moe_in, TOP, axis=0)
-    packed = jnp.zeros((experts_total * capacity, width_here), jnp.bfloat16).at[target].set(source)
+    slots = lax.broadcasted_iota(jnp.int32, (experts_total * capacity, token_count, TOP), 0)
+    chosen = jnp.any(slots == target.reshape(token_count, TOP)[None], axis=2)
+    packed = jnp.dot(
+        chosen.astype(jnp.bfloat16), moe_in, preferred_element_type=jnp.float32
+    ).astype(jnp.bfloat16)
     arrived = lax.all_to_all(
         packed.reshape(experts_total, capacity, width_here),
         "ctx",
@@ -168,10 +171,17 @@
         tiled=True,
     )
     lookup = returned.reshape(experts_total * capacity, slice_width)
-    picked = lookup[target].reshape(token_count, TOP, slice_width).astype(jnp.float32)
-    final_out = (
-        base_slice + gate_weights[:, 0:1] * picked[:, 0] + gate_weights[:, 1:2] * picked[:, 1]
-    )
+    columns = lax.broadcasted_iota(jnp.int32, (token_count, experts_total * capacity), 1)
+    ranked = target.reshape(token_count, TOP)
+    picked = [
+        jnp.dot(
+            (columns == ranked[:, k : k + 1]).astype(jnp.bfloat16),
+            lookup,
+            preferred_element_type=jnp.float32,
+        )
+        for k in range(TOP)
+    ]
+    final_out = base_slice + gate_weights[:, 0:1] * picked[0] + gate_weights[:, 1:2] * picked[1]
     return final_out.astype(jnp.bfloat16)
 
 

time: 317 us -> 283 us (0.89)
  local copies, waits for them, and re-layouts: 57.1 us -> 21.8 us
  other arithmetic: 20.5 us -> 11.9 us
  waiting for transfers between devices: 97.3 us -> 103 us
  matrix products: 19.7 us -> 24.5 us
    all_to_all x1, waiting for transfers between devices: 0.39 us -> 10.7 us  [body(): lax.all_to_all(jnp.broadcast_to(mixed_slice[None], (head_count,) + mixed_...]
    reshape x2 -> x0, local copies, waits for them, and re-layouts: 6.18 us -> none  [the longest x1 4.61 us: body(): source = jnp.repeat(moe_in, TOP, axis=0)]
    scatter x1 -> x0, local copies, waits for them, and re-layouts: 5.75 us -> none  [body(): jnp.zeros((experts_total * capacity, width_here), jnp.bfloat16).at[target]]
    convert_element_type x3 -> x1, local copies, waits for them, and re-layouts: 5.79 us -> 0.16 us  [body(): mixed_wide = mixed_rows.astype(jnp.float32)]
    convert_element_type x2 -> x0, other arithmetic: 4.73 us -> none  [the longest x1 2.94 us: body(): moe_in = (scaled * inv_rms).astype(jnp.bfloat16)]
    unnamed x3, waiting for transfers between devices: 40.3 us -> 36 us
    dot_general x0 -> x3, matrix products: none -> 4.3 us  [the longest x2 3.25 us: body(): jnp.dot((columns == ranked[:, k:k + 1]).astype(jnp.bfloat16), lookup, pre...]
    unnamed x27 -> x31, local copies, waits for them, and re-layouts: 13.1 us -> 9.63 us
  transfers between devices with their start and end apart: 11 -> 11, of which waited for: 10 -> 10; matrix products, arithmetic and copies ran while one was open for 10% -> 8% of each run, Pallas kernels for 0% -> 0%
where the time goes in v5:
time: 283 us; the launch traced here: 282 us
  waiting for transfers between devices  103 us (36%)
  starting transfers between devices  58.8 us (21%)
  blocking collectives  48.4 us (17%)
  matrix products  24.5 us (9%)
  local copies, waits for them, and re-layouts  21.8 us (8%)
  between operations  13.7 us (5%)
  other arithmetic  11.9 us (4%)
    all_to_all x1, blocking collectives, body(): lax.all_to_all(packed.reshape(experts_total, capacity, width_here), 'ctx'...  48.4 us
    unnamed x3, waiting for transfers between devices  36 us
    ppermute x6, starting transfers between devices, shifted(): return lax.ppermute(value, axis, pairs)  32.2 us
    ppermute x6, waiting for transfers between devices, shifted(): return lax.ppermute(value, axis, pairs)  28 us
    all_to_all x1, waiting for transfers between devices, body(): lax.all_to_all(partial_out.astype(jnp.bfloat16).transpose(1, 0, 2), 'head...  21.1 us
    all_to_all x1, starting transfers between devices, body(): lax.all_to_all(partial_out.astype(jnp.bfloat16).transpose(1, 0, 2), 'head...  11.6 us
    all_to_all x1, starting transfers between devices, body(): lax.all_to_all(summed.reshape(experts_total, capacity, slice_width), 'ctx...  10.7 us
    all_to_all x1, waiting for transfers between devices, body(): lax.all_to_all(jnp.broadcast_to(mixed_slice[None], (head_count,) + mixed_...  10.7 us
  transfers between devices with their start and end apart: 11, of which 10 were waited for; matrix products, arithmetic and copies ran while one was open for 8% of the time, Pallas kernels for 0%

profile of v5, /device:TPU:1, one launch (start us, length us, event | category | flops | bytes accessed | tf_op | source)
XLA Modules:
  0.0 281.9 jit_solution(15608541897899543348)
XLA Ops:
  7.3 2.0 copy.101
  9.3 1.0 reduce_window_sum.26
  10.5 1.2 fusion.36
  11.8 4.5 %collective-permute-start = (f32[4,136,128]{2,1,0:T(8,128)S(1)}, f32[4,136,128]{2,1,0:T(8,128)S(1)}, u32[]{:S(2)}, u32[]{:S(2)}) collective-permute-start(f32[4,136,128]{2,1,0:T(8,128)S(1)} %pad_maximum_fusion), channel_id=1, source_target_pairs={{0,8},{8,16},{16,24},{24,32},{32,40},{40,48},{48,56},{56,64},{64,7... | collective-permute-start | bytes 835592 | tf_op jit(solution)/shard_map/ppermute | solution.py:25
  16.3 3.1 %collective-permute-start.1 = (f32[4,136,128]{2,1,0:T(8,128)S(1)}, f32[4,136,128]{2,1,0:T(8,128)S(1)}, u32[]{:S(2)}, u32[]{:S(2)}) collective-permute-start(f32[4,136,128]{2,1,0:T(8,128)S(1)} %pad_maximum_fusion), channel_id=1, source_target_pairs={{0,16},{8,24},{16,32},{24,40},{32,48},{40,56},{48,64},{56,72},{64,... | collective-permute-start | bytes 835592 | tf_op jit(solution)/shard_map/ppermute | solution.py:25
  19.5 0.8 collective-permute-done
  20.4 5.4 %collective-permute-done.1 = f32[4,136,128]{2,1,0:T(8,128)S(1)} collective-permute-done((f32[4,136,128]{2,1,0:T(8,128)S(1)}, f32[4,136,128]{2,1,0:T(8,128)S(1)}, u32[]{:S(2)}, u32[]{:S(2)}) %collective-permute-start.1) | collective-permute-done | bytes 278560 | tf_op jit(solution)/shard_map/ppermute | solution.py:25
  25.9 3.8 %collective-permute-start.2 = (f32[4,136,128]{2,1,0:T(8,128)S(1)}, f32[4,136,128]{2,1,0:T(8,128)S(1)}, u32[]{:S(2)}, u32[]{:S(2)}) collective-permute-start(f32[4,136,128]{2,1,0:T(8,128)S(1)} %multiply_add_fusion.3), channel_id=1, source_target_pairs={{0,16},{8,24},{16,32},{24,40},{32,48},{40,56},{48,64},{56,72},{64,... | collective-permute-start | bytes 835592 | tf_op jit(solution)/shard_map/ppermute | solution.py:25
  29.9 6.7 %collective-permute-done.2 = f32[4,136,128]{2,1,0:T(8,128)S(1)} collective-permute-done((f32[4,136,128]{2,1,0:T(8,128)S(1)}, f32[4,136,128]{2,1,0:T(8,128)S(1)}, u32[]{:S(2)}, u32[]{:S(2)}) %collective-permute-start.2) | collective-permute-done | bytes 278560 | tf_op jit(solution)/shard_map/ppermute | solution.py:25
  36.7 5.7 %collective-permute-start.3 = (f32[4,136,128]{2,1,0:T(8,128)S(1)}, f32[4,136,128]{2,1,0:T(8,128)S(1)}, u32[]{:S(2)}, u32[]{:S(2)}) collective-permute-start(f32[4,136,128]{2,1,0:T(8,128)S(1)} %multiply_add_fusion.2), channel_id=1, source_target_pairs={{0,32},{8,40},{16,48},{24,56},{32,64},{40,72},{48,80},{56,88},{64,... | collective-permute-start | bytes 835592 | tf_op jit(solution)/shard_map/ppermute | solution.py:25
  42.5 5.1 %collective-permute-done.3 = f32[4,136,128]{2,1,0:T(8,128)S(1)} collective-permute-done((f32[4,136,128]{2,1,0:T(8,128)S(1)}, f32[4,136,128]{2,1,0:T(8,128)S(1)}, u32[]{:S(2)}, u32[]{:S(2)}) %collective-permute-start.3) | collective-permute-done | bytes 278560 | tf_op jit(solution)/shard_map/ppermute | solution.py:25
  47.7 8.4 %collective-permute-start.4 = (f32[4,136,128]{2,1,0:T(8,128)S(1)}, f32[4,136,128]{2,1,0:T(8,128)S(1)}, u32[]{:S(2)}, u32[]{:S(2)}) collective-permute-start(f32[4,136,128]{2,1,0:T(8,128)S(1)} %multiply_add_fusion.1), channel_id=1, source_target_pairs={{0,64},{8,72},{16,80},{24,88},{32,96},{40,104},{48,112},{56,120},{... | collective-permute-start | bytes 835592 | tf_op jit(solution)/shard_map/ppermute | solution.py:25
  56.2 6.9 %collective-permute-done.4 = f32[4,136,128]{2,1,0:T(8,128)S(1)} collective-permute-done((f32[4,136,128]{2,1,0:T(8,128)S(1)}, f32[4,136,128]{2,1,0:T(8,128)S(1)}, u32[]{:S(2)}, u32[]{:S(2)}) %collective-permute-start.4) | collective-permute-done | bytes 278560 | tf_op jit(solution)/shard_map/ppermute | solution.py:25
  63.2 6.7 %collective-permute-start.5 = (f32[4,136,128]{2,1,0:T(8,128)S(1)}, f32[4,136,128]{2,1,0:T(8,128)S(1)}, u32[]{:S(2)}, u32[]{:S(2)}) collective-permute-start(f32[4,136,128]{2,1,0:T(8,128)S(1)} %multiply_add_fusion), channel_id=1, source_target_pairs={{0,128},{8,136},{16,144},{24,152},{32,160},{40,168},{48,176},{56,1... | collective-permute-start | bytes 835592 | tf_op jit(solution)/shard_map/ppermute | solution.py:25
  70.3 3.1 %collective-permute-done.5 = f32[4,136,128]{2,1,0:T(8,128)S(1)} collective-permute-done((f32[4,136,128]{2,1,0:T(8,128)S(1)}, f32[4,136,128]{2,1,0:T(8,128)S(1)}, u32[]{:S(2)}, u32[]{:S(2)}) %collective-permute-start.5) | collective-permute-done | bytes 278560 | tf_op jit(solution)/shard_map/ppermute | solution.py:25
  74.4 0.8 fusion.34
  75.2 2.3 copy.132
  77.5 2.1 fusion.14
  79.6 11.6 %all-to-all-start = ((bf16[8,128,384]{2,1,0:T(8,128)(2,1)}), bf16[8,128,384]{2,1,0:T(8,128)(2,1)}, u32[]{:S(2)}, u32[]{:S(2)}) async-start(bf16[8,128,384]{2,1,0:T(8,128)(2,1)} %fusion.14), calls=%async_computation | async-start | bytes 1572864 | tf_op jit(solution)/shard_map/all_to_all | solution.py:119
  91.2 21.1 %all-to-all-done = bf16[8,128,384]{2,1,0:T(8,128)(2,1)} async-done(((bf16[8,128,384]{2,1,0:T(8,128)(2,1)}), bf16[8,128,384]{2,1,0:T(8,128)(2,1)}, u32[]{:S(2)}, u32[]{:S(2)}) %all-to-all-start) | async-done | bytes 786464 | tf_op jit(solution)/shard_map/all_to_all | solution.py:119
  112.3 1.3 convert_reduce_fusion
  113.6 0.9 add_convert_fusion
  114.5 1.0 broadcast_in_dim.111
  115.5 4.2 %all-to-all-start.1 = ((bf16[8,128,384]{2,1,0:T(8,128)(2,1)}), bf16[8,128,384]{2,1,0:T(8,128)(2,1)}, u32[]{:S(2)}, u32[]{:S(2)}) async-start(bf16[8,128,384]{2,1,0:T(8,128)(2,1)} %broadcast_in_dim.111), calls=%async_computation.1 | async-start | bytes 1572864 | tf_op jit(solution)/shard_map/all_to_all | solution.py:129
  120.5 1.0 eq.67
  121.5 1.0 eq.63
  123.1 1.9 reduce-window.6
  124.9 0.9 slice_reduce_fusion
  125.9 0.9 fusion.52
  126.8 0.8 reshape.110
  127.6 0.9 copy.96
  129.8 10.7 %all-to-all-done.1 = bf16[8,128,384]{2,1,0:T(8,128)(2,1)} async-done(((bf16[8,128,384]{2,1,0:T(8,128)(2,1)}), bf16[8,128,384]{2,1,0:T(8,128)(2,1)}, u32[]{:S(2)}, u32[]{:S(2)}) %all-to-all-start.1) | async-done | bytes 786464 | tf_op jit(solution)/shard_map/all_to_all | solution.py:129
  140.4 1.3 convert_bitcast_fusion
  141.9 1.9 fusion.5
  143.8 1.0 convolution_convert_fusion.1
  144.9 48.4 %all_to_all.20 = bf16[32,16,3072]{2,1,0:T(8,128)(2,1)S(1)} all-to-all(bf16[32,16,3072]{2,1,0:T(8,128)(2,1)S(1)} %bitcast.140), channel_id=1, replica_groups=mesh['ctx'=32,'head'=8] {'ctx'}, dimensions={0} | all-to-all | bytes 6291456 | tf_op jit(solution)/shard_map/all_to_all | solution.py:151
  193.3 1.7 copy-done.2
  195.0 3.2 %fusion.3 = f32[512,576]{0,1:T(8,128)} fusion(bf16[512,3072]{1,0:T(8,128)(2,1)S(1)} %bitcast.143, bf16[1,3072,576]{1,2,0:T(8,128)(2,1)S(1)} %copy-done.13), kind=kOutput, calls=%fused_computation.5 | convolution fusion | flops 1811939328 | bytes 7864320 | tf_op jit(solution)/shard_map/dot_general | solution.py:159
  198.1 9.5 %convolution_convert_fusion = bf16[512,3072]{1,0:T(8,128)(2,1)} fusion(bf16[1,576,3072]{2,1,0:T(8,128)(2,1)S(1)} %copy-done, bf16[512,3072]{1,0:T(8,128)(2,1)} %bitcast.144, bf16[1,3072,576]{1,2,0:T(8,128)(2,1)} %param.23, f32[512,576]{0,1:T(8,128)} %fusion.3), kind=kOutput, calls=%fused_computation | convolution fusion | flops 3627220992 | bytes 14548992 | tf_op jit(solution)/shard_map/dot_general | solution.py:162
  207.7 4.7 %copy.105 = bf16[512,3072]{0,1:T(8,128)(2,1)} copy(bf16[512,3072]{1,0:T(8,128)(2,1)} %convolution_convert_fusion) | data formatting | bytes 6291456
  212.4 1.3 slice_bitcast_fusion
  213.7 35.3 %reduce-scatter.4.cloned.1.call-done = bf16[384,512]{1,0:T(8,128)(2,1)} async-done(((bf16[3072,512]{1,0:T(8,128)(2,1)}), bf16[384,512]{1,0:T(8,128)(2,1)}) %reduce-scatter.4.cloned.1.call-update) | async-done | bytes 393232
  249.0 1.9 copy.106
  250.9 10.7 %all-to-all-start.3 = ((bf16[32,16,384]{2,1,0:T(8,128)(2,1)}), bf16[32,16,384]{2,1,0:T(8,128)(2,1)}, u32[]{:S(2)}, u32[]{:S(2)}) async-start(bf16[32,16,384]{2,1,0:T(8,128)(2,1)} %bitcast.145), calls=%async_computation.3 | async-start | bytes 786432 | tf_op jit(solution)/shard_map/all_to_all | solution.py:166
  261.6 3.1 %fusion.18 = f32[128,32]{0,1:T(8,128)S(1)} fusion(f32[3072,32]{0,1:T(8,128)} %param.21, f32[128,3072]{1,0:T(8,128)} %bitcast.137, f32[3072]{0:T(1024)S(1)} %copy-done.8, f32[128]{0:T(128)} %copy-done.12), kind=kOutput, calls=%fused_computation.25 | convolution fusion | flops 151392256 | bytes 1995264 | tf_op jit(solution)/shard_map/dot_general | solution.py:141
  264.7 7.1 %all-to-all-done.3 = bf16[32,16,384]{2,1,0:T(8,128)(2,1)} async-done(((bf16[32,16,384]{2,1,0:T(8,128)(2,1)}), bf16[32,16,384]{2,1,0:T(8,128)(2,1)}, u32[]{:S(2)}, u32[]{:S(2)}) %all-to-all-start.3) | async-done | bytes 393248 | tf_op jit(solution)/shard_map/all_to_all | solution.py:166
  271.8 1.3 fusion.16
  273.2 1.9 fusion.17
  (61 shorter events, 6.2 us)
Async XLA Ops:
  6.5 191.6 %copy-start = (bf16[1,576,3072]{2,1,0:T(8,128)(2,1)S(1)}, bf16[1,576,3072]{2,1,0:T(8,128)(2,1)}, u32[]{:S(2)}) copy-start(bf16[1,576,3072]{2,1,0:T(8,128)(2,1)} %param.24) | copy-start | bytes 10616836
  6.5 68.6 %all-gather.3.cloned.1.call-start = ((), (), s32[]{:S(2)}) async-start(), calls=%async_computation.5 | async-start | bytes 3244032 | tf_op jit(solution)/shard_map/all_gather | solution.py:110
  10.2 59.7 %copy-start.5 = (bf16[128,512]{0,1:T(8,128)(2,1)S(1)}, bf16[128,512]{0,1:T(8,128)(2,1)}, u32[]{:S(2)}) copy-start(bf16[128,512]{0,1:T(8,128)(2,1)} %copy.101) | copy-start | bytes 393220
  10.2 59.7 %copy-start.7 = (bf16[128,512]{1,0:T(8,128)(2,1)S(1)}, bf16[128,512]{1,0:T(8,128)(2,1)}, u32[]{:S(2)}) copy-start(bf16[128,512]{1,0:T(8,128)(2,1)} %param.13) | copy-start | bytes 393220
  10.2 63.7 %copy-start.4 = (bf16[128,512]{1,0:T(8,128)(2,1)S(1)}, bf16[128,512]{1,0:T(8,128)(2,1)}, u32[]{:S(2)}) copy-start(bf16[128,512]{1,0:T(8,128)(2,1)} %param.15) | copy-start | bytes 393220
  11.8 62.5 %copy-start.11 = (f32[512]{0:T(512)S(1)}, f32[512]{0:T(512)}, u32[]{:S(2)}) copy-start(f32[512]{0:T(512)} %param.19) | copy-start | bytes 6148
  11.8 8.5 %collective-permute-start = (f32[4,136,128]{2,1,0:T(8,128)S(1)}, f32[4,136,128]{2,1,0:T(8,128)S(1)}, u32[]{:S(2)}, u32[]{:S(2)}) collective-permute-start(f32[4,136,128]{2,1,0:T(8,128)S(1)} %pad_maximum_fusion), channel_id=1, source_target_pairs={{0,8},{8,16},{16,24},{24,32},{32,40},{40,48},{48,56},{56,64},{64,7... | collective-permute-start | bytes 835592 | tf_op jit(solution)/shard_map/ppermute | solution.py:25
  16.3 9.4 %collective-permute-start.1 = (f32[4,136,128]{2,1,0:T(8,128)S(1)}, f32[4,136,128]{2,1,0:T(8,128)S(1)}, u32[]{:S(2)}, u32[]{:S(2)}) collective-permute-start(f32[4,136,128]{2,1,0:T(8,128)S(1)} %pad_maximum_fusion), channel_id=1, source_target_pairs={{0,16},{8,24},{16,32},{24,40},{32,48},{40,56},{48,64},{56,72},{64,... | collective-permute-start | bytes 835592 | tf_op jit(solution)/shard_map/ppermute | solution.py:25
  25.9 10.7 %collective-permute-start.2 = (f32[4,136,128]{2,1,0:T(8,128)S(1)}, f32[4,136,128]{2,1,0:T(8,128)S(1)}, u32[]{:S(2)}, u32[]{:S(2)}) collective-permute-start(f32[4,136,128]{2,1,0:T(8,128)S(1)} %multiply_add_fusion.3), channel_id=1, source_target_pairs={{0,16},{8,24},{16,32},{24,40},{32,48},{40,56},{48,64},{56,72},{64,... | collective-permute-start | bytes 835592 | tf_op jit(solution)/shard_map/ppermute | solution.py:25
  36.7 10.8 %collective-permute-start.3 = (f32[4,136,128]{2,1,0:T(8,128)S(1)}, f32[4,136,128]{2,1,0:T(8,128)S(1)}, u32[]{:S(2)}, u32[]{:S(2)}) collective-permute-start(f32[4,136,128]{2,1,0:T(8,128)S(1)} %multiply_add_fusion.2), channel_id=1, source_target_pairs={{0,32},{8,40},{16,48},{24,56},{32,64},{40,72},{48,80},{56,88},{64,... | collective-permute-start | bytes 835592 | tf_op jit(solution)/shard_map/ppermute | solution.py:25
  47.7 15.4 %collective-permute-start.4 = (f32[4,136,128]{2,1,0:T(8,128)S(1)}, f32[4,136,128]{2,1,0:T(8,128)S(1)}, u32[]{:S(2)}, u32[]{:S(2)}) collective-permute-start(f32[4,136,128]{2,1,0:T(8,128)S(1)} %multiply_add_fusion.1), channel_id=1, source_target_pairs={{0,64},{8,72},{16,80},{24,88},{32,96},{40,104},{48,112},{56,120},{... | collective-permute-start | bytes 835592 | tf_op jit(solution)/shard_map/ppermute | solution.py:25
  63.2 10.2 %collective-permute-start.5 = (f32[4,136,128]{2,1,0:T(8,128)S(1)}, f32[4,136,128]{2,1,0:T(8,128)S(1)}, u32[]{:S(2)}, u32[]{:S(2)}) collective-permute-start(f32[4,136,128]{2,1,0:T(8,128)S(1)} %multiply_add_fusion), channel_id=1, source_target_pairs={{0,128},{8,136},{16,144},{24,152},{32,160},{40,168},{48,176},{56,1... | collective-permute-start | bytes 835592 | tf_op jit(solution)/shard_map/ppermute | solution.py:25
  75.2 2.3 copy-start.3
  79.6 40.2 %copy-start.9 = (s32[128,2]{0,1:T(2,128)S(1)}, s32[128,2]{0,1:T(2,128)}, u32[]{:S(2)}) copy-start(s32[128,2]{0,1:T(2,128)} %param.25) | copy-start | bytes 3076
  79.6 32.7 %all-to-all-start = ((bf16[8,128,384]{2,1,0:T(8,128)(2,1)}), bf16[8,128,384]{2,1,0:T(8,128)(2,1)}, u32[]{:S(2)}, u32[]{:S(2)}) async-start(bf16[8,128,384]{2,1,0:T(8,128)(2,1)} %fusion.14), calls=%async_computation | async-start | bytes 1572864 | tf_op jit(solution)/shard_map/all_to_all | solution.py:119
  115.5 24.9 %all-to-all-start.1 = ((bf16[8,128,384]{2,1,0:T(8,128)(2,1)}), bf16[8,128,384]{2,1,0:T(8,128)(2,1)}, u32[]{:S(2)}, u32[]{:S(2)}) async-start(bf16[8,128,384]{2,1,0:T(8,128)(2,1)} %broadcast_in_dim.111), calls=%async_computation.1 | async-start | bytes 1572864 | tf_op jit(solution)/shard_map/all_to_all | solution.py:129
  119.7 129.3 %reduce-scatter.4.cloned.1.call-start = ((), (), s32[]{:S(2)}) async-start(), calls=%async_computation.6 | async-start | bytes 3538944
  128.5 0.6 copy-start.10
  129.8 14.1 %copy-start.8 = (f32[3072]{0:T(1024)S(1)}, f32[3072]{0:T(1024)}, u32[]{:S(2)}) copy-start(f32[3072]{0:T(1024)} %param.20) | copy-start | bytes 36868
  140.4 3.4 %copy-start.6 = (pred[512,128]{1,0:T(8,128)(4,1)S(1)}, pred[512,128]{1,0:T(8,128)(4,1)}, u32[]{:S(2)}) copy-start(pred[512,128]{1,0:T(8,128)(4,1)} %fusion.27) | copy-start | bytes 196612
  141.9 51.4 %copy-start.1 = (f32[8,16,8,384]{3,2,0,1:T(8,128)}, f32[8,16,8,384]{3,2,0,1:T(8,128)S(1)}, u32[]{:S(2)}) copy-start(f32[8,16,8,384]{3,2,0,1:T(8,128)S(1)} %copy.110) | copy-start | bytes 4718596
  143.8 1.1 copy-start.12
  144.9 50.1 %copy-start.13 = (bf16[1,3072,576]{1,2,0:T(8,128)(2,1)S(1)}, bf16[1,3072,576]{1,2,0:T(8,128)(2,1)}, u32[]{:S(2)}) copy-start(bf16[1,3072,576]{1,2,0:T(8,128)(2,1)} %param.22) | copy-start | bytes 10616836
  193.3 1.7 copy-start.2
  250.9 20.9 %all-to-all-start.3 = ((bf16[32,16,384]{2,1,0:T(8,128)(2,1)}), bf16[32,16,384]{2,1,0:T(8,128)(2,1)}, u32[]{:S(2)}, u32[]{:S(2)}) async-start(bf16[32,16,384]{2,1,0:T(8,128)(2,1)} %bitcast.145), calls=%async_computation.3 | async-start | bytes 786432 | tf_op jit(solution)/shard_map/all_to_all | solution.py:166
Sparse Core Ops, SparseCore 0:
  9.8 60.5 all-gather.2
  212.5 36.4 reduce-scatter.3

commit v6 on v5

--- a/solution.py
+++ b/solution.py
@@ -12,24 +12,39 @@
 def prior_states(final_log, local_state, axis):
     peers = lax.axis_size(axis)
     heads_here, head_size = local_state.shape[0], local_state.shape[2]
-    totals = jnp.broadcast_to(final_log[:, None, None], (heads_here, 8, head_size))
-    packed = jnp.concatenate([local_state, totals], axis=1)
-    row = lax.broadcasted_iota(jnp.int32, packed.shape, 1)
+
+    def pack(value):
+        state, total = value
+        high = total.astype(jnp.bfloat16)
+        rest = total - high.astype(jnp.float32)
+        middle = rest.astype(jnp.bfloat16)
+        low = (rest - middle.astype(jnp.float32)).astype(jnp.bfloat16)
+        extra = jnp.zeros((heads_here, 16, head_size), jnp.bfloat16)
+        extra = extra.at[:, 0:3, 0].set(jnp.stack([high, middle, low], axis=1))
+        return jnp.concatenate([state.astype(jnp.bfloat16), extra], axis=1)
+
+    def unpack(packed):
+        state = packed[:, :head_size].astype(jnp.float32)
+        total = jnp.sum(packed[:, head_size : head_size + 3, 0].astype(jnp.float32), axis=1)
+        return (state, total)
 
     def combine(earlier, later):
-        scale = jnp.exp(later[:, head_size : head_size + 1, 0:1])
-        return later + jnp.where(row < head_size, scale, 1.0) * earlier
+        return (
+            jnp.exp(later[1])[:, None, None] * earlier[0] + later[0],
+            earlier[1] + later[1],
+        )
 
     def shifted(value, distance):
         pairs = [(k, k + distance) for k in range(peers - distance)]
-        return lax.ppermute(value, axis, pairs)
-
-    before = combine(shifted(packed, 2), shifted(packed, 1))
+        return unpack(lax.ppermute(pack(value), axis, pairs))
+
+    own = (local_state, final_log)
+    before = combine(shifted(own, 2), shifted(own, 1))
     distance = 2
     while distance < peers:
         before = combine(shifted(before, distance), before)
         distance *= 2
-    return before[:, :head_size]
+    return before[0]
 
 
 def local_attention(query_block, key_block, value_block, decay_block):

time: 283 us -> 279 us (0.986)
  waiting for transfers between devices: 103 us -> 74.8 us
  other arithmetic: 11.9 us -> 28.4 us
  local copies, waits for them, and re-layouts: 21.8 us -> 28 us
  starting transfers between devices: 58.8 us -> 54.1 us
    ppermute x6, waiting for transfers between devices: 28 us -> 7.29 us  [shifted(): return unpack(lax.ppermute(pack(value), axis, pairs))]
    convert_element_type x0 -> x12, other arithmetic: none -> 6.9 us  [the longest x4 4.9 us: pack(): return jnp.concatenate([state.astype(jnp.bfloat16), extra], axis=1)]
    another operation x1 -> x7, local copies, waits for them, and re-layouts: 0.01 us -> 4.23 us
    unnamed x31 -> x46, local copies, waits for them, and re-layouts: 9.63 us -> 13.7 us
    all_to_all x1, waiting for transfers between devices: 21.1 us -> 17.7 us  [body(): lax.all_to_all(partial_out.astype(jnp.bfloat16).transpose(1, 0, 2), 'head...]
    all_to_all x1, waiting for transfers between devices: 10.7 us -> 7.26 us  [body(): lax.all_to_all(jnp.broadcast_to(mixed_slice[None], (head_count,) + mixed_...]
  transfers between devices with their start and end apart: 11 -> 11, of which waited for: 10 -> 10; matrix products, arithmetic and copies ran while one was open for 8% -> 13% of each run, Pallas kernels for 0% -> 0%
where the time goes in v6:
time: 279 us; the launch traced here: 278 us
  waiting for transfers between devices  74.8 us (27%)
  starting transfers between devices  54.1 us (19%)
  blocking collectives  51.2 us (18%)
  other arithmetic  28.4 us (10%)
  local copies, waits for them, and re-layouts  28 us (10%)
  matrix products  27.3 us (10%)
  between operations  13.7 us (5%)
    all_to_all x1, blocking collectives, body(): lax.all_to_all(packed.reshape(experts_total, capacity, width_here), 'ctx'...  51.2 us
    unnamed x3, waiting for transfers between devices  35.3 us
    ppermute x6, starting transfers between devices, shifted(): return unpack(lax.ppermute(pack(value), axis, pairs))  29.5 us
    all_to_all x1, waiting for transfers between devices, body(): lax.all_to_all(partial_out.astype(jnp.bfloat16).transpose(1, 0, 2), 'head...  17.7 us
    unnamed x46, local copies, waits for them, and re-layouts  13.7 us
    all_to_all x1, starting transfers between devices, body(): lax.all_to_all(summed.reshape(experts_total, capacity, slice_width), 'ctx...  10.8 us
    dot_general x1, matrix products, body(): jnp.dot(hidden, w_down[0], preferred_element_type=jnp.float32)  9.52 us
    all_to_all x1, starting transfers between devices, body(): lax.all_to_all(partial_out.astype(jnp.bfloat16).transpose(1, 0, 2), 'head...  9.52 us
  transfers between devices with their start and end apart: 11, of which 10 were waited for; matrix products, arithmetic and copies ran while one was open for 13% of the time, Pallas kernels for 0%

profile of v6, /device:TPU:1, one launch (start us, length us, event | category | flops | bytes accessed | tf_op | source)
XLA Modules:
  0.0 277.6 jit_solution(9748958444263697980)
XLA Ops:
  6.5 1.1 reduce_window_sum.26
  8.4 1.3 exponential_bitcast_fusion
  9.6 1.7 copy.157
  11.3 1.2 convolution_convert_fusion.3
  13.2 4.6 %collective-permute-start.1 = (bf16[4,144,128]{2,1,0:T(8,128)(2,1)}, bf16[4,144,128]{2,1,0:T(8,128)(2,1)}, u32[]{:S(2)}, u32[]{:S(2)}) collective-permute-start(bf16[4,144,128]{2,1,0:T(8,128)(2,1)} %fusion.47), channel_id=1, source_target_pairs={{0,16},{8,24},{16,32},{24,40},{32,48},{40,56},{48,64},{56,72},{64,... | collective-permute-start | bytes 442376 | tf_op jit(solution)/shard_map/ppermute | solution.py:39
  17.7 3.3 %collective-permute-start = (bf16[4,144,128]{2,1,0:T(8,128)(2,1)}, bf16[4,144,128]{2,1,0:T(8,128)(2,1)}, u32[]{:S(2)}, u32[]{:S(2)}) collective-permute-start(bf16[4,144,128]{2,1,0:T(8,128)(2,1)} %fusion.47), channel_id=1, source_target_pairs={{0,8},{8,16},{16,24},{24,32},{32,40},{40,48},{48,56},{56,64},{64,7... | collective-permute-start | bytes 442376 | tf_op jit(solution)/shard_map/ppermute | solution.py:39
  21.9 1.5 collective-permute-done
  26.7 1.1 fusion.45
  27.8 2.8 %collective-permute-start.2 = (bf16[4,144,128]{2,1,0:T(8,128)(2,1)S(1)}, bf16[4,144,128]{2,1,0:T(8,128)(2,1)S(1)}, u32[]{:S(2)}, u32[]{:S(2)}) collective-permute-start(bf16[4,144,128]{2,1,0:T(8,128)(2,1)S(1)} %fusion.48), channel_id=1, source_target_pairs={{0,16},{8,24},{16,32},{24,40},{32,48},{40,56},{48,64},{56,72},{64,... | collective-permute-start | bytes 442376 | tf_op jit(solution)/shard_map/ppermute | solution.py:39
  30.7 2.1 collective-permute-done.2
  36.1 1.2 fusion.74
  37.3 5.3 %collective-permute-start.3 = (bf16[4,144,128]{2,1,0:T(8,128)(2,1)S(1)}, bf16[4,144,128]{2,1,0:T(8,128)(2,1)S(1)}, u32[]{:S(2)}, u32[]{:S(2)}) collective-permute-start(bf16[4,144,128]{2,1,0:T(8,128)(2,1)S(1)} %fusion.49), channel_id=1, source_target_pairs={{0,32},{8,40},{16,48},{24,56},{32,64},{40,72},{48,80},{56,88},{64,... | collective-permute-start | bytes 442376 | tf_op jit(solution)/shard_map/ppermute | solution.py:39
  42.6 1.2 add_exponential_fusion.2
  48.1 1.3 fusion.46
  49.4 7.5 %collective-permute-start.4 = (bf16[4,144,128]{2,1,0:T(8,128)(2,1)S(1)}, bf16[4,144,128]{2,1,0:T(8,128)(2,1)S(1)}, u32[]{:S(2)}, u32[]{:S(2)}) collective-permute-start(bf16[4,144,128]{2,1,0:T(8,128)(2,1)S(1)} %fusion.50), channel_id=1, source_target_pairs={{0,64},{8,72},{16,80},{24,88},{32,96},{40,104},{48,112},{56,120},{... | collective-permute-start | bytes 442376 | tf_op jit(solution)/shard_map/ppermute | solution.py:39
  57.6 1.9 collective-permute-done.4
  62.9 1.4 fusion.73
  64.3 5.9 %collective-permute-start.5 = (bf16[4,144,128]{2,1,0:T(8,128)(2,1)S(1)}, bf16[4,144,128]{2,1,0:T(8,128)(2,1)S(1)}, u32[]{:S(2)}, u32[]{:S(2)}) collective-permute-start(bf16[4,144,128]{2,1,0:T(8,128)(2,1)S(1)} %fusion.51), channel_id=1, source_target_pairs={{0,128},{8,136},{16,144},{24,152},{32,160},{40,168},{48,176},{56,1... | collective-permute-start | bytes 442376 | tf_op jit(solution)/shard_map/ppermute | solution.py:39
  70.2 1.1 convolution_multiply_fusion
  72.3 1.7 fusion.39
  74.1 1.1 fusion.34
  75.2 1.5 fusion.38
  76.9 2.3 copy.199
  79.3 2.1 fusion.14
  81.4 9.5 %all-to-all-start = ((bf16[8,128,384]{2,1,0:T(8,128)(2,1)}), bf16[8,128,384]{2,1,0:T(8,128)(2,1)}, u32[]{:S(2)}, u32[]{:S(2)}) async-start(bf16[8,128,384]{2,1,0:T(8,128)(2,1)} %fusion.14), calls=%async_computation | async-start | bytes 1572864 | tf_op jit(solution)/shard_map/all_to_all | solution.py:134
  90.9 17.7 %all-to-all-done = bf16[8,128,384]{2,1,0:T(8,128)(2,1)} async-done(((bf16[8,128,384]{2,1,0:T(8,128)(2,1)}), bf16[8,128,384]{2,1,0:T(8,128)(2,1)}, u32[]{:S(2)}, u32[]{:S(2)}) %all-to-all-start) | async-done | bytes 786464 | tf_op jit(solution)/shard_map/all_to_all | solution.py:134
  108.6 1.3 convert_reduce_fusion
  111.7 4.2 %all-to-all-start.1 = ((bf16[8,128,384]{2,1,0:T(8,128)(2,1)}), bf16[8,128,384]{2,1,0:T(8,128)(2,1)}, u32[]{:S(2)}, u32[]{:S(2)}) async-start(bf16[8,128,384]{2,1,0:T(8,128)(2,1)} %broadcast_in_dim.30), calls=%async_computation.1 | async-start | bytes 1572864 | tf_op jit(solution)/shard_map/all_to_all | solution.py:144
  116.8 1.0 eq.67
  117.7 1.0 eq.63
  119.3 1.9 reduce-window.6
  126.0 7.3 %all-to-all-done.1 = bf16[8,128,384]{2,1,0:T(8,128)(2,1)} async-done(((bf16[8,128,384]{2,1,0:T(8,128)(2,1)}), bf16[8,128,384]{2,1,0:T(8,128)(2,1)}, u32[]{:S(2)}, u32[]{:S(2)}) %all-to-all-start.1) | async-done | bytes 786464 | tf_op jit(solution)/shard_map/all_to_all | solution.py:144
  133.3 1.3 convert_bitcast_fusion
  134.7 1.9 fusion.5
  136.7 1.0 convolution_convert_fusion.1
  137.8 51.2 %all_to_all.20 = bf16[32,16,3072]{2,1,0:T(8,128)(2,1)S(1)} all-to-all(bf16[32,16,3072]{2,1,0:T(8,128)(2,1)S(1)} %bitcast.179), channel_id=1, replica_groups=mesh['ctx'=32,'head'=8] {'ctx'}, dimensions={0} | all-to-all | bytes 6291456 | tf_op jit(solution)/shard_map/all_to_all | solution.py:166
  189.0 1.6 copy-done.2
  190.6 3.1 %fusion.3 = f32[512,576]{0,1:T(8,128)} fusion(bf16[512,3072]{1,0:T(8,128)(2,1)S(1)} %bitcast.182, bf16[1,3072,576]{1,2,0:T(8,128)(2,1)S(1)} %copy-done.20), kind=kOutput, calls=%fused_computation.5 | convolution fusion | flops 1811939328 | bytes 7864320 | tf_op jit(solution)/shard_map/dot_general | solution.py:174
  193.8 9.5 %convolution_convert_fusion = bf16[512,3072]{1,0:T(8,128)(2,1)} fusion(bf16[1,576,3072]{2,1,0:T(8,128)(2,1)S(1)} %copy-done, bf16[512,3072]{1,0:T(8,128)(2,1)} %bitcast.183, bf16[1,3072,576]{1,2,0:T(8,128)(2,1)} %param.35, f32[512,576]{0,1:T(8,128)} %fusion.3), kind=kOutput, calls=%fused_computation | convolution fusion | flops 3627220992 | bytes 14548992 | tf_op jit(solution)/shard_map/dot_general | solution.py:177
  203.3 4.7 %copy.171 = bf16[512,3072]{0,1:T(8,128)(2,1)} copy(bf16[512,3072]{1,0:T(8,128)(2,1)} %convolution_convert_fusion) | data formatting | bytes 6291456
  208.0 1.3 slice_bitcast_fusion
  209.3 35.2 %reduce-scatter.4.cloned.1.call-done = bf16[384,512]{1,0:T(8,128)(2,1)} async-done(((bf16[3072,512]{1,0:T(8,128)(2,1)}), bf16[384,512]{1,0:T(8,128)(2,1)}) %reduce-scatter.4.cloned.1.call-update) | async-done | bytes 393232
  244.5 1.9 copy.172
  246.4 10.8 %all-to-all-start.3 = ((bf16[32,16,384]{2,1,0:T(8,128)(2,1)}), bf16[32,16,384]{2,1,0:T(8,128)(2,1)}, u32[]{:S(2)}, u32[]{:S(2)}) async-start(bf16[32,16,384]{2,1,0:T(8,128)(2,1)} %bitcast.184), calls=%async_computation.3 | async-start | bytes 786432 | tf_op jit(solution)/shard_map/all_to_all | solution.py:181
  257.3 3.1 %fusion.18 = f32[128,32]{0,1:T(8,128)S(1)} fusion(f32[3072,32]{0,1:T(8,128)} %param.33, f32[128,3072]{1,0:T(8,128)} %bitcast.176, f32[3072]{0:T(1024)S(1)} %copy-done.9, f32[128]{0:T(128)} %copy-done.17), kind=kOutput, calls=%fused_computation.26 | convolution fusion | flops 151392256 | bytes 1995264 | tf_op jit(solution)/shard_map/dot_general | solution.py:156
  260.4 7.1 %all-to-all-done.3 = bf16[32,16,384]{2,1,0:T(8,128)(2,1)} async-done(((bf16[32,16,384]{2,1,0:T(8,128)(2,1)}), bf16[32,16,384]{2,1,0:T(8,128)(2,1)}, u32[]{:S(2)}, u32[]{:S(2)}) %all-to-all-start.3) | async-done | bytes 393248 | tf_op jit(solution)/shard_map/all_to_all | solution.py:181
  267.5 1.3 fusion.16
  268.8 1.9 fusion.17
  (99 shorter events, 26.7 us)
Async XLA Ops:
  6.5 187.3 %copy-start = (bf16[1,576,3072]{2,1,0:T(8,128)(2,1)S(1)}, bf16[1,576,3072]{2,1,0:T(8,128)(2,1)}, u32[]{:S(2)}) copy-start(bf16[1,576,3072]{2,1,0:T(8,128)(2,1)} %param.36) | copy-start | bytes 10616836
  6.5 70.4 %all-gather.3.cloned.1.call-start = ((), (), s32[]{:S(2)}) async-start(), calls=%async_computation.5 | async-start | bytes 3244032 | tf_op jit(solution)/shard_map/all_gather | solution.py:125
  7.8 0.5 copy-start.13
  13.2 7.9 %collective-permute-start.1 = (bf16[4,144,128]{2,1,0:T(8,128)(2,1)}, bf16[4,144,128]{2,1,0:T(8,128)(2,1)}, u32[]{:S(2)}, u32[]{:S(2)}) collective-permute-start(bf16[4,144,128]{2,1,0:T(8,128)(2,1)} %fusion.47), channel_id=1, source_target_pairs={{0,16},{8,24},{16,32},{24,40},{32,48},{40,56},{48,64},{56,72},{64,... | collective-permute-start | bytes 442376 | tf_op jit(solution)/shard_map/ppermute | solution.py:39
  17.7 5.7 %collective-permute-start = (bf16[4,144,128]{2,1,0:T(8,128)(2,1)}, bf16[4,144,128]{2,1,0:T(8,128)(2,1)}, u32[]{:S(2)}, u32[]{:S(2)}) collective-permute-start(bf16[4,144,128]{2,1,0:T(8,128)(2,1)} %fusion.47), channel_id=1, source_target_pairs={{0,8},{8,16},{16,24},{24,32},{32,40},{40,48},{48,56},{56,64},{64,7... | collective-permute-start | bytes 442376 | tf_op jit(solution)/shard_map/ppermute | solution.py:39
  24.8 0.5 copy-start.14
  27.8 4.9 %collective-permute-start.2 = (bf16[4,144,128]{2,1,0:T(8,128)(2,1)S(1)}, bf16[4,144,128]{2,1,0:T(8,128)(2,1)S(1)}, u32[]{:S(2)}, u32[]{:S(2)}) collective-permute-start(bf16[4,144,128]{2,1,0:T(8,128)(2,1)S(1)} %fusion.48), channel_id=1, source_target_pairs={{0,16},{8,24},{16,32},{24,40},{32,48},{40,56},{48,64},{56,72},{64,... | collective-permute-start | bytes 442376 | tf_op jit(solution)/shard_map/ppermute | solution.py:39
  32.8 0.6 copy-start.3
  33.5 0.6 copy-start.15
  34.2 0.6 copy-start.19
  37.3 7.4 %collective-permute-start.3 = (bf16[4,144,128]{2,1,0:T(8,128)(2,1)S(1)}, bf16[4,144,128]{2,1,0:T(8,128)(2,1)S(1)}, u32[]{:S(2)}, u32[]{:S(2)}) collective-permute-start(bf16[4,144,128]{2,1,0:T(8,128)(2,1)S(1)} %fusion.49), channel_id=1, source_target_pairs={{0,32},{8,40},{16,48},{24,56},{32,64},{40,72},{48,80},{56,88},{64,... | collective-permute-start | bytes 442376 | tf_op jit(solution)/shard_map/ppermute | solution.py:39
  44.7 0.7 copy-start.6
  45.5 0.7 copy-start.16
  46.2 0.6 copy-start.18
  49.4 10.0 %collective-permute-start.4 = (bf16[4,144,128]{2,1,0:T(8,128)(2,1)S(1)}, bf16[4,144,128]{2,1,0:T(8,128)(2,1)S(1)}, u32[]{:S(2)}, u32[]{:S(2)}) collective-permute-start(bf16[4,144,128]{2,1,0:T(8,128)(2,1)S(1)} %fusion.50), channel_id=1, source_target_pairs={{0,64},{8,72},{16,80},{24,88},{32,96},{40,104},{48,112},{56,120},{... | collective-permute-start | bytes 442376 | tf_op jit(solution)/shard_map/ppermute | solution.py:39
  59.4 0.7 copy-start.8
  60.2 0.7 copy-start.12
  62.2 11.9 %copy-start.4 = (bf16[128,512]{1,0:T(8,128)(2,1)S(1)}, bf16[128,512]{1,0:T(8,128)(2,1)}, u32[]{:S(2)}) copy-start(bf16[128,512]{1,0:T(8,128)(2,1)} %param.27) | copy-start | bytes 393220
  64.3 8.0 %collective-permute-start.5 = (bf16[4,144,128]{2,1,0:T(8,128)(2,1)S(1)}, bf16[4,144,128]{2,1,0:T(8,128)(2,1)S(1)}, u32[]{:S(2)}, u32[]{:S(2)}) collective-permute-start(bf16[4,144,128]{2,1,0:T(8,128)(2,1)S(1)} %fusion.51), channel_id=1, source_target_pairs={{0,128},{8,136},{16,144},{24,152},{32,160},{40,168},{48,176},{56,1... | collective-permute-start | bytes 442376 | tf_op jit(solution)/shard_map/ppermute | solution.py:39
  76.9 2.3 copy-start.5
  81.4 34.6 %copy-start.10 = (s32[128,2]{0,1:T(2,128)S(1)}, s32[128,2]{0,1:T(2,128)}, u32[]{:S(2)}) copy-start(s32[128,2]{0,1:T(2,128)} %param.37) | copy-start | bytes 3076
  81.4 27.2 %all-to-all-start = ((bf16[8,128,384]{2,1,0:T(8,128)(2,1)}), bf16[8,128,384]{2,1,0:T(8,128)(2,1)}, u32[]{:S(2)}, u32[]{:S(2)}) async-start(bf16[8,128,384]{2,1,0:T(8,128)(2,1)} %fusion.14), calls=%async_computation | async-start | bytes 1572864 | tf_op jit(solution)/shard_map/all_to_all | solution.py:134
  111.7 21.6 %all-to-all-start.1 = ((bf16[8,128,384]{2,1,0:T(8,128)(2,1)}), bf16[8,128,384]{2,1,0:T(8,128)(2,1)}, u32[]{:S(2)}, u32[]{:S(2)}) async-start(bf16[8,128,384]{2,1,0:T(8,128)(2,1)} %broadcast_in_dim.30), calls=%async_computation.1 | async-start | bytes 1572864 | tf_op jit(solution)/shard_map/all_to_all | solution.py:144
  116.0 128.6 %reduce-scatter.4.cloned.1.call-start = ((), (), s32[]{:S(2)}) async-start(), calls=%async_computation.6 | async-start | bytes 3538944
  124.7 0.6 copy-start.11
  126.0 10.7 %copy-start.9 = (f32[3072]{0:T(1024)S(1)}, f32[3072]{0:T(1024)}, u32[]{:S(2)}) copy-start(f32[3072]{0:T(1024)} %param.32) | copy-start | bytes 36868
  133.3 3.4 %copy-start.7 = (pred[512,128]{1,0:T(8,128)(4,1)S(1)}, pred[512,128]{1,0:T(8,128)(4,1)}, u32[]{:S(2)}) copy-start(pred[512,128]{1,0:T(8,128)(4,1)} %fusion.27) | copy-start | bytes 196612
  134.7 54.3 %copy-start.1 = (f32[8,16,8,384]{3,2,0,1:T(8,128)}, f32[8,16,8,384]{3,2,0,1:T(8,128)S(1)}, u32[]{:S(2)}) copy-start(f32[8,16,8,384]{3,2,0,1:T(8,128)S(1)} %copy.177) | copy-start | bytes 4718596
  136.7 1.1 copy-start.17
  137.8 52.9 %copy-start.20 = (bf16[1,3072,576]{1,2,0:T(8,128)(2,1)S(1)}, bf16[1,3072,576]{1,2,0:T(8,128)(2,1)}, u32[]{:S(2)}) copy-start(bf16[1,3072,576]{1,2,0:T(8,128)(2,1)} %param.34) | copy-start | bytes 10616836
  189.0 1.6 copy-start.2
  246.4 21.0 %all-to-all-start.3 = ((bf16[32,16,384]{2,1,0:T(8,128)(2,1)}), bf16[32,16,384]{2,1,0:T(8,128)(2,1)}, u32[]{:S(2)}, u32[]{:S(2)}) async-start(bf16[32,16,384]{2,1,0:T(8,128)(2,1)} %bitcast.184), calls=%async_computation.3 | async-start | bytes 786432 | tf_op jit(solution)/shard_map/all_to_all | solution.py:181
Sparse Core Ops, SparseCore 0:
  21.2 55.6 all-gather.2
  208.1 36.3 reduce-scatter.3

commit v7 on v6

--- a/solution.py
+++ b/solution.py
@@ -141,40 +141,51 @@
     projected = jnp.sum(pieces.astype(jnp.float32), axis=0)
     own_residual = lax.dynamic_slice_in_dim(residual, slice_start, slice_width, 1)
     mixed_slice = (own_residual.astype(jnp.float32) + projected).astype(jnp.bfloat16)
-    mixed_all = lax.all_to_all(
-        jnp.broadcast_to(mixed_slice[None], (head_count,) + mixed_slice.shape),
-        "head",
-        split_axis=0,
-        concat_axis=0,
-        tiled=True,
-    )
-    mixed_rows = mixed_all.transpose(1, 0, 2).reshape(token_count, model_width)
-    mixed_wide = mixed_rows.astype(jnp.float32)
-    inv_rms = lax.rsqrt(jnp.mean(mixed_wide * mixed_wide, axis=1, keepdims=True) + 1e-06)
-    scaled = mixed_wide * moe_gain[None, :]
-    moe_in = (scaled * inv_rms).astype(jnp.bfloat16)
-    logits = inv_rms * jnp.dot(scaled, router, precision=PRECISE)
-    base_slice = lax.dynamic_slice_in_dim(mixed_wide, slice_start, slice_width, 1)
+    mixed_part = mixed_slice.astype(jnp.float32)
+    gain_slice = lax.dynamic_slice_in_dim(moe_gain, slice_start, slice_width, 0)
+    router_slice = lax.dynamic_slice_in_dim(router, slice_start, slice_width, 0)
+    partial_logits = jnp.dot(mixed_part * gain_slice[None, :], router_slice, precision=PRECISE)
+    partial_squares = jnp.sum(mixed_part * mixed_part, axis=1, keepdims=True)
+    reduced = lax.psum(jnp.concatenate([partial_logits, partial_squares], axis=1), "head")
+    inv_rms = lax.rsqrt(reduced[:, experts_total:] / model_width + 1e-06)
+    logits = inv_rms * reduced[:, :experts_total]
+    base_slice = mixed_part
     gate_weights, slot_index = route_tokens(logits, expert_ids, experts_total)
     target = (expert_ids * capacity + slot_index).reshape(-1)
-    width_here = moe_in.shape[1]
     slots = lax.broadcasted_iota(jnp.int32, (experts_total * capacity, token_count, TOP), 0)
     chosen = jnp.any(slots == target.reshape(token_count, TOP)[None], axis=2)
     packed = jnp.dot(
-        chosen.astype(jnp.bfloat16), moe_in, preferred_element_type=jnp.float32
+        chosen.astype(jnp.bfloat16), mixed_slice, preferred_element_type=jnp.float32
     ).astype(jnp.bfloat16)
+    spread = jnp.broadcast_to(
+        packed.reshape(experts_total, 1, capacity, slice_width),
+        (experts_total, head_count, capacity, slice_width),
+    )
     arrived = lax.all_to_all(
-        packed.reshape(experts_total, capacity, width_here),
-        "ctx",
-        split_axis=0,
-        concat_axis=0,
-        tiled=True,
-    )
-    flat_rows = arrived.reshape(-1, model_width)
-    gate_part = jnp.dot(flat_rows, w_gate[0], preferred_element_type=jnp.float32)
-    up_part = jnp.dot(flat_rows, w_up[0], preferred_element_type=jnp.float32)
+        spread.reshape(-1, slice_width), ("ctx", "head"), split_axis=0, concat_axis=0, tiled=True
+    ).reshape(ctx_size, head_count, capacity, slice_width)
+    rows = arrived.astype(jnp.float32)
+    inv_rows = lax.rsqrt(jnp.sum(rows * rows, axis=(1, 3)) / model_width + 1e-06)
+    moe_rows = (
+        rows * moe_gain.reshape(1, head_count, 1, slice_width) * inv_rows[:, None, :, None]
+    ).astype(jnp.bfloat16)
+    hidden_width = w_gate.shape[2]
+    gate_part = jnp.einsum(
+        "chsj,hjf->csf",
+        moe_rows,
+        w_gate[0].reshape(head_count, slice_width, hidden_width),
+        preferred_element_type=jnp.float32,
+    )
+    up_part = jnp.einsum(
+        "chsj,hjf->csf",
+        moe_rows,
+        w_up[0].reshape(head_count, slice_width, hidden_width),
+        preferred_element_type=jnp.float32,
+    )
     hidden = (jax.nn.silu(gate_part) * up_part).astype(jnp.bfloat16)
-    partial_down = jnp.dot(hidden, w_down[0], preferred_element_type=jnp.float32)
+    partial_down = jnp.einsum(
+        "csf,fd->csd", hidden, w_down[0], preferred_element_type=jnp.float32
+    ).reshape(ctx_size * capacity, model_width)
     summed = lax.psum_scatter(
         partial_down.astype(jnp.bfloat16), "head", scatter_dimension=1, tiled=True
     )

time: 279 us -> 299 us (1.072)
  waiting for transfers between devices: 74.8 us -> 101 us
  blocking collectives: 51.2 us -> 25.6 us
  local copies, waits for them, and re-layouts: 28 us -> 38.7 us
  starting transfers between devices: 54.1 us -> 61.9 us
  other arithmetic: 28.4 us -> 34.3 us
  matrix products: 27.3 us -> 22.2 us
    all_to_all x1, waiting for transfers between devices: 7.26 us -> 66.4 us  [body(): lax.all_to_all(spread.reshape(-1, slice_width), ('ctx', 'head'), split_ax...]
    all_to_all x1 -> x0, blocking collectives: 51.2 us -> none  [body(): lax.all_to_all(packed.reshape(experts_total, capacity, width_here), 'ctx'...]
    unnamed x3, waiting for transfers between devices: 35.3 us -> 9.38 us
    psum x0 -> x1, blocking collectives: none -> 25.6 us  [body(): lax.psum(jnp.concatenate([partial_logits, partial_squares], axis=1), 'head')]
    all_to_all x1, waiting for transfers between devices: 17.7 us -> 7.81 us  [body(): lax.all_to_all(partial_out.astype(jnp.bfloat16).transpose(1, 0, 2), 'head...]
    all_to_all x1, starting transfers between devices: 4.21 us -> 13 us  [body(): lax.all_to_all(spread.reshape(-1, slice_width), ('ctx', 'head'), split_ax...]
    unnamed x46 -> x51, local copies, waits for them, and re-layouts: 13.7 us -> 21.2 us
    dot_general x4 -> x5, matrix products: 16.8 us -> 11.7 us  [the longest x1 4.1 us: body(): jnp.einsum('csf,fd->csd', hidden, w_down[0], preferred_element_type=jnp.f...]
  transfers between devices with their start and end apart: 11 -> 11, of which waited for: 10 -> 10; matrix products, arithmetic and copies ran while one was open for 13% -> 15% of each run, Pallas kernels for 0% -> 0%
where the time goes in v7:
time: 299 us; the launch traced here: 297 us
  waiting for transfers between devices  101 us (34%)
  starting transfers between devices  61.9 us (21%)
  local copies, waits for them, and re-layouts  38.7 us (13%)
  other arithmetic  34.3 us (11%)
  blocking collectives  25.6 us (9%)
  matrix products  22.2 us (7%)
  between operations  13.7 us (5%)
    all_to_all x1, waiting for transfers between devices, body(): lax.all_to_all(spread.reshape(-1, slice_width), ('ctx', 'head'), split_ax...  66.4 us
    ppermute x6, starting transfers between devices, shifted(): return unpack(lax.ppermute(pack(value), axis, pairs))  29.5 us
    psum x1, blocking collectives, body(): lax.psum(jnp.concatenate([partial_logits, partial_squares], axis=1), 'head')  25.6 us
    unnamed x51, local copies, waits for them, and re-layouts  21.2 us
    all_to_all x1, starting transfers between devices, body(): lax.all_to_all(spread.reshape(-1, slice_width), ('ctx', 'head'), split_ax...  13 us
    all_to_all x1, starting transfers between devices, body(): lax.all_to_all(summed.reshape(experts_total, capacity, slice_width), 'ctx...  9.72 us
    all_to_all x1, waiting for transfers between devices, body(): lax.all_to_all(summed.reshape(experts_total, capacity, slice_width), 'ctx...  9.44 us
    unnamed x3, waiting for transfers between devices  9.38 us
  transfers between devices with their start and end apart: 11, of which 10 were waited for; matrix products, arithmetic and copies ran while one was open for 15% of the time, Pallas kernels for 0%

profile of v7, /device:TPU:1, one launch (start us, length us, event | category | flops | bytes accessed | tf_op | source)
XLA Modules:
  0.0 296.9 jit_solution(16351781480813821262)
XLA Ops:
  6.5 1.1 reduce_window_sum.26
  8.4 1.3 exponential_bitcast_fusion
  9.6 1.7 copy.198
  11.3 1.2 convolution_convert_fusion.3
  13.2 4.6 %collective-permute-start.1 = (bf16[4,144,128]{2,1,0:T(8,128)(2,1)}, bf16[4,144,128]{2,1,0:T(8,128)(2,1)}, u32[]{:S(2)}, u32[]{:S(2)}) collective-permute-start(bf16[4,144,128]{2,1,0:T(8,128)(2,1)} %fusion.48), channel_id=1, source_target_pairs={{0,16},{8,24},{16,32},{24,40},{32,48},{40,56},{48,64},{56,72},{64,... | collective-permute-start | bytes 442376 | tf_op jit(solution)/shard_map/ppermute | solution.py:39
  17.8 3.3 %collective-permute-start = (bf16[4,144,128]{2,1,0:T(8,128)(2,1)}, bf16[4,144,128]{2,1,0:T(8,128)(2,1)}, u32[]{:S(2)}, u32[]{:S(2)}) collective-permute-start(bf16[4,144,128]{2,1,0:T(8,128)(2,1)} %fusion.48), channel_id=1, source_target_pairs={{0,8},{8,16},{16,24},{24,32},{32,40},{40,48},{48,56},{56,64},{64,7... | collective-permute-start | bytes 442376 | tf_op jit(solution)/shard_map/ppermute | solution.py:39
  21.9 1.5 collective-permute-done
  27.9 2.8 collective-permute-start.2
  30.7 2.1 collective-permute-done.2
  36.1 1.2 fusion.80
  37.3 5.3 %collective-permute-start.3 = (bf16[4,144,128]{2,1,0:T(8,128)(2,1)S(1)}, bf16[4,144,128]{2,1,0:T(8,128)(2,1)S(1)}, u32[]{:S(2)}, u32[]{:S(2)}) collective-permute-start(bf16[4,144,128]{2,1,0:T(8,128)(2,1)S(1)} %fusion.50), channel_id=1, source_target_pairs={{0,32},{8,40},{16,48},{24,56},{32,64},{40,72},{48,80},{56,88},{64,... | collective-permute-start | bytes 442376 | tf_op jit(solution)/shard_map/ppermute | solution.py:39
  42.7 1.2 add_exponential_fusion.2
  48.1 1.3 fusion.47
  49.4 7.5 %collective-permute-start.4 = (bf16[4,144,128]{2,1,0:T(8,128)(2,1)S(1)}, bf16[4,144,128]{2,1,0:T(8,128)(2,1)S(1)}, u32[]{:S(2)}, u32[]{:S(2)}) collective-permute-start(bf16[4,144,128]{2,1,0:T(8,128)(2,1)S(1)} %fusion.51), channel_id=1, source_target_pairs={{0,64},{8,72},{16,80},{24,88},{32,96},{40,104},{48,112},{56,120},{... | collective-permute-start | bytes 442376 | tf_op jit(solution)/shard_map/ppermute | solution.py:39
  57.6 1.9 collective-permute-done.4
  63.0 1.4 fusion.79
  64.4 6.0 %collective-permute-start.5 = (bf16[4,144,128]{2,1,0:T(8,128)(2,1)S(1)}, bf16[4,144,128]{2,1,0:T(8,128)(2,1)S(1)}, u32[]{:S(2)}, u32[]{:S(2)}) collective-permute-start(bf16[4,144,128]{2,1,0:T(8,128)(2,1)S(1)} %fusion.52), channel_id=1, source_target_pairs={{0,128},{8,136},{16,144},{24,152},{32,160},{40,168},{48,176},{56,1... | collective-permute-start | bytes 442376 | tf_op jit(solution)/shard_map/ppermute | solution.py:39
  70.4 1.1 convolution_multiply_fusion
  72.5 1.7 fusion.38
  74.3 1.1 fusion.33
  75.4 1.5 fusion.37
  77.0 2.3 copy.258
  79.4 2.1 fusion.22
  81.5 9.4 %all-to-all-start = ((bf16[8,128,384]{2,1,0:T(8,128)(2,1)}), bf16[8,128,384]{2,1,0:T(8,128)(2,1)}, u32[]{:S(2)}, u32[]{:S(2)}) async-start(bf16[8,128,384]{2,1,0:T(8,128)(2,1)} %fusion.22), calls=%async_computation | async-start | bytes 1572864 | tf_op jit(solution)/shard_map/all_to_all | solution.py:134
  94.2 1.9 reduce-window.6
  100.8 7.8 %all-to-all-done = bf16[8,128,384]{2,1,0:T(8,128)(2,1)} async-done(((bf16[8,128,384]{2,1,0:T(8,128)(2,1)}), bf16[8,128,384]{2,1,0:T(8,128)(2,1)}, u32[]{:S(2)}, u32[]{:S(2)}) %all-to-all-start) | async-done | bytes 786464 | tf_op jit(solution)/shard_map/all_to_all | solution.py:134
  108.6 1.3 convert_reduce_fusion
  109.9 1.5 fusion.46
  113.1 2.0 broadcast_in_dim.61
  115.1 13.0 %all-to-all-start.1 = ((bf16[256,16,384]{2,1,0:T(8,128)(2,1)}), bf16[256,16,384]{2,1,0:T(8,128)(2,1)}, u32[]{:S(2)}, u32[]{:S(2)}) async-start(bf16[256,16,384]{2,1,0:T(8,128)(2,1)} %bitcast.206), calls=%async_computation.1 | async-start | bytes 6291456 | tf_op jit(solution)/shard_map/all_to_all | solution.py:164
  129.1 4.8 %copy.220 = bf16[72,8,8,384]{3,2,1,0:T(8,128)(2,1)} copy(bf16[72,8,8,384]{3,1,2,0:T(8,128)(2,1)} %bitcast.208) | data formatting | bytes 7077888
  133.9 2.6 copy.221
  137.3 66.4 %all-to-all-done.1 = bf16[256,16,384]{2,1,0:T(8,128)(2,1)} async-done(((bf16[256,16,384]{2,1,0:T(8,128)(2,1)}), bf16[256,16,384]{2,1,0:T(8,128)(2,1)}, u32[]{:S(2)}, u32[]{:S(2)}) %all-to-all-start.1) | async-done | bytes 3145760 | tf_op jit(solution)/shard_map/all_to_all | solution.py:164
  203.7 2.6 fusion.2
  207.0 1.3 add_rsqrt_fusion
  209.1 2.6 fusion.1
  212.1 2.6 fusion.10
  214.8 2.7 fusion.19
  217.5 4.1 %convolution_convert_fusion = bf16[512,3072]{1,0:T(8,128)(2,1)} fusion(bf16[512,576]{1,0:T(8,128)(2,1)S(1)} %bitcast.225, bf16[1,576,3072]{2,1,0:T(8,128)(2,1)S(1)} %copy-done), kind=kOutput, calls=%fused_computation.5 | convolution fusion | flops 1813512192 | bytes 7274496 | tf_op jit(solution)/shard_map/csf,fd->csd/dot_general | solution.py:186
  221.6 4.7 %copy.212 = bf16[512,3072]{0,1:T(8,128)(2,1)} copy(bf16[512,3072]{1,0:T(8,128)(2,1)} %convolution_convert_fusion) | data formatting | bytes 6291456
  227.5 1.2 fusion.45
  229.3 25.6 %psum.7 = f32[128,33]{0,1:T(8,128)} all-reduce(f32[128,33]{0,1:T(8,128)} %pad_maximum_fusion), channel_id=1, replica_groups=mesh['ctx'=32,'head'=8] {'head'}, use_global_device_ids=true, to_apply=%region_9.10 | all-reduce | flops 4224 | bytes 33792 | tf_op jit(solution)/shard_map/psum | solution.py:149
  255.7 9.3 %reduce-scatter.4.cloned.1.call-done = bf16[384,512]{1,0:T(8,128)(2,1)} async-done(((bf16[3072,512]{1,0:T(8,128)(2,1)}), bf16[384,512]{1,0:T(8,128)(2,1)}) %reduce-scatter.4.cloned.1.call-update) | async-done | bytes 393232
  265.0 1.9 copy.213
  266.9 9.7 %all-to-all-start.2 = ((bf16[32,16,384]{2,1,0:T(8,128)(2,1)}), bf16[32,16,384]{2,1,0:T(8,128)(2,1)}, u32[]{:S(2)}, u32[]{:S(2)}) async-start(bf16[32,16,384]{2,1,0:T(8,128)(2,1)} %bitcast.215), calls=%async_computation.2 | async-start | bytes 786432 | tf_op jit(solution)/shard_map/all_to_all | solution.py:192
  277.4 9.4 %all-to-all-done.2 = bf16[32,16,384]{2,1,0:T(8,128)(2,1)} async-done(((bf16[32,16,384]{2,1,0:T(8,128)(2,1)}), bf16[32,16,384]{2,1,0:T(8,128)(2,1)}, u32[]{:S(2)}, u32[]{:S(2)}) %all-to-all-start.2) | async-done | bytes 393248 | tf_op jit(solution)/shard_map/all_to_all | solution.py:192
  286.9 1.3 fusion.24
  288.2 1.9 fusion.25
  (113 shorter events, 36.3 us)
Async XLA Ops:
  6.5 210.9 %copy-start = (bf16[1,576,3072]{2,1,0:T(8,128)(2,1)S(1)}, bf16[1,576,3072]{2,1,0:T(8,128)(2,1)}, u32[]{:S(2)}) copy-start(bf16[1,576,3072]{2,1,0:T(8,128)(2,1)} %param.36) | copy-start | bytes 10616836
  6.5 70.5 %all-gather.3.cloned.1.call-start = ((), (), s32[]{:S(2)}) async-start(), calls=%async_computation.4 | async-start | bytes 3244032 | tf_op jit(solution)/shard_map/all_gather | solution.py:125
  7.8 0.5 copy-start.15
  13.2 7.9 %collective-permute-start.1 = (bf16[4,144,128]{2,1,0:T(8,128)(2,1)}, bf16[4,144,128]{2,1,0:T(8,128)(2,1)}, u32[]{:S(2)}, u32[]{:S(2)}) collective-permute-start(bf16[4,144,128]{2,1,0:T(8,128)(2,1)} %fusion.48), channel_id=1, source_target_pairs={{0,16},{8,24},{16,32},{24,40},{32,48},{40,56},{48,64},{56,72},{64,... | collective-permute-start | bytes 442376 | tf_op jit(solution)/shard_map/ppermute | solution.py:39
  17.8 5.7 %collective-permute-start = (bf16[4,144,128]{2,1,0:T(8,128)(2,1)}, bf16[4,144,128]{2,1,0:T(8,128)(2,1)}, u32[]{:S(2)}, u32[]{:S(2)}) collective-permute-start(bf16[4,144,128]{2,1,0:T(8,128)(2,1)} %fusion.48), channel_id=1, source_target_pairs={{0,8},{8,16},{16,24},{24,32},{32,40},{40,48},{48,56},{56,64},{64,7... | collective-permute-start | bytes 442376 | tf_op jit(solution)/shard_map/ppermute | solution.py:39
  24.9 0.5 copy-start.16
  27.9 4.9 %collective-permute-start.2 = (bf16[4,144,128]{2,1,0:T(8,128)(2,1)S(1)}, bf16[4,144,128]{2,1,0:T(8,128)(2,1)S(1)}, u32[]{:S(2)}, u32[]{:S(2)}) collective-permute-start(bf16[4,144,128]{2,1,0:T(8,128)(2,1)S(1)} %fusion.49), channel_id=1, source_target_pairs={{0,16},{8,24},{16,32},{24,40},{32,48},{40,56},{48,64},{56,72},{64,... | collective-permute-start | bytes 442376 | tf_op jit(solution)/shard_map/ppermute | solution.py:39
  32.8 0.7 copy-start.5
  33.6 0.6 copy-start.17
  34.2 0.6 copy-start.21
  37.3 7.4 %collective-permute-start.3 = (bf16[4,144,128]{2,1,0:T(8,128)(2,1)S(1)}, bf16[4,144,128]{2,1,0:T(8,128)(2,1)S(1)}, u32[]{:S(2)}, u32[]{:S(2)}) collective-permute-start(bf16[4,144,128]{2,1,0:T(8,128)(2,1)S(1)} %fusion.50), channel_id=1, source_target_pairs={{0,32},{8,40},{16,48},{24,56},{32,64},{40,72},{48,80},{56,88},{64,... | collective-permute-start | bytes 442376 | tf_op jit(solution)/shard_map/ppermute | solution.py:39
  44.8 0.6 copy-start.8
  45.5 0.7 copy-start.18
  46.2 0.6 copy-start.20
  49.4 10.1 %collective-permute-start.4 = (bf16[4,144,128]{2,1,0:T(8,128)(2,1)S(1)}, bf16[4,144,128]{2,1,0:T(8,128)(2,1)S(1)}, u32[]{:S(2)}, u32[]{:S(2)}) collective-permute-start(bf16[4,144,128]{2,1,0:T(8,128)(2,1)S(1)} %fusion.51), channel_id=1, source_target_pairs={{0,64},{8,72},{16,80},{24,88},{32,96},{40,104},{48,112},{56,120},{... | collective-permute-start | bytes 442376 | tf_op jit(solution)/shard_map/ppermute | solution.py:39
  59.5 0.7 copy-start.9
  60.3 0.7 copy-start.14
  62.3 11.9 %copy-start.6 = (bf16[128,512]{1,0:T(8,128)(2,1)S(1)}, bf16[128,512]{1,0:T(8,128)(2,1)}, u32[]{:S(2)}) copy-start(bf16[128,512]{1,0:T(8,128)(2,1)} %param.27) | copy-start | bytes 393220
  64.4 8.1 %collective-permute-start.5 = (bf16[4,144,128]{2,1,0:T(8,128)(2,1)S(1)}, bf16[4,144,128]{2,1,0:T(8,128)(2,1)S(1)}, u32[]{:S(2)}, u32[]{:S(2)}) collective-permute-start(bf16[4,144,128]{2,1,0:T(8,128)(2,1)S(1)} %fusion.52), channel_id=1, source_target_pairs={{0,128},{8,136},{16,144},{24,152},{32,160},{40,168},{48,176},{56,1... | collective-permute-start | bytes 442376 | tf_op jit(solution)/shard_map/ppermute | solution.py:39
  77.0 2.4 copy-start.7
  79.4 11.5 %copy-start.10 = (s32[128,2]{0,1:T(2,128)S(1)}, s32[128,2]{0,1:T(2,128)}, u32[]{:S(2)}) copy-start(s32[128,2]{0,1:T(2,128)} %param.37) | copy-start | bytes 3076
  81.5 27.1 %all-to-all-start = ((bf16[8,128,384]{2,1,0:T(8,128)(2,1)}), bf16[8,128,384]{2,1,0:T(8,128)(2,1)}, u32[]{:S(2)}, u32[]{:S(2)}) async-start(bf16[8,128,384]{2,1,0:T(8,128)(2,1)} %fusion.22), calls=%async_computation | async-start | bytes 1572864 | tf_op jit(solution)/shard_map/all_to_all | solution.py:134
  99.6 0.6 copy-start.12
  111.4 0.6 copy-start.4
  115.1 88.5 %all-to-all-start.1 = ((bf16[256,16,384]{2,1,0:T(8,128)(2,1)}), bf16[256,16,384]{2,1,0:T(8,128)(2,1)}, u32[]{:S(2)}, u32[]{:S(2)}) async-start(bf16[256,16,384]{2,1,0:T(8,128)(2,1)} %bitcast.206), calls=%async_computation.1 | async-start | bytes 6291456 | tf_op jit(solution)/shard_map/all_to_all | solution.py:164
  128.1 136.9 %reduce-scatter.4.cloned.1.call-start = ((), (), s32[]{:S(2)}) async-start(), calls=%async_computation.5 | async-start | bytes 3538944
  129.1 4.8 %copy-start.1 = (bf16[1,3072,576]{1,2,0:T(8,128)(2,1)S(1)}, bf16[1,3072,576]{1,2,0:T(8,128)(2,1)}, u32[]{:S(2)}) copy-start(bf16[1,3072,576]{1,2,0:T(8,128)(2,1)} %param.35) | copy-start | bytes 10616836
  209.0 3.1 %copy-start.3 = (bf16[72,8,8,384]{3,2,1,0:T(8,128)(2,1)S(1)}, bf16[72,8,8,384]{3,2,1,0:T(8,128)(2,1)}, u32[]{:S(2)}) copy-start(bf16[72,8,8,384]{3,2,1,0:T(8,128)(2,1)} %copy.220) | copy-start | bytes 10616836
  212.1 2.6 copy-start.2
  226.2 0.8 copy-start.13
  226.2 2.5 copy-start.19
  226.2 51.2 %copy-start.11 = (s32[128,2]{0,1:T(2,128)S(1)}, s32[128,2]{0,1:T(2,128)}, u32[]{:S(2)}) copy-start(s32[128,2]{0,1:T(2,128)} %param.37) | copy-start | bytes 3076
  266.9 19.9 %all-to-all-start.2 = ((bf16[32,16,384]{2,1,0:T(8,128)(2,1)}), bf16[32,16,384]{2,1,0:T(8,128)(2,1)}, u32[]{:S(2)}, u32[]{:S(2)}) async-start(bf16[32,16,384]{2,1,0:T(8,128)(2,1)} %bitcast.215), calls=%async_computation.2 | async-start | bytes 786432 | tf_op jit(solution)/shard_map/all_to_all | solution.py:192
Sparse Core Ops, SparseCore 0:
  21.2 55.7 all-gather.2
  226.4 38.6 reduce-scatter.3

commit v8 on v6

--- a/solution.py
+++ b/solution.py
@@ -163,21 +163,23 @@
     packed = jnp.dot(
         chosen.astype(jnp.bfloat16), moe_in, preferred_element_type=jnp.float32
     ).astype(jnp.bfloat16)
-    arrived = lax.all_to_all(
-        packed.reshape(experts_total, capacity, width_here),
-        "ctx",
-        split_axis=0,
-        concat_axis=0,
-        tiled=True,
-    )
-    flat_rows = arrived.reshape(-1, model_width)
-    gate_part = jnp.dot(flat_rows, w_gate[0], preferred_element_type=jnp.float32)
-    up_part = jnp.dot(flat_rows, w_up[0], preferred_element_type=jnp.float32)
-    hidden = (jax.nn.silu(gate_part) * up_part).astype(jnp.bfloat16)
-    partial_down = jnp.dot(hidden, w_down[0], preferred_element_type=jnp.float32)
-    summed = lax.psum_scatter(
-        partial_down.astype(jnp.bfloat16), "head", scatter_dimension=1, tiled=True
-    )
+    halves = packed.reshape(experts_total, 2, capacity // 2, width_here)
+    partial_halves = []
+    for half in range(2):
+        arrived = lax.all_to_all(
+            halves[:, half], "ctx", split_axis=0, concat_axis=0, tiled=True
+        )
+        flat_rows = arrived.reshape(-1, model_width)
+        gate_part = jnp.dot(flat_rows, w_gate[0], preferred_element_type=jnp.float32)
+        up_part = jnp.dot(flat_rows, w_up[0], preferred_element_type=jnp.float32)
+        hidden = (jax.nn.silu(gate_part) * up_part).astype(jnp.bfloat16)
+        partial_halves.append(
+            jnp.dot(hidden, w_down[0], preferred_element_type=jnp.float32)
+            .astype(jnp.bfloat16)
+            .reshape(arrived.shape)
+        )
+    partial_down = jnp.stack(partial_halves, axis=1).reshape(-1, model_width)
+    summed = lax.psum_scatter(partial_down, "head", scatter_dimension=1, tiled=True)
     returned = lax.all_to_all(
         summed.reshape(experts_total, capacity, slice_width),
         "ctx",

time: 279 us -> 300 us (1.075)
  waiting for transfers between devices: 74.8 us -> 95.1 us
  blocking collectives: 51.2 us -> 34.2 us
  matrix products: 27.3 us -> 38.8 us
  other arithmetic: 28.4 us -> 31.4 us
  starting transfers between devices: 54.1 us -> 57.1 us
    all_to_all x0 -> x1, waiting for transfers between devices: none -> 17.7 us  [body(): lax.all_to_all(halves[:, half], 'ctx', split_axis=0, concat_axis=0, tiled...]
    all_to_all x1, blocking collectives: 51.2 us -> 34.2 us  [body(): lax.all_to_all(halves[:, half], 'ctx', split_axis=0, concat_axis=0, tiled...]
    dot_general x1 -> x2, matrix products: 9.52 us -> 16.2 us  [body(): jnp.dot(hidden, w_down[0], preferred_element_type=jnp.float32)]
    dot_general x1 -> x2, matrix products: 3.15 us -> 8.87 us  [body(): jnp.dot(flat_rows, w_gate[0], preferred_element_type=jnp.float32)]
    all_to_all x0 -> x1, starting transfers between devices: none -> 4.68 us  [body(): lax.all_to_all(halves[:, half], 'ctx', split_axis=0, concat_axis=0, tiled...]
    another operation x7 -> x8, other arithmetic: 4.24 us -> 8.11 us
    unnamed x46 -> x56, local copies, waits for them, and re-layouts: 13.7 us -> 11.9 us
  transfers between devices with their start and end apart: 11 -> 12, of which waited for: 10 -> 11; matrix products, arithmetic and copies ran while one was open for 13% -> 13% of each run, Pallas kernels for 0% -> 0%
where the time goes in v8:
time: 300 us; the launch traced here: 298 us
  waiting for transfers between devices  95.1 us (32%)
  starting transfers between devices  57.1 us (19%)
  matrix products  38.8 us (13%)
  blocking collectives  34.2 us (11%)
  other arithmetic  31.4 us (10%)
  local copies, waits for them, and re-layouts  27.7 us (9%)
  between operations  13.8 us (5%)
    unnamed x3, waiting for transfers between devices  36.2 us
    all_to_all x1, blocking collectives, body(): lax.all_to_all(halves[:, half], 'ctx', split_axis=0, concat_axis=0, tiled...  34.2 us
    ppermute x6, starting transfers between devices, shifted(): return unpack(lax.ppermute(pack(value), axis, pairs))  28.9 us
    all_to_all x1, waiting for transfers between devices, body(): lax.all_to_all(halves[:, half], 'ctx', split_axis=0, concat_axis=0, tiled...  17.7 us
    all_to_all x1, waiting for transfers between devices, body(): lax.all_to_all(partial_out.astype(jnp.bfloat16).transpose(1, 0, 2), 'head...  17.7 us
    dot_general x2, matrix products, body(): jnp.dot(hidden, w_down[0], preferred_element_type=jnp.float32)  16.2 us
    unnamed x56, local copies, waits for them, and re-layouts  11.9 us
    all_to_all x1, starting transfers between devices, body(): lax.all_to_all(summed.reshape(experts_total, capacity, slice_width), 'ctx...  10.6 us
  transfers between devices with their start and end apart: 12, of which 11 were waited for; matrix products, arithmetic and copies ran while one was open for 13% of the time, Pallas kernels for 0%

profile of v8, /device:TPU:1, one launch (start us, length us, event | category | flops | bytes accessed | tf_op | source)
XLA Modules:
  0.0 298.1 jit_solution(1462773491374866444)
XLA Ops:
  8.4 1.3 exponential_bitcast_fusion
  9.6 1.6 copy.167
  11.3 1.2 convolution_convert_fusion.4
  13.1 4.6 %collective-permute-start.1 = (bf16[4,144,128]{2,1,0:T(8,128)(2,1)}, bf16[4,144,128]{2,1,0:T(8,128)(2,1)}, u32[]{:S(2)}, u32[]{:S(2)}) collective-permute-start(bf16[4,144,128]{2,1,0:T(8,128)(2,1)} %fusion.85), channel_id=1, source_target_pairs={{0,16},{8,24},{16,32},{24,40},{32,48},{40,56},{48,64},{56,72},{64,... | collective-permute-start | bytes 442376 | tf_op jit(solution)/shard_map/ppermute | solution.py:39
  17.7 3.3 %collective-permute-start = (bf16[4,144,128]{2,1,0:T(8,128)(2,1)}, bf16[4,144,128]{2,1,0:T(8,128)(2,1)}, u32[]{:S(2)}, u32[]{:S(2)}) collective-permute-start(bf16[4,144,128]{2,1,0:T(8,128)(2,1)} %fusion.85), channel_id=1, source_target_pairs={{0,8},{8,16},{16,24},{24,32},{32,40},{40,48},{48,56},{56,64},{64,7... | collective-permute-start | bytes 442376 | tf_op jit(solution)/shard_map/ppermute | solution.py:39
  21.9 1.5 collective-permute-done
  27.8 2.8 collective-permute-start.2
  30.6 2.1 collective-permute-done.2
  36.0 1.2 fusion.113
  37.2 5.3 %collective-permute-start.3 = (bf16[4,144,128]{2,1,0:T(8,128)(2,1)S(1)}, bf16[4,144,128]{2,1,0:T(8,128)(2,1)S(1)}, u32[]{:S(2)}, u32[]{:S(2)}) collective-permute-start(bf16[4,144,128]{2,1,0:T(8,128)(2,1)S(1)} %fusion.87), channel_id=1, source_target_pairs={{0,32},{8,40},{16,48},{24,56},{32,64},{40,72},{48,80},{56,88},{64,... | collective-permute-start | bytes 442376 | tf_op jit(solution)/shard_map/ppermute | solution.py:39
  42.5 1.2 add_exponential_fusion.2
  47.8 1.3 fusion.84
  49.1 7.6 %collective-permute-start.4 = (bf16[4,144,128]{2,1,0:T(8,128)(2,1)S(1)}, bf16[4,144,128]{2,1,0:T(8,128)(2,1)S(1)}, u32[]{:S(2)}, u32[]{:S(2)}) collective-permute-start(bf16[4,144,128]{2,1,0:T(8,128)(2,1)S(1)} %fusion.88), channel_id=1, source_target_pairs={{0,64},{8,72},{16,80},{24,88},{32,96},{40,104},{48,112},{56,120},{... | collective-permute-start | bytes 442376 | tf_op jit(solution)/shard_map/ppermute | solution.py:39
  57.4 1.7 collective-permute-done.4
  62.6 1.4 fusion.112
  64.0 5.3 %collective-permute-start.5 = (bf16[4,144,128]{2,1,0:T(8,128)(2,1)S(1)}, bf16[4,144,128]{2,1,0:T(8,128)(2,1)S(1)}, u32[]{:S(2)}, u32[]{:S(2)}) collective-permute-start(bf16[4,144,128]{2,1,0:T(8,128)(2,1)S(1)} %fusion.89), channel_id=1, source_target_pairs={{0,128},{8,136},{16,144},{24,152},{32,160},{40,168},{48,176},{56,1... | collective-permute-start | bytes 442376 | tf_op jit(solution)/shard_map/ppermute | solution.py:39
  69.3 1.2 convolution_multiply_fusion
  70.5 1.4 collective-permute-done.5
  72.0 1.5 fusion.77
  74.8 1.6 all-gather.3.cloned.1.call-done
  76.4 2.3 copy.209
  78.7 2.1 fusion.19
  80.8 8.5 %all-to-all-start = ((bf16[8,128,384]{2,1,0:T(8,128)(2,1)}), bf16[8,128,384]{2,1,0:T(8,128)(2,1)}, u32[]{:S(2)}, u32[]{:S(2)}) async-start(bf16[8,128,384]{2,1,0:T(8,128)(2,1)} %fusion.19), calls=%async_computation | async-start | bytes 1572864 | tf_op jit(solution)/shard_map/all_to_all | solution.py:134
  89.3 17.7 %all-to-all-done = bf16[8,128,384]{2,1,0:T(8,128)(2,1)} async-done(((bf16[8,128,384]{2,1,0:T(8,128)(2,1)}), bf16[8,128,384]{2,1,0:T(8,128)(2,1)}, u32[]{:S(2)}, u32[]{:S(2)}) %all-to-all-start) | async-done | bytes 786464 | tf_op jit(solution)/shard_map/all_to_all | solution.py:134
  106.9 1.3 convert_reduce_fusion
  110.1 4.2 %all-to-all-start.1 = ((bf16[8,128,384]{2,1,0:T(8,128)(2,1)}), bf16[8,128,384]{2,1,0:T(8,128)(2,1)}, u32[]{:S(2)}, u32[]{:S(2)}) async-start(bf16[8,128,384]{2,1,0:T(8,128)(2,1)} %broadcast_in_dim.30), calls=%async_computation.1 | async-start | bytes 1572864 | tf_op jit(solution)/shard_map/all_to_all | solution.py:144
  117.7 1.9 reduce-window.6
  124.4 7.3 %all-to-all-done.1 = bf16[8,128,384]{2,1,0:T(8,128)(2,1)} async-done(((bf16[8,128,384]{2,1,0:T(8,128)(2,1)}), bf16[8,128,384]{2,1,0:T(8,128)(2,1)}, u32[]{:S(2)}, u32[]{:S(2)}) %all-to-all-start.1) | async-done | bytes 786464 | tf_op jit(solution)/shard_map/all_to_all | solution.py:144
  131.7 1.2 convert_bitcast_fusion
  133.1 1.9 fusion.12
  136.2 1.4 slice_bitcast_fusion.1
  137.6 34.2 %all_to_all.25 = bf16[32,8,3072]{2,1,0:T(8,128)(2,1)} all-to-all(bf16[32,8,3072]{2,1,0:T(8,128)(2,1)S(1)} %get-tuple-element.81), channel_id=1, replica_groups=mesh['ctx'=32,'head'=8] {'ctx'}, dimensions={0} | all-to-all | bytes 3145728 | tf_op jit(solution)/shard_map/all_to_all | solution.py:169
  171.7 4.7 %all-to-all-start.3 = ((bf16[32,8,3072]{2,1,0:T(8,128)(2,1)}), bf16[32,8,3072]{2,1,0:T(8,128)(2,1)}, u32[]{:S(2)}, u32[]{:S(2)}) async-start(bf16[32,8,3072]{2,1,0:T(8,128)(2,1)} %get-tuple-element.82), calls=%async_computation.3 | async-start | bytes 3145728 | tf_op jit(solution)/shard_map/all_to_all | solution.py:169
  176.6 4.5 %fusion.10 = f32[256,576]{0,1:T(8,128)} fusion(bf16[1,3072,576]{1,2,0:T(8,128)(2,1)} %param.34, bf16[32,8,3072]{2,1,0:T(8,128)(2,1)} %all_to_all.25), kind=kOutput, calls=%fused_computation.13 | convolution fusion | flops 905969664 | bytes 5701632 | tf_op jit(solution)/shard_map/dot_general | solution.py:173
  181.1 17.7 %all-to-all-done.3 = bf16[32,8,3072]{2,1,0:T(8,128)(2,1)} async-done(((bf16[32,8,3072]{2,1,0:T(8,128)(2,1)}), bf16[32,8,3072]{2,1,0:T(8,128)(2,1)}, u32[]{:S(2)}, u32[]{:S(2)}) %all-to-all-start.3) | async-done | bytes 1572896 | tf_op jit(solution)/shard_map/all_to_all | solution.py:169
  198.8 4.4 %fusion.8 = f32[256,576]{0,1:T(8,128)} fusion(bf16[1,3072,576]{1,2,0:T(8,128)(2,1)} %param.34, bf16[32,8,3072]{2,1,0:T(8,128)(2,1)} %all-to-all-done.3), kind=kOutput, calls=%fused_computation.11 | convolution fusion | flops 905969664 | bytes 5701632 | tf_op jit(solution)/shard_map/dot_general | solution.py:173
  203.2 8.0 %fusion = bf16[32,1,8,3072]{3,2,1,0:T(8,128)(2,1)} fusion(bf16[1,576,3072]{2,1,0:T(8,128)(2,1)S(1)} %copy-done, bf16[1,3072,576]{1,2,0:T(8,128)(2,1)} %param.35, bf16[32,8,3072]{2,1,0:T(8,128)(2,1)} %all_to_all.25, f32[256,576]{0,1:T(8,128)} %fusion.10), kind=kOutput, calls=%fused_computation.3 | convolution fusion | flops 1813610496 | bytes 10813440 | tf_op jit(solution)/shard_map/dot_general | solution.py:177
  211.2 8.1 %fusion.1 = bf16[32,1,8,3072]{3,2,1,0:T(8,128)(2,1)} fusion(bf16[1,576,3072]{2,1,0:T(8,128)(2,1)S(1)} %copy-done, bf16[1,3072,576]{1,2,0:T(8,128)(2,1)} %param.35, bf16[32,8,3072]{2,1,0:T(8,128)(2,1)} %all-to-all-done.3, f32[256,576]{0,1:T(8,128)} %fusion.8), kind=kOutput, calls=%fused_computation.4 | convolution fusion | flops 1813610496 | bytes 10813440 | tf_op jit(solution)/shard_map/dot_general | solution.py:177
  219.4 3.9 %pad_maximum_fusion = bf16[32,2,8,3072]{3,2,1,0:T(8,128)(2,1)} fusion(bf16[32,1,8,3072]{3,2,1,0:T(8,128)(2,1)} %fusion.1, bf16[32,1,8,3072]{3,2,1,0:T(8,128)(2,1)} %fusion), kind=kLoop, calls=%fused_computation.16 | loop fusion | flops 1572864 | bytes 6291456 | tf_op jit(solution)/shard_map/stack | solution.py:181
  223.2 4.7 %copy.181 = bf16[512,3072]{0,1:T(8,128)(2,1)} copy(bf16[512,3072]{1,0:T(8,128)(2,1)} %bitcast.224) | data formatting | bytes 6291456
  227.9 1.3 slice_bitcast_fusion.2
  229.2 36.1 %reduce-scatter.4.cloned.1.call-done = bf16[384,512]{1,0:T(8,128)(2,1)} async-done(((bf16[3072,512]{1,0:T(8,128)(2,1)}), bf16[384,512]{1,0:T(8,128)(2,1)}) %reduce-scatter.4.cloned.1.call-update) | async-done | bytes 393232
  265.4 1.9 copy.182
  267.3 10.6 %all-to-all-start.4 = ((bf16[32,16,384]{2,1,0:T(8,128)(2,1)}), bf16[32,16,384]{2,1,0:T(8,128)(2,1)}, u32[]{:S(2)}, u32[]{:S(2)}) async-start(bf16[32,16,384]{2,1,0:T(8,128)(2,1)} %bitcast.227), calls=%async_computation.4 | async-start | bytes 786432 | tf_op jit(solution)/shard_map/all_to_all | solution.py:183
  277.8 3.1 %fusion.43 = f32[128,32]{0,1:T(8,128)S(1)} fusion(f32[3072,32]{0,1:T(8,128)} %param.33, f32[128,3072]{1,0:T(8,128)} %bitcast.220, f32[3072]{0:T(1024)S(1)} %copy-done.11, f32[128]{0:T(128)} %copy-done.21), kind=kOutput, calls=%fused_computation.43 | convolution fusion | flops 151392256 | bytes 1995264 | tf_op jit(solution)/shard_map/dot_general | solution.py:156
  281.0 7.1 %all-to-all-done.4 = bf16[32,16,384]{2,1,0:T(8,128)(2,1)} async-done(((bf16[32,16,384]{2,1,0:T(8,128)(2,1)}), bf16[32,16,384]{2,1,0:T(8,128)(2,1)}, u32[]{:S(2)}, u32[]{:S(2)}) %all-to-all-start.4) | async-done | bytes 393248 | tf_op jit(solution)/shard_map/all_to_all | solution.py:183
  288.0 1.3 fusion.41
  289.4 1.9 fusion.42
  (115 shorter events, 31.9 us)
Async XLA Ops:
  6.5 196.7 %copy-start = (bf16[1,576,3072]{2,1,0:T(8,128)(2,1)S(1)}, bf16[1,576,3072]{2,1,0:T(8,128)(2,1)}, u32[]{:S(2)}) copy-start(bf16[1,576,3072]{2,1,0:T(8,128)(2,1)} %param.36) | copy-start | bytes 10616836
  6.5 69.8 %all-gather.3.cloned.1.call-start = ((), (), s32[]{:S(2)}) async-start(), calls=%async_computation.6 | async-start | bytes 3244032 | tf_op jit(solution)/shard_map/all_gather | solution.py:125
  7.8 0.5 copy-start.16
  13.1 7.9 %collective-permute-start.1 = (bf16[4,144,128]{2,1,0:T(8,128)(2,1)}, bf16[4,144,128]{2,1,0:T(8,128)(2,1)}, u32[]{:S(2)}, u32[]{:S(2)}) collective-permute-start(bf16[4,144,128]{2,1,0:T(8,128)(2,1)} %fusion.85), channel_id=1, source_target_pairs={{0,16},{8,24},{16,32},{24,40},{32,48},{40,56},{48,64},{56,72},{64,... | collective-permute-start | bytes 442376 | tf_op jit(solution)/shard_map/ppermute | solution.py:39
  17.7 5.7 %collective-permute-start = (bf16[4,144,128]{2,1,0:T(8,128)(2,1)}, bf16[4,144,128]{2,1,0:T(8,128)(2,1)}, u32[]{:S(2)}, u32[]{:S(2)}) collective-permute-start(bf16[4,144,128]{2,1,0:T(8,128)(2,1)} %fusion.85), channel_id=1, source_target_pairs={{0,8},{8,16},{16,24},{24,32},{32,40},{40,48},{48,56},{56,64},{64,7... | collective-permute-start | bytes 442376 | tf_op jit(solution)/shard_map/ppermute | solution.py:39
  24.8 0.5 copy-start.17
  27.8 4.9 %collective-permute-start.2 = (bf16[4,144,128]{2,1,0:T(8,128)(2,1)S(1)}, bf16[4,144,128]{2,1,0:T(8,128)(2,1)S(1)}, u32[]{:S(2)}, u32[]{:S(2)}) collective-permute-start(bf16[4,144,128]{2,1,0:T(8,128)(2,1)S(1)} %fusion.86), channel_id=1, source_target_pairs={{0,16},{8,24},{16,32},{24,40},{32,48},{40,56},{48,64},{56,72},{64,... | collective-permute-start | bytes 442376 | tf_op jit(solution)/shard_map/ppermute | solution.py:39
  32.7 0.6 copy-start.2
  33.5 0.7 copy-start.18
  34.1 0.5 copy-start.23
  37.2 7.4 %collective-permute-start.3 = (bf16[4,144,128]{2,1,0:T(8,128)(2,1)S(1)}, bf16[4,144,128]{2,1,0:T(8,128)(2,1)S(1)}, u32[]{:S(2)}, u32[]{:S(2)}) collective-permute-start(bf16[4,144,128]{2,1,0:T(8,128)(2,1)S(1)} %fusion.87), channel_id=1, source_target_pairs={{0,32},{8,40},{16,48},{24,56},{32,64},{40,72},{48,80},{56,88},{64,... | collective-permute-start | bytes 442376 | tf_op jit(solution)/shard_map/ppermute | solution.py:39
  44.6 0.6 copy-start.6
  45.4 0.6 copy-start.19
  46.0 0.5 copy-start.22
  49.1 9.9 %collective-permute-start.4 = (bf16[4,144,128]{2,1,0:T(8,128)(2,1)S(1)}, bf16[4,144,128]{2,1,0:T(8,128)(2,1)S(1)}, u32[]{:S(2)}, u32[]{:S(2)}) collective-permute-start(bf16[4,144,128]{2,1,0:T(8,128)(2,1)S(1)} %fusion.88), channel_id=1, source_target_pairs={{0,64},{8,72},{16,80},{24,88},{32,96},{40,104},{48,112},{56,120},{... | collective-permute-start | bytes 442376 | tf_op jit(solution)/shard_map/ppermute | solution.py:39
  59.1 0.7 copy-start.9
  59.8 0.6 copy-start.15
  61.8 10.1 %copy-start.3 = (bf16[4,144,128]{2,1,0:T(8,128)(2,1)S(1)}, bf16[4,144,128]{2,1,0:T(8,128)(2,1)}, u32[]{:S(2)}) copy-start(bf16[4,144,128]{2,1,0:T(8,128)(2,1)} %copy-done.2) | copy-start | bytes 442372
  61.8 10.1 %copy-start.7 = (bf16[4,144,128]{2,1,0:T(8,128)(2,1)S(1)}, bf16[4,144,128]{2,1,0:T(8,128)(2,1)}, u32[]{:S(2)}) copy-start(bf16[4,144,128]{2,1,0:T(8,128)(2,1)} %copy-done.6) | copy-start | bytes 442372
  61.8 10.1 %copy-start.10 = (bf16[4,144,128]{2,1,0:T(8,128)(2,1)S(1)}, bf16[4,144,128]{2,1,0:T(8,128)(2,1)}, u32[]{:S(2)}) copy-start(bf16[4,144,128]{2,1,0:T(8,128)(2,1)} %copy-done.9) | copy-start | bytes 442372
  61.8 10.1 %copy-start.24 = (f32[4]{0:T(128)S(1)}, f32[4]{0:T(128)}, u32[]{:S(2)}) copy-start(f32[4]{0:T(128)} %add_exponential_fusion.2) | copy-start | bytes 52
  61.9 10.1 %copy-start.25 = (bf16[128,512]{1,0:T(8,128)(2,1)S(1)}, bf16[128,512]{1,0:T(8,128)(2,1)}, u32[]{:S(2)}) copy-start(bf16[128,512]{1,0:T(8,128)(2,1)} %param.25) | copy-start | bytes 393220
  62.6 10.9 %copy-start.4 = (bf16[128,512]{1,0:T(8,128)(2,1)S(1)}, bf16[128,512]{1,0:T(8,128)(2,1)}, u32[]{:S(2)}) copy-start(bf16[128,512]{1,0:T(8,128)(2,1)} %param.27) | copy-start | bytes 393220
  62.6 10.9 %copy-start.14 = (f32[4,128]{1,0:T(4,128)S(1)}, f32[4,128]{1,0:T(4,128)}, u32[]{:S(2)}) copy-start(f32[4,128]{1,0:T(4,128)} %get-tuple-element.84) | copy-start | bytes 6148
  64.0 10.0 %copy-start.20 = (f32[512]{0:T(512)S(1)}, f32[512]{0:T(512)}, u32[]{:S(2)}) copy-start(f32[512]{0:T(512)} %param.31) | copy-start | bytes 6148
  64.0 7.9 %collective-permute-start.5 = (bf16[4,144,128]{2,1,0:T(8,128)(2,1)S(1)}, bf16[4,144,128]{2,1,0:T(8,128)(2,1)S(1)}, u32[]{:S(2)}, u32[]{:S(2)}) collective-permute-start(bf16[4,144,128]{2,1,0:T(8,128)(2,1)S(1)} %fusion.89), channel_id=1, source_target_pairs={{0,128},{8,136},{16,144},{24,152},{32,160},{40,168},{48,176},{56,1... | collective-permute-start | bytes 442376 | tf_op jit(solution)/shard_map/ppermute | solution.py:39
  76.4 2.3 copy-start.5
  80.8 26.2 %all-to-all-start = ((bf16[8,128,384]{2,1,0:T(8,128)(2,1)}), bf16[8,128,384]{2,1,0:T(8,128)(2,1)}, u32[]{:S(2)}, u32[]{:S(2)}) async-start(bf16[8,128,384]{2,1,0:T(8,128)(2,1)} %fusion.19), calls=%async_computation | async-start | bytes 1572864 | tf_op jit(solution)/shard_map/all_to_all | solution.py:134
  108.2 6.1 %copy-start.12 = (s32[128,2]{0,1:T(2,128)S(1)}, s32[128,2]{0,1:T(2,128)}, u32[]{:S(2)}) copy-start(s32[128,2]{0,1:T(2,128)} %param.37) | copy-start | bytes 3076
  110.1 21.6 %all-to-all-start.1 = ((bf16[8,128,384]{2,1,0:T(8,128)(2,1)}), bf16[8,128,384]{2,1,0:T(8,128)(2,1)}, u32[]{:S(2)}, u32[]{:S(2)}) async-start(bf16[8,128,384]{2,1,0:T(8,128)(2,1)} %broadcast_in_dim.30), calls=%async_computation.1 | async-start | bytes 1572864 | tf_op jit(solution)/shard_map/all_to_all | solution.py:144
  123.1 0.6 copy-start.13
  132.9 2.2 copy-start.8
  132.9 2.2 copy-start.11
  133.1 3.0 %copy-start.1 = (f32[8,16,8,384]{3,2,0,1:T(8,128)}, f32[8,16,8,384]{3,2,0,1:T(8,128)S(1)}, u32[]{:S(2)}) copy-start(f32[8,16,8,384]{3,2,0,1:T(8,128)S(1)} %copy.187) | copy-start | bytes 4718596
  135.1 1.1 copy-start.21
  171.7 27.1 %all-to-all-start.3 = ((bf16[32,8,3072]{2,1,0:T(8,128)(2,1)}), bf16[32,8,3072]{2,1,0:T(8,128)(2,1)}, u32[]{:S(2)}, u32[]{:S(2)}) async-start(bf16[32,8,3072]{2,1,0:T(8,128)(2,1)} %get-tuple-element.82), calls=%async_computation.3 | async-start | bytes 3145728 | tf_op jit(solution)/shard_map/all_to_all | solution.py:169
  176.4 89.0 %reduce-scatter.4.cloned.1.call-start = ((), (), s32[]{:S(2)}) async-start(), calls=%async_computation.7 | async-start | bytes 3538944
  267.3 20.8 %all-to-all-start.4 = ((bf16[32,16,384]{2,1,0:T(8,128)(2,1)}), bf16[32,16,384]{2,1,0:T(8,128)(2,1)}, u32[]{:S(2)}, u32[]{:S(2)}) async-start(bf16[32,16,384]{2,1,0:T(8,128)(2,1)} %bitcast.227), calls=%async_computation.4 | async-start | bytes 786432 | tf_op jit(solution)/shard_map/all_to_all | solution.py:183
Sparse Core Ops, SparseCore 0:
  21.2 55.1 all-gather.2
  228.0 37.3 reduce-scatter.3

commit v9 on v6

--- a/solution.py
+++ b/solution.py
@@ -122,14 +122,14 @@
     )
     ctx_size = lax.axis_size("ctx")
     head_count = lax.axis_size("head")
-    weight_blocks = lax.all_gather(out_weight, "ctx")
+    weight_blocks = lax.all_gather(out_weight, "ctx", axis=1, tiled=True)
     model_width = residual.shape[1]
     experts_total = router.shape[1]
     capacity = 2 * token_count * TOP // experts_total
     slice_width = model_width // head_count
     slice_start = lax.axis_index("head") * slice_width
-    partial_out = jnp.einsum(
-        "tk,ckd->tcd", heads_normed, weight_blocks, preferred_element_type=jnp.float32
+    partial_out = jnp.dot(
+        heads_normed, weight_blocks, preferred_element_type=jnp.float32
     ).reshape(token_count, head_count, slice_width)
     pieces = lax.all_to_all(
         partial_out.astype(jnp.bfloat16).transpose(1, 0, 2),

time: 279 us -> 278 us (level)
    unnamed x46 -> x44, local copies, waits for them, and re-layouts: 13.7 us -> 13.5 us
  transfers between devices with their start and end apart: 11 -> 11, of which waited for: 10 -> 9; matrix products, arithmetic and copies ran while one was open for 13% -> 13% of each run, Pallas kernels for 0% -> 0%
where the time goes in v9:
time: 278 us; the launch traced here: 277 us
  waiting for transfers between devices  75.7 us (27%)
  starting transfers between devices  53.4 us (19%)
  blocking collectives  50.7 us (18%)
  matrix products  29.3 us (11%)
  other arithmetic  28.4 us (10%)
  local copies, waits for them, and re-layouts  25.6 us (9%)
  between operations  13.7 us (5%)
    all_to_all x1, blocking collectives, body(): lax.all_to_all(packed.reshape(experts_total, capacity, width_here), 'ctx'...  50.7 us
    unnamed x3, waiting for transfers between devices  36 us
    ppermute x6, starting transfers between devices, shifted(): return unpack(lax.ppermute(pack(value), axis, pairs))  28.9 us
    all_to_all x1, waiting for transfers between devices, body(): lax.all_to_all(partial_out.astype(jnp.bfloat16).transpose(1, 0, 2), 'head...  17.3 us
    unnamed x44, local copies, waits for them, and re-layouts  13.5 us
    all_to_all x1, starting transfers between devices, body(): lax.all_to_all(summed.reshape(experts_total, capacity, slice_width), 'ctx...  10.5 us
    all_to_all x1, starting transfers between devices, body(): lax.all_to_all(partial_out.astype(jnp.bfloat16).transpose(1, 0, 2), 'head...  9.78 us
    dot_general x1, matrix products, body(): jnp.dot(hidden, w_down[0], preferred_element_type=jnp.float32)  9.51 us
  transfers between devices with their start and end apart: 11, of which 9 were waited for; matrix products, arithmetic and copies ran while one was open for 13% of the time, Pallas kernels for 0%

profile of v9, /device:TPU:1, one launch (start us, length us, event | category | flops | bytes accessed | tf_op | source)
XLA Modules:
  0.0 276.8 jit_solution(12161434649635747426)
XLA Ops:
  6.5 1.1 reduce_window_sum.26
  8.4 1.2 exponential_bitcast_fusion
  9.6 1.7 copy.151
  11.2 1.2 convolution_convert_fusion.3
  13.1 4.6 %collective-permute-start.1 = (bf16[4,144,128]{2,1,0:T(8,128)(2,1)}, bf16[4,144,128]{2,1,0:T(8,128)(2,1)}, u32[]{:S(2)}, u32[]{:S(2)}) collective-permute-start(bf16[4,144,128]{2,1,0:T(8,128)(2,1)} %fusion.47), channel_id=1, source_target_pairs={{0,16},{8,24},{16,32},{24,40},{32,48},{40,56},{48,64},{56,72},{64,... | collective-permute-start | bytes 442376 | tf_op jit(solution)/shard_map/ppermute | solution.py:39
  17.7 3.3 %collective-permute-start = (bf16[4,144,128]{2,1,0:T(8,128)(2,1)}, bf16[4,144,128]{2,1,0:T(8,128)(2,1)}, u32[]{:S(2)}, u32[]{:S(2)}) collective-permute-start(bf16[4,144,128]{2,1,0:T(8,128)(2,1)} %fusion.47), channel_id=1, source_target_pairs={{0,8},{8,16},{16,24},{24,32},{32,40},{40,48},{48,56},{56,64},{64,7... | collective-permute-start | bytes 442376 | tf_op jit(solution)/shard_map/ppermute | solution.py:39
  21.9 1.5 collective-permute-done
  26.8 1.1 fusion.45
  27.9 2.8 %collective-permute-start.2 = (bf16[4,144,128]{2,1,0:T(8,128)(2,1)S(1)}, bf16[4,144,128]{2,1,0:T(8,128)(2,1)S(1)}, u32[]{:S(2)}, u32[]{:S(2)}) collective-permute-start(bf16[4,144,128]{2,1,0:T(8,128)(2,1)S(1)} %fusion.48), channel_id=1, source_target_pairs={{0,16},{8,24},{16,32},{24,40},{32,48},{40,56},{48,64},{56,72},{64,... | collective-permute-start | bytes 442376 | tf_op jit(solution)/shard_map/ppermute | solution.py:39
  30.7 2.1 collective-permute-done.2
  36.1 1.2 fusion.74
  37.3 5.3 %collective-permute-start.3 = (bf16[4,144,128]{2,1,0:T(8,128)(2,1)S(1)}, bf16[4,144,128]{2,1,0:T(8,128)(2,1)S(1)}, u32[]{:S(2)}, u32[]{:S(2)}) collective-permute-start(bf16[4,144,128]{2,1,0:T(8,128)(2,1)S(1)} %fusion.49), channel_id=1, source_target_pairs={{0,32},{8,40},{16,48},{24,56},{32,64},{40,72},{48,80},{56,88},{64,... | collective-permute-start | bytes 442376 | tf_op jit(solution)/shard_map/ppermute | solution.py:39
  42.7 1.2 add_exponential_fusion.2
  43.9 1.1 collective-permute-done.3
  48.2 1.3 fusion.46
  49.5 7.5 %collective-permute-start.4 = (bf16[4,144,128]{2,1,0:T(8,128)(2,1)S(1)}, bf16[4,144,128]{2,1,0:T(8,128)(2,1)S(1)}, u32[]{:S(2)}, u32[]{:S(2)}) collective-permute-start(bf16[4,144,128]{2,1,0:T(8,128)(2,1)S(1)} %fusion.50), channel_id=1, source_target_pairs={{0,64},{8,72},{16,80},{24,88},{32,96},{40,104},{48,112},{56,120},{... | collective-permute-start | bytes 442376 | tf_op jit(solution)/shard_map/ppermute | solution.py:39
  57.6 2.7 collective-permute-done.4
  63.8 1.4 fusion.73
  65.2 5.3 %collective-permute-start.5 = (bf16[4,144,128]{2,1,0:T(8,128)(2,1)S(1)}, bf16[4,144,128]{2,1,0:T(8,128)(2,1)S(1)}, u32[]{:S(2)}, u32[]{:S(2)}) collective-permute-start(bf16[4,144,128]{2,1,0:T(8,128)(2,1)S(1)} %fusion.51), channel_id=1, source_target_pairs={{0,128},{8,136},{16,144},{24,152},{32,160},{40,168},{48,176},{56,1... | collective-permute-start | bytes 442376 | tf_op jit(solution)/shard_map/ppermute | solution.py:39
  70.5 1.1 convolution_multiply_fusion
  72.6 1.8 fusion.39
  74.4 1.1 fusion.34
  75.5 1.5 fusion.38
  77.0 4.0 %fusion.14 = bf16[8,128,384]{2,1,0:T(8,128)(2,1)} fusion(bf16[128,512,1]{0,1,2:T(8,128)(2,1)} %bitcast.180, bf16[8,384,512]{2,1,0:T(8,128)(2,1)} %bitcast.178), kind=kOutput, calls=%fused_computation.17 | convolution fusion | flops 403046400 | bytes 4063232 | tf_op jit(solution)/shard_map/dot_general | solution.py:131
  81.0 9.8 %all-to-all-start = ((bf16[8,128,384]{2,1,0:T(8,128)(2,1)}), bf16[8,128,384]{2,1,0:T(8,128)(2,1)}, u32[]{:S(2)}, u32[]{:S(2)}) async-start(bf16[8,128,384]{2,1,0:T(8,128)(2,1)} %fusion.14), calls=%async_computation | async-start | bytes 1572864 | tf_op jit(solution)/shard_map/all_to_all | solution.py:134
  90.8 17.3 %all-to-all-done = bf16[8,128,384]{2,1,0:T(8,128)(2,1)} async-done(((bf16[8,128,384]{2,1,0:T(8,128)(2,1)}), bf16[8,128,384]{2,1,0:T(8,128)(2,1)}, u32[]{:S(2)}, u32[]{:S(2)}) %all-to-all-start) | async-done | bytes 786464 | tf_op jit(solution)/shard_map/all_to_all | solution.py:134
  108.1 1.3 convert_reduce_fusion
  111.2 4.2 %all-to-all-start.1 = ((bf16[8,128,384]{2,1,0:T(8,128)(2,1)}), bf16[8,128,384]{2,1,0:T(8,128)(2,1)}, u32[]{:S(2)}, u32[]{:S(2)}) async-start(bf16[8,128,384]{2,1,0:T(8,128)(2,1)} %broadcast_in_dim.30), calls=%async_computation.1 | async-start | bytes 1572864 | tf_op jit(solution)/shard_map/all_to_all | solution.py:144
  116.2 1.0 eq.67
  117.2 1.0 eq.63
  118.8 1.9 reduce-window.6
  125.5 7.0 %all-to-all-done.1 = bf16[8,128,384]{2,1,0:T(8,128)(2,1)} async-done(((bf16[8,128,384]{2,1,0:T(8,128)(2,1)}), bf16[8,128,384]{2,1,0:T(8,128)(2,1)}, u32[]{:S(2)}, u32[]{:S(2)}) %all-to-all-start.1) | async-done | bytes 786464 | tf_op jit(solution)/shard_map/all_to_all | solution.py:144
  132.5 1.3 convert_bitcast_fusion
  134.0 1.9 fusion.5
  135.9 1.0 convolution_convert_fusion.1
  137.0 50.7 %all_to_all.20 = bf16[32,16,3072]{2,1,0:T(8,128)(2,1)S(1)} all-to-all(bf16[32,16,3072]{2,1,0:T(8,128)(2,1)S(1)} %bitcast.175), channel_id=1, replica_groups=mesh['ctx'=32,'head'=8] {'ctx'}, dimensions={0} | all-to-all | bytes 6291456 | tf_op jit(solution)/shard_map/all_to_all | solution.py:166
  187.8 1.6 copy-done.2
  189.4 3.1 %fusion.3 = f32[512,576]{0,1:T(8,128)} fusion(bf16[512,3072]{1,0:T(8,128)(2,1)S(1)} %bitcast.176, bf16[1,3072,576]{1,2,0:T(8,128)(2,1)S(1)} %copy-done.19), kind=kOutput, calls=%fused_computation.5 | convolution fusion | flops 1811939328 | bytes 7864320 | tf_op jit(solution)/shard_map/dot_general | solution.py:174
  192.6 9.5 %convolution_convert_fusion = bf16[512,3072]{1,0:T(8,128)(2,1)} fusion(bf16[1,576,3072]{2,1,0:T(8,128)(2,1)S(1)} %copy-done, bf16[512,3072]{1,0:T(8,128)(2,1)} %bitcast.177, bf16[1,3072,576]{1,2,0:T(8,128)(2,1)} %param.35, f32[512,576]{0,1:T(8,128)} %fusion.3), kind=kOutput, calls=%fused_computation | convolution fusion | flops 3627220992 | bytes 14548992 | tf_op jit(solution)/shard_map/dot_general | solution.py:177
  202.1 4.7 %copy.165 = bf16[512,3072]{0,1:T(8,128)(2,1)} copy(bf16[512,3072]{1,0:T(8,128)(2,1)} %convolution_convert_fusion) | data formatting | bytes 6291456
  206.8 1.3 slice_bitcast_fusion
  208.1 36.0 %reduce-scatter.4.cloned.1.call-done = bf16[384,512]{1,0:T(8,128)(2,1)} async-done(((bf16[3072,512]{1,0:T(8,128)(2,1)}), bf16[384,512]{1,0:T(8,128)(2,1)}) %reduce-scatter.4.cloned.1.call-update) | async-done | bytes 393232
  244.1 1.9 copy.166
  246.0 10.5 %all-to-all-start.3 = ((bf16[32,16,384]{2,1,0:T(8,128)(2,1)}), bf16[32,16,384]{2,1,0:T(8,128)(2,1)}, u32[]{:S(2)}, u32[]{:S(2)}) async-start(bf16[32,16,384]{2,1,0:T(8,128)(2,1)} %bitcast.179), calls=%async_computation.3 | async-start | bytes 786432 | tf_op jit(solution)/shard_map/all_to_all | solution.py:181
  256.5 3.1 %fusion.18 = f32[128,32]{0,1:T(8,128)S(1)} fusion(f32[3072,32]{0,1:T(8,128)} %param.33, f32[128,3072]{1,0:T(8,128)} %bitcast.172, f32[3072]{0:T(1024)S(1)} %copy-done.8, f32[128]{0:T(128)} %copy-done.16), kind=kOutput, calls=%fused_computation.25 | convolution fusion | flops 151392256 | bytes 1995264 | tf_op jit(solution)/shard_map/dot_general | solution.py:156
  259.6 7.1 %all-to-all-done.3 = bf16[32,16,384]{2,1,0:T(8,128)(2,1)} async-done(((bf16[32,16,384]{2,1,0:T(8,128)(2,1)}), bf16[32,16,384]{2,1,0:T(8,128)(2,1)}, u32[]{:S(2)}, u32[]{:S(2)}) %all-to-all-start.3) | async-done | bytes 393248 | tf_op jit(solution)/shard_map/all_to_all | solution.py:181
  266.7 1.3 fusion.16
  268.0 1.9 fusion.17
  (96 shorter events, 25.4 us)
Async XLA Ops:
  6.5 186.0 %copy-start = (bf16[1,576,3072]{2,1,0:T(8,128)(2,1)S(1)}, bf16[1,576,3072]{2,1,0:T(8,128)(2,1)}, u32[]{:S(2)}) copy-start(bf16[1,576,3072]{2,1,0:T(8,128)(2,1)} %param.36) | copy-start | bytes 10616836
  6.5 70.4 %all-gather.2.cloned.1.call-start = ((), (), s32[]{:S(2)}) async-start(), calls=%async_computation.5 | async-start | bytes 3244032 | tf_op jit(solution)/shard_map/all_gather | solution.py:125
  7.8 0.5 copy-start.12
  13.1 7.9 %collective-permute-start.1 = (bf16[4,144,128]{2,1,0:T(8,128)(2,1)}, bf16[4,144,128]{2,1,0:T(8,128)(2,1)}, u32[]{:S(2)}, u32[]{:S(2)}) collective-permute-start(bf16[4,144,128]{2,1,0:T(8,128)(2,1)} %fusion.47), channel_id=1, source_target_pairs={{0,16},{8,24},{16,32},{24,40},{32,48},{40,56},{48,64},{56,72},{64,... | collective-permute-start | bytes 442376 | tf_op jit(solution)/shard_map/ppermute | solution.py:39
  17.7 5.7 %collective-permute-start = (bf16[4,144,128]{2,1,0:T(8,128)(2,1)}, bf16[4,144,128]{2,1,0:T(8,128)(2,1)}, u32[]{:S(2)}, u32[]{:S(2)}) collective-permute-start(bf16[4,144,128]{2,1,0:T(8,128)(2,1)} %fusion.47), channel_id=1, source_target_pairs={{0,8},{8,16},{16,24},{24,32},{32,40},{40,48},{48,56},{56,64},{64,7... | collective-permute-start | bytes 442376 | tf_op jit(solution)/shard_map/ppermute | solution.py:39
  24.8 0.6 copy-start.13
  27.9 4.9 %collective-permute-start.2 = (bf16[4,144,128]{2,1,0:T(8,128)(2,1)S(1)}, bf16[4,144,128]{2,1,0:T(8,128)(2,1)S(1)}, u32[]{:S(2)}, u32[]{:S(2)}) collective-permute-start(bf16[4,144,128]{2,1,0:T(8,128)(2,1)S(1)} %fusion.48), channel_id=1, source_target_pairs={{0,16},{8,24},{16,32},{24,40},{32,48},{40,56},{48,64},{56,72},{64,... | collective-permute-start | bytes 442376 | tf_op jit(solution)/shard_map/ppermute | solution.py:39
  32.8 0.7 copy-start.3
  33.6 0.7 copy-start.14
  34.3 0.5 copy-start.18
  37.3 7.7 %collective-permute-start.3 = (bf16[4,144,128]{2,1,0:T(8,128)(2,1)S(1)}, bf16[4,144,128]{2,1,0:T(8,128)(2,1)S(1)}, u32[]{:S(2)}, u32[]{:S(2)}) collective-permute-start(bf16[4,144,128]{2,1,0:T(8,128)(2,1)S(1)} %fusion.49), channel_id=1, source_target_pairs={{0,32},{8,40},{16,48},{24,56},{32,64},{40,72},{48,80},{56,88},{64,... | collective-permute-start | bytes 442376 | tf_op jit(solution)/shard_map/ppermute | solution.py:39
  45.0 0.6 copy-start.5
  45.8 0.6 copy-start.15
  46.3 0.5 copy-start.17
  49.5 10.8 %collective-permute-start.4 = (bf16[4,144,128]{2,1,0:T(8,128)(2,1)S(1)}, bf16[4,144,128]{2,1,0:T(8,128)(2,1)S(1)}, u32[]{:S(2)}, u32[]{:S(2)}) collective-permute-start(bf16[4,144,128]{2,1,0:T(8,128)(2,1)S(1)} %fusion.50), channel_id=1, source_target_pairs={{0,64},{8,72},{16,80},{24,88},{32,96},{40,104},{48,112},{56,120},{... | collective-permute-start | bytes 442376 | tf_op jit(solution)/shard_map/ppermute | solution.py:39
  60.3 0.6 copy-start.7
  61.0 0.6 copy-start.11
  63.0 11.3 %copy-start.4 = (bf16[128,512]{1,0:T(8,128)(2,1)S(1)}, bf16[128,512]{1,0:T(8,128)(2,1)}, u32[]{:S(2)}) copy-start(bf16[128,512]{1,0:T(8,128)(2,1)} %param.27) | copy-start | bytes 393220
  65.2 7.4 %collective-permute-start.5 = (bf16[4,144,128]{2,1,0:T(8,128)(2,1)S(1)}, bf16[4,144,128]{2,1,0:T(8,128)(2,1)S(1)}, u32[]{:S(2)}, u32[]{:S(2)}) collective-permute-start(bf16[4,144,128]{2,1,0:T(8,128)(2,1)S(1)} %fusion.51), channel_id=1, source_target_pairs={{0,128},{8,136},{16,144},{24,152},{32,160},{40,168},{48,176},{56,1... | collective-permute-start | bytes 442376 | tf_op jit(solution)/shard_map/ppermute | solution.py:39
  81.0 34.5 %copy-start.9 = (s32[128,2]{0,1:T(2,128)S(1)}, s32[128,2]{0,1:T(2,128)}, u32[]{:S(2)}) copy-start(s32[128,2]{0,1:T(2,128)} %param.37) | copy-start | bytes 3076
  81.0 27.1 %all-to-all-start = ((bf16[8,128,384]{2,1,0:T(8,128)(2,1)}), bf16[8,128,384]{2,1,0:T(8,128)(2,1)}, u32[]{:S(2)}, u32[]{:S(2)}) async-start(bf16[8,128,384]{2,1,0:T(8,128)(2,1)} %fusion.14), calls=%async_computation | async-start | bytes 1572864 | tf_op jit(solution)/shard_map/all_to_all | solution.py:134
  111.2 21.3 %all-to-all-start.1 = ((bf16[8,128,384]{2,1,0:T(8,128)(2,1)}), bf16[8,128,384]{2,1,0:T(8,128)(2,1)}, u32[]{:S(2)}, u32[]{:S(2)}) async-start(bf16[8,128,384]{2,1,0:T(8,128)(2,1)} %broadcast_in_dim.30), calls=%async_computation.1 | async-start | bytes 1572864 | tf_op jit(solution)/shard_map/all_to_all | solution.py:144
  115.4 128.6 %reduce-scatter.4.cloned.1.call-start = ((), (), s32[]{:S(2)}) async-start(), calls=%async_computation.6 | async-start | bytes 3538944
  124.2 0.6 copy-start.10
  125.5 10.4 %copy-start.8 = (f32[3072]{0:T(1024)S(1)}, f32[3072]{0:T(1024)}, u32[]{:S(2)}) copy-start(f32[3072]{0:T(1024)} %param.32) | copy-start | bytes 36868
  132.5 3.4 %copy-start.6 = (pred[512,128]{1,0:T(8,128)(4,1)S(1)}, pred[512,128]{1,0:T(8,128)(4,1)}, u32[]{:S(2)}) copy-start(pred[512,128]{1,0:T(8,128)(4,1)} %fusion.27) | copy-start | bytes 196612
  134.0 53.8 %copy-start.1 = (f32[8,16,8,384]{3,2,0,1:T(8,128)}, f32[8,16,8,384]{3,2,0,1:T(8,128)S(1)}, u32[]{:S(2)}) copy-start(f32[8,16,8,384]{3,2,0,1:T(8,128)S(1)} %copy.170) | copy-start | bytes 4718596
  135.9 1.1 copy-start.16
  137.0 52.4 %copy-start.19 = (bf16[1,3072,576]{1,2,0:T(8,128)(2,1)S(1)}, bf16[1,3072,576]{1,2,0:T(8,128)(2,1)}, u32[]{:S(2)}) copy-start(bf16[1,3072,576]{1,2,0:T(8,128)(2,1)} %param.34) | copy-start | bytes 10616836
  187.8 1.6 copy-start.2
  246.0 20.7 %all-to-all-start.3 = ((bf16[32,16,384]{2,1,0:T(8,128)(2,1)}), bf16[32,16,384]{2,1,0:T(8,128)(2,1)}, u32[]{:S(2)}, u32[]{:S(2)}) async-start(bf16[32,16,384]{2,1,0:T(8,128)(2,1)} %bitcast.179), calls=%async_computation.3 | async-start | bytes 786432 | tf_op jit(solution)/shard_map/all_to_all | solution.py:181
Sparse Core Ops, SparseCore 0:
  21.2 53.1 all-gather.1
  206.9 37.1 reduce-scatter.3

commit v10 on v6

--- a/solution.py
+++ b/solution.py
@@ -174,10 +174,15 @@
     gate_part = jnp.dot(flat_rows, w_gate[0], preferred_element_type=jnp.float32)
     up_part = jnp.dot(flat_rows, w_up[0], preferred_element_type=jnp.float32)
     hidden = (jax.nn.silu(gate_part) * up_part).astype(jnp.bfloat16)
-    partial_down = jnp.dot(hidden, w_down[0], preferred_element_type=jnp.float32)
+    partial_down = jnp.einsum(
+        "sf,fhj->hsj",
+        hidden,
+        w_down[0].reshape(w_down.shape[1], head_count, slice_width),
+        preferred_element_type=jnp.float32,
+    )
     summed = lax.psum_scatter(
-        partial_down.astype(jnp.bfloat16), "head", scatter_dimension=1, tiled=True
-    )
+        partial_down.astype(jnp.bfloat16), "head", scatter_dimension=0, tiled=True
+    ).reshape(-1, slice_width)
     returned = lax.all_to_all(
         summed.reshape(experts_total, capacity, slice_width),
         "ctx",

time: 279 us -> 276 us (0.989)
  blocking collectives: 51.2 us -> 0 us
  waiting for transfers between devices: 74.8 us -> 111 us
  starting transfers between devices: 54.1 us -> 65.8 us
  matrix products: 27.3 us -> 32 us
  local copies, waits for them, and re-layouts: 28 us -> 24 us
    all_to_all x1 -> x0, blocking collectives: 51.2 us -> none  [body(): lax.all_to_all(packed.reshape(experts_total, capacity, width_here), 'ctx'...]
    reduce_scatter x0 -> x1, waiting for transfers between devices: none -> 36.3 us  [body(): lax.psum_scatter(partial_down.astype(jnp.bfloat16), 'head', scatter_dimen...]
    unnamed x3 -> x2, waiting for transfers between devices: 35.3 us -> 0.03 us
    all_to_all x0 -> x1, waiting for transfers between devices: none -> 35 us  [body(): lax.all_to_all(packed.reshape(experts_total, capacity, width_here), 'ctx'...]
    all_to_all x0 -> x1, starting transfers between devices: none -> 11.7 us  [body(): lax.all_to_all(packed.reshape(experts_total, capacity, width_here), 'ctx'...]
    unnamed x46 -> x41, local copies, waits for them, and re-layouts: 13.7 us -> 9.65 us
    dot_general x1, matrix products: 3.15 us -> 6 us  [body(): jnp.dot(flat_rows, w_gate[0], preferred_element_type=jnp.float32)]
  transfers between devices with their start and end apart: 11 -> 12, of which waited for: 10 -> 11; matrix products, arithmetic and copies ran while one was open for 13% -> 15% of each run, Pallas kernels for 0% -> 0%
where the time goes in v10:
time: 276 us; the launch traced here: 275 us
  waiting for transfers between devices  111 us (40%)
  starting transfers between devices  65.8 us (24%)
  matrix products  32 us (12%)
  other arithmetic  28.4 us (10%)
  local copies, waits for them, and re-layouts  24 us (9%)
  between operations  13.7 us (5%)
    reduce_scatter x1, waiting for transfers between devices, body(): lax.psum_scatter(partial_down.astype(jnp.bfloat16), 'head', scatter_dimen...  36.3 us
    all_to_all x1, waiting for transfers between devices, body(): lax.all_to_all(packed.reshape(experts_total, capacity, width_here), 'ctx'...  35 us
    ppermute x6, starting transfers between devices, shifted(): return unpack(lax.ppermute(pack(value), axis, pairs))  29.5 us
    all_to_all x1, waiting for transfers between devices, body(): lax.all_to_all(partial_out.astype(jnp.bfloat16).transpose(1, 0, 2), 'head...  17.7 us
    all_to_all x1, starting transfers between devices, body(): lax.all_to_all(packed.reshape(experts_total, capacity, width_here), 'ctx'...  11.7 us
    all_to_all x1, starting transfers between devices, body(): lax.all_to_all(summed.reshape(experts_total, capacity, slice_width), 'ctx...  10.7 us
    dot_general x1, matrix products, body(): jnp.einsum('sf,fhj->hsj', hidden, w_down[0].reshape(w_down.shape[1], head...  9.69 us
    unnamed x41, local copies, waits for them, and re-layouts  9.65 us
  transfers between devices with their start and end apart: 12, of which 11 were waited for; matrix products, arithmetic and copies ran while one was open for 15% of the time, Pallas kernels for 0%

profile of v10, /device:TPU:1, one launch (start us, length us, event | category | flops | bytes accessed | tf_op | source)
XLA Modules:
  0.0 274.9 jit_solution(7314895987584407772)
XLA Ops:
  6.5 1.1 reduce_window_sum.26
  8.0 1.7 copy.163
  9.6 1.3 exponential_bitcast_fusion
  10.9 1.2 convolution_convert_fusion.2
  12.8 4.6 %collective-permute-start.1 = (bf16[4,144,128]{2,1,0:T(8,128)(2,1)}, bf16[4,144,128]{2,1,0:T(8,128)(2,1)}, u32[]{:S(2)}, u32[]{:S(2)}) collective-permute-start(bf16[4,144,128]{2,1,0:T(8,128)(2,1)} %fusion.53), channel_id=1, source_target_pairs={{0,16},{8,24},{16,32},{24,40},{32,48},{40,56},{48,64},{56,72},{64,... | collective-permute-start | bytes 442376 | tf_op jit(solution)/shard_map/ppermute | solution.py:39
  17.4 3.3 %collective-permute-start = (bf16[4,144,128]{2,1,0:T(8,128)(2,1)}, bf16[4,144,128]{2,1,0:T(8,128)(2,1)}, u32[]{:S(2)}, u32[]{:S(2)}) collective-permute-start(bf16[4,144,128]{2,1,0:T(8,128)(2,1)} %fusion.53), channel_id=1, source_target_pairs={{0,8},{8,16},{16,24},{24,32},{32,40},{40,48},{48,56},{56,64},{64,7... | collective-permute-start | bytes 442376 | tf_op jit(solution)/shard_map/ppermute | solution.py:39
  21.5 1.5 collective-permute-done
  26.4 1.1 fusion.51
  27.5 2.8 %collective-permute-start.2 = (bf16[4,144,128]{2,1,0:T(8,128)(2,1)S(1)}, bf16[4,144,128]{2,1,0:T(8,128)(2,1)S(1)}, u32[]{:S(2)}, u32[]{:S(2)}) collective-permute-start(bf16[4,144,128]{2,1,0:T(8,128)(2,1)S(1)} %fusion.54), channel_id=1, source_target_pairs={{0,16},{8,24},{16,32},{24,40},{32,48},{40,56},{48,64},{56,72},{64,... | collective-permute-start | bytes 442376 | tf_op jit(solution)/shard_map/ppermute | solution.py:39
  30.3 2.1 collective-permute-done.2
  35.7 1.2 fusion.80
  36.9 5.3 %collective-permute-start.3 = (bf16[4,144,128]{2,1,0:T(8,128)(2,1)S(1)}, bf16[4,144,128]{2,1,0:T(8,128)(2,1)S(1)}, u32[]{:S(2)}, u32[]{:S(2)}) collective-permute-start(bf16[4,144,128]{2,1,0:T(8,128)(2,1)S(1)} %fusion.55), channel_id=1, source_target_pairs={{0,32},{8,40},{16,48},{24,56},{32,64},{40,72},{48,80},{56,88},{64,... | collective-permute-start | bytes 442376 | tf_op jit(solution)/shard_map/ppermute | solution.py:39
  42.3 1.2 add_exponential_fusion.2
  47.7 1.3 fusion.52
  49.0 7.5 %collective-permute-start.4 = (bf16[4,144,128]{2,1,0:T(8,128)(2,1)S(1)}, bf16[4,144,128]{2,1,0:T(8,128)(2,1)S(1)}, u32[]{:S(2)}, u32[]{:S(2)}) collective-permute-start(bf16[4,144,128]{2,1,0:T(8,128)(2,1)S(1)} %fusion.56), channel_id=1, source_target_pairs={{0,64},{8,72},{16,80},{24,88},{32,96},{40,104},{48,112},{56,120},{... | collective-permute-start | bytes 442376 | tf_op jit(solution)/shard_map/ppermute | solution.py:39
  57.2 1.9 collective-permute-done.4
  62.6 1.4 fusion.79
  64.0 5.9 %collective-permute-start.5 = (bf16[4,144,128]{2,1,0:T(8,128)(2,1)S(1)}, bf16[4,144,128]{2,1,0:T(8,128)(2,1)S(1)}, u32[]{:S(2)}, u32[]{:S(2)}) collective-permute-start(bf16[4,144,128]{2,1,0:T(8,128)(2,1)S(1)} %fusion.57), channel_id=1, source_target_pairs={{0,128},{8,136},{16,144},{24,152},{32,160},{40,168},{48,176},{56,1... | collective-permute-start | bytes 442376 | tf_op jit(solution)/shard_map/ppermute | solution.py:39
  69.9 1.1 convolution_multiply_fusion
  72.0 1.7 fusion.45
  73.8 1.1 fusion.40
  74.9 1.5 fusion.44
  76.6 2.3 copy.208
  79.0 2.1 fusion.17
  81.0 9.5 %all-to-all-start = ((bf16[8,128,384]{2,1,0:T(8,128)(2,1)}), bf16[8,128,384]{2,1,0:T(8,128)(2,1)}, u32[]{:S(2)}, u32[]{:S(2)}) async-start(bf16[8,128,384]{2,1,0:T(8,128)(2,1)} %fusion.17), calls=%async_computation | async-start | bytes 1572864 | tf_op jit(solution)/shard_map/all_to_all | solution.py:134
  90.5 17.7 %all-to-all-done = bf16[8,128,384]{2,1,0:T(8,128)(2,1)} async-done(((bf16[8,128,384]{2,1,0:T(8,128)(2,1)}), bf16[8,128,384]{2,1,0:T(8,128)(2,1)}, u32[]{:S(2)}, u32[]{:S(2)}) %all-to-all-start) | async-done | bytes 786464 | tf_op jit(solution)/shard_map/all_to_all | solution.py:134
  108.2 1.3 convert_reduce_fusion
  110.4 1.0 broadcast_in_dim.30
  111.4 4.2 %all-to-all-start.1 = ((bf16[8,128,384]{2,1,0:T(8,128)(2,1)}), bf16[8,128,384]{2,1,0:T(8,128)(2,1)}, u32[]{:S(2)}, u32[]{:S(2)}) async-start(bf16[8,128,384]{2,1,0:T(8,128)(2,1)} %broadcast_in_dim.30), calls=%async_computation.1 | async-start | bytes 1572864 | tf_op jit(solution)/shard_map/all_to_all | solution.py:144
  116.4 1.0 eq.63
  117.3 1.0 eq.67
  118.9 1.9 reduce-window.6
  125.6 7.3 %all-to-all-done.1 = bf16[8,128,384]{2,1,0:T(8,128)(2,1)} async-done(((bf16[8,128,384]{2,1,0:T(8,128)(2,1)}), bf16[8,128,384]{2,1,0:T(8,128)(2,1)}, u32[]{:S(2)}, u32[]{:S(2)}) %all-to-all-start.1) | async-done | bytes 786464 | tf_op jit(solution)/shard_map/all_to_all | solution.py:144
  132.9 1.3 convert_bitcast_fusion.1
  134.4 1.9 fusion.8
  136.4 2.7 convolution_convert_fusion
  139.1 11.7 %all-to-all-start.2 = ((bf16[32,16,3072]{2,1,0:T(8,128)(2,1)}), bf16[32,16,3072]{2,1,0:T(8,128)(2,1)}, u32[]{:S(2)}, u32[]{:S(2)}) async-start(bf16[32,16,3072]{2,1,0:T(8,128)(2,1)} %bitcast.184), calls=%async_computation.2 | async-start | bytes 6291456 | tf_op jit(solution)/shard_map/all_to_all | solution.py:166
  151.0 4.6 %copy.183 = bf16[72,8,8,384]{3,2,1,0:T(8,128)(2,1)} copy(bf16[72,8,8,384]{3,1,2,0:T(8,128)(2,1)} %bitcast.186) | data formatting | bytes 7077888
  155.6 35.0 %all-to-all-done.2 = bf16[32,16,3072]{2,1,0:T(8,128)(2,1)} async-done(((bf16[32,16,3072]{2,1,0:T(8,128)(2,1)}), bf16[32,16,3072]{2,1,0:T(8,128)(2,1)}, u32[]{:S(2)}, u32[]{:S(2)}) %all-to-all-start.2) | async-done | bytes 3145760 | tf_op jit(solution)/shard_map/all_to_all | solution.py:166
  190.6 6.0 %fusion.2 = f32[512,576]{0,1:T(8,128)} fusion(bf16[512,3072]{1,0:T(8,128)(2,1)} %bitcast.33, bf16[1,3072,576]{1,2,0:T(8,128)(2,1)} %param.34), kind=kOutput, calls=%fused_computation.3 | convolution fusion | flops 1811939328 | bytes 7864320 | tf_op jit(solution)/shard_map/dot_general | solution.py:174
  196.6 9.7 %convert_bitcast_fusion = bf16[8,512,384]{2,1,0:T(8,128)(2,1)} fusion(bf16[576,8,384]{2,1,0:T(8,128)(2,1)} %bitcast.187, bf16[512,3072]{1,0:T(8,128)(2,1)} %bitcast.33, bf16[1,3072,576]{1,2,0:T(8,128)(2,1)S(1)} %copy-done, f32[512,576]{0,1:T(8,128)} %fusion.2), kind=kOutput, calls=%fused_computation.8 | convolution fusion | flops 3627220992 | bytes 14548992 | tf_op jit(solution)/shard_map/sf,fhj->hsj/dot_general | solution.py:177
  206.3 1.3 slice_bitcast_fusion
  207.6 36.3 %reduce-scatter.2.cloned.1.call-done = bf16[1,512,384]{2,1,0:T(8,128)(2,1)} async-done(((bf16[8,512,384]{2,1,0:T(8,128)(2,1)}), bf16[1,512,384]{2,1,0:T(8,128)(2,1)}) %reduce-scatter.2.cloned.1.call-update) | async-done | bytes 393232 | tf_op jit(solution)/shard_map/reduce_scatter | solution.py:183
  243.9 10.7 %all-to-all-start.3 = ((bf16[32,16,384]{2,1,0:T(8,128)(2,1)}), bf16[32,16,384]{2,1,0:T(8,128)(2,1)}, u32[]{:S(2)}, u32[]{:S(2)}) async-start(bf16[32,16,384]{2,1,0:T(8,128)(2,1)} %bitcast.192), calls=%async_computation.4 | async-start | bytes 786432 | tf_op jit(solution)/shard_map/all_to_all | solution.py:186
  254.6 3.1 %fusion.24 = f32[128,32]{0,1:T(8,128)S(1)} fusion(f32[3072,32]{0,1:T(8,128)} %param.33, f32[128,3072]{1,0:T(8,128)} %bitcast.182, f32[3072]{0:T(1024)S(1)} %copy-done.8, f32[128]{0:T(128)} %copy-done.16), kind=kOutput, calls=%fused_computation.28 | convolution fusion | flops 151392256 | bytes 1995264 | tf_op jit(solution)/shard_map/dot_general | solution.py:156
  257.7 7.1 %all-to-all-done.3 = bf16[32,16,384]{2,1,0:T(8,128)(2,1)} async-done(((bf16[32,16,384]{2,1,0:T(8,128)(2,1)}), bf16[32,16,384]{2,1,0:T(8,128)(2,1)}, u32[]{:S(2)}, u32[]{:S(2)}) %all-to-all-start.3) | async-done | bytes 393248 | tf_op jit(solution)/shard_map/all_to_all | solution.py:186
  264.8 1.3 fusion.22
  266.1 1.9 fusion.23
  (95 shorter events, 25.5 us)
Async XLA Ops:
  6.5 190.1 %copy-start = (bf16[1,3072,576]{1,2,0:T(8,128)(2,1)S(1)}, bf16[1,3072,576]{1,2,0:T(8,128)(2,1)}, u32[]{:S(2)}) copy-start(bf16[1,3072,576]{1,2,0:T(8,128)(2,1)} %param.35) | copy-start | bytes 10616836
  6.5 70.1 %all-gather.3.cloned.1.call-start = ((), (), s32[]{:S(2)}) async-start(), calls=%async_computation.6 | async-start | bytes 3244032 | tf_op jit(solution)/shard_map/all_gather | solution.py:125
  7.8 1.8 copy-start.12
  12.8 7.9 %collective-permute-start.1 = (bf16[4,144,128]{2,1,0:T(8,128)(2,1)}, bf16[4,144,128]{2,1,0:T(8,128)(2,1)}, u32[]{:S(2)}, u32[]{:S(2)}) collective-permute-start(bf16[4,144,128]{2,1,0:T(8,128)(2,1)} %fusion.53), channel_id=1, source_target_pairs={{0,16},{8,24},{16,32},{24,40},{32,48},{40,56},{48,64},{56,72},{64,... | collective-permute-start | bytes 442376 | tf_op jit(solution)/shard_map/ppermute | solution.py:39
  17.4 5.7 %collective-permute-start = (bf16[4,144,128]{2,1,0:T(8,128)(2,1)}, bf16[4,144,128]{2,1,0:T(8,128)(2,1)}, u32[]{:S(2)}, u32[]{:S(2)}) collective-permute-start(bf16[4,144,128]{2,1,0:T(8,128)(2,1)} %fusion.53), channel_id=1, source_target_pairs={{0,8},{8,16},{16,24},{24,32},{32,40},{40,48},{48,56},{56,64},{64,7... | collective-permute-start | bytes 442376 | tf_op jit(solution)/shard_map/ppermute | solution.py:39
  24.5 0.5 copy-start.13
  27.5 4.9 %collective-permute-start.2 = (bf16[4,144,128]{2,1,0:T(8,128)(2,1)S(1)}, bf16[4,144,128]{2,1,0:T(8,128)(2,1)S(1)}, u32[]{:S(2)}, u32[]{:S(2)}) collective-permute-start(bf16[4,144,128]{2,1,0:T(8,128)(2,1)S(1)} %fusion.54), channel_id=1, source_target_pairs={{0,16},{8,24},{16,32},{24,40},{32,48},{40,56},{48,64},{56,72},{64,... | collective-permute-start | bytes 442376 | tf_op jit(solution)/shard_map/ppermute | solution.py:39
  32.4 0.6 copy-start.2
  33.2 0.6 copy-start.14
  33.8 0.6 copy-start.18
  36.9 7.4 %collective-permute-start.3 = (bf16[4,144,128]{2,1,0:T(8,128)(2,1)S(1)}, bf16[4,144,128]{2,1,0:T(8,128)(2,1)S(1)}, u32[]{:S(2)}, u32[]{:S(2)}) collective-permute-start(bf16[4,144,128]{2,1,0:T(8,128)(2,1)S(1)} %fusion.55), channel_id=1, source_target_pairs={{0,32},{8,40},{16,48},{24,56},{32,64},{40,72},{48,80},{56,88},{64,... | collective-permute-start | bytes 442376 | tf_op jit(solution)/shard_map/ppermute | solution.py:39
  44.4 0.7 copy-start.5
  45.1 0.7 copy-start.15
  45.8 0.6 copy-start.17
  49.0 10.0 %collective-permute-start.4 = (bf16[4,144,128]{2,1,0:T(8,128)(2,1)S(1)}, bf16[4,144,128]{2,1,0:T(8,128)(2,1)S(1)}, u32[]{:S(2)}, u32[]{:S(2)}) collective-permute-start(bf16[4,144,128]{2,1,0:T(8,128)(2,1)S(1)} %fusion.56), channel_id=1, source_target_pairs={{0,64},{8,72},{16,80},{24,88},{32,96},{40,104},{48,112},{56,120},{... | collective-permute-start | bytes 442376 | tf_op jit(solution)/shard_map/ppermute | solution.py:39
  59.1 0.7 copy-start.7
  59.8 0.7 copy-start.11
  61.9 11.9 %copy-start.3 = (bf16[128,512]{1,0:T(8,128)(2,1)S(1)}, bf16[128,512]{1,0:T(8,128)(2,1)}, u32[]{:S(2)}) copy-start(bf16[128,512]{1,0:T(8,128)(2,1)} %param.27) | copy-start | bytes 393220
  64.0 8.0 %collective-permute-start.5 = (bf16[4,144,128]{2,1,0:T(8,128)(2,1)S(1)}, bf16[4,144,128]{2,1,0:T(8,128)(2,1)S(1)}, u32[]{:S(2)}, u32[]{:S(2)}) collective-permute-start(bf16[4,144,128]{2,1,0:T(8,128)(2,1)S(1)} %fusion.57), channel_id=1, source_target_pairs={{0,128},{8,136},{16,144},{24,152},{32,160},{40,168},{48,176},{56,1... | collective-permute-start | bytes 442376 | tf_op jit(solution)/shard_map/ppermute | solution.py:39
  76.6 2.3 copy-start.4
  81.0 34.6 %copy-start.9 = (s32[128,2]{0,1:T(2,128)S(1)}, s32[128,2]{0,1:T(2,128)}, u32[]{:S(2)}) copy-start(s32[128,2]{0,1:T(2,128)} %param.37) | copy-start | bytes 3076
  81.0 27.2 %all-to-all-start = ((bf16[8,128,384]{2,1,0:T(8,128)(2,1)}), bf16[8,128,384]{2,1,0:T(8,128)(2,1)}, u32[]{:S(2)}, u32[]{:S(2)}) async-start(bf16[8,128,384]{2,1,0:T(8,128)(2,1)} %fusion.17), calls=%async_computation | async-start | bytes 1572864 | tf_op jit(solution)/shard_map/all_to_all | solution.py:134
  111.4 21.6 %all-to-all-start.1 = ((bf16[8,128,384]{2,1,0:T(8,128)(2,1)}), bf16[8,128,384]{2,1,0:T(8,128)(2,1)}, u32[]{:S(2)}, u32[]{:S(2)}) async-start(bf16[8,128,384]{2,1,0:T(8,128)(2,1)} %broadcast_in_dim.30), calls=%async_computation.1 | async-start | bytes 1572864 | tf_op jit(solution)/shard_map/all_to_all | solution.py:144
  124.4 0.6 copy-start.10
  125.6 10.8 %copy-start.8 = (f32[3072]{0:T(1024)S(1)}, f32[3072]{0:T(1024)}, u32[]{:S(2)}) copy-start(f32[3072]{0:T(1024)} %param.32) | copy-start | bytes 36868
  132.9 3.4 %copy-start.6 = (pred[512,128]{1,0:T(8,128)(4,1)S(1)}, pred[512,128]{1,0:T(8,128)(4,1)}, u32[]{:S(2)}) copy-start(pred[512,128]{1,0:T(8,128)(4,1)} %fusion.33) | copy-start | bytes 196612
  134.4 2.0 copy-start.1
  136.4 2.8 %copy-start.16 = (f32[128]{0:T(128)}, f32[128]{0:T(128)S(1)}, u32[]{:S(2)}) copy-start(f32[128]{0:T(128)S(1)} %add_rsqrt_fusion) | copy-start | bytes 1540
  139.1 51.5 %all-to-all-start.2 = ((bf16[32,16,3072]{2,1,0:T(8,128)(2,1)}), bf16[32,16,3072]{2,1,0:T(8,128)(2,1)}, u32[]{:S(2)}, u32[]{:S(2)}) async-start(bf16[32,16,3072]{2,1,0:T(8,128)(2,1)} %bitcast.184), calls=%async_computation.2 | async-start | bytes 6291456 | tf_op jit(solution)/shard_map/all_to_all | solution.py:166
  150.8 93.1 %reduce-scatter.2.cloned.1.call-start = ((), (), s32[]{:S(2)}) async-start(), calls=%async_computation.5 | async-start | bytes 3538944 | tf_op jit(solution)/shard_map/reduce_scatter | solution.py:183
  243.9 20.9 %all-to-all-start.3 = ((bf16[32,16,384]{2,1,0:T(8,128)(2,1)}), bf16[32,16,384]{2,1,0:T(8,128)(2,1)}, u32[]{:S(2)}, u32[]{:S(2)}) async-start(bf16[32,16,384]{2,1,0:T(8,128)(2,1)} %bitcast.192), calls=%async_computation.4 | async-start | bytes 786432 | tf_op jit(solution)/shard_map/all_to_all | solution.py:186
Sparse Core Ops, SparseCore 0:
  20.8 55.7 all-gather.2
  206.4 37.3 reduce-scatter.1

commit v11 on v10

--- a/solution.py
+++ b/solution.py
@@ -174,11 +174,15 @@
     gate_part = jnp.dot(flat_rows, w_gate[0], preferred_element_type=jnp.float32)
     up_part = jnp.dot(flat_rows, w_up[0], preferred_element_type=jnp.float32)
     hidden = (jax.nn.silu(gate_part) * up_part).astype(jnp.bfloat16)
-    partial_down = jnp.einsum(
-        "sf,fhj->hsj",
-        hidden,
-        w_down[0].reshape(w_down.shape[1], head_count, slice_width),
-        preferred_element_type=jnp.float32,
+    partial_down = jnp.stack(
+        [
+            jnp.dot(
+                hidden,
+                w_down[0][:, group * slice_width : (group + 1) * slice_width],
+                preferred_element_type=jnp.float32,
+            )
+            for group in range(head_count)
+        ]
     )
     summed = lax.psum_scatter(
         partial_down.astype(jnp.bfloat16), "head", scatter_dimension=0, tiled=True

time: 276 us -> 273 us (0.989)
  blocking collectives: 0 us -> 50.9 us
  waiting for transfers between devices: 111 us -> 74.9 us
  starting transfers between devices: 65.8 us -> 53.9 us
  local copies, waits for them, and re-layouts: 24 us -> 19.8 us
    all_to_all x0 -> x1, blocking collectives: none -> 50.9 us  [body(): lax.all_to_all(packed.reshape(experts_total, capacity, width_here), 'ctx'...]
    all_to_all x1 -> x0, waiting for transfers between devices: 35 us -> none  [body(): lax.all_to_all(packed.reshape(experts_total, capacity, width_here), 'ctx'...]
    all_to_all x1 -> x0, starting transfers between devices: 11.7 us -> none  [body(): lax.all_to_all(packed.reshape(experts_total, capacity, width_here), 'ctx'...]
    unnamed x41 -> x44, local copies, waits for them, and re-layouts: 9.65 us -> 5.44 us
    dot_general x1, matrix products: 6 us -> 2.05 us  [body(): jnp.dot(flat_rows, w_gate[0], preferred_element_type=jnp.float32)]
    dot_general x1 -> x9, matrix products: 9.69 us -> 12.9 us  [the longest x8 10.8 us: body(): jnp.dot(hidden, w_down[0][:, group * slice_width:(group + 1) * slice_widt...]
  transfers between devices with their start and end apart: 12 -> 11, of which waited for: 11 -> 10; matrix products, arithmetic and copies ran while one was open for 15% -> 14% of each run, Pallas kernels for 0% -> 0%
where the time goes in v11:
time: 273 us; the launch traced here: 271 us
  waiting for transfers between devices  74.9 us (27%)
  starting transfers between devices  53.9 us (20%)
  blocking collectives  50.9 us (19%)
  matrix products  29.6 us (11%)
  other arithmetic  28.4 us (10%)
  local copies, waits for them, and re-layouts  19.8 us (7%)
  between operations  13.8 us (5%)
    all_to_all x1, blocking collectives, body(): lax.all_to_all(packed.reshape(experts_total, capacity, width_here), 'ctx'...  50.9 us
    reduce_scatter x1, waiting for transfers between devices, body(): lax.psum_scatter(partial_down.astype(jnp.bfloat16), 'head', scatter_dimen...  35.3 us
    ppermute x6, starting transfers between devices, shifted(): return unpack(lax.ppermute(pack(value), axis, pairs))  29.5 us
    all_to_all x1, waiting for transfers between devices, body(): lax.all_to_all(partial_out.astype(jnp.bfloat16).transpose(1, 0, 2), 'head...  17.7 us
    dot_general x8, matrix products, body(): jnp.dot(hidden, w_down[0][:, group * slice_width:(group + 1) * slice_widt...  10.8 us
    all_to_all x1, starting transfers between devices, body(): lax.all_to_all(summed.reshape(experts_total, capacity, slice_width), 'ctx...  10.6 us
    all_to_all x1, starting transfers between devices, body(): lax.all_to_all(partial_out.astype(jnp.bfloat16).transpose(1, 0, 2), 'head...  9.52 us
    ppermute x6, waiting for transfers between devices, shifted(): return unpack(lax.ppermute(pack(value), axis, pairs))  7.29 us
  transfers between devices with their start and end apart: 11, of which 10 were waited for; matrix products, arithmetic and copies ran while one was open for 14% of the time, Pallas kernels for 0%

profile of v11, /device:TPU:1, one launch (start us, length us, event | category | flops | bytes accessed | tf_op | source)
XLA Modules:
  0.0 271.3 jit_solution(8845427463955231313)
XLA Ops:
  6.5 1.1 reduce_window_sum.26
  8.4 1.3 exponential_bitcast_fusion
  9.6 1.7 copy.157
  11.3 1.2 convolution_convert_fusion.10
  13.2 4.6 %collective-permute-start.1 = (bf16[4,144,128]{2,1,0:T(8,128)(2,1)}, bf16[4,144,128]{2,1,0:T(8,128)(2,1)}, u32[]{:S(2)}, u32[]{:S(2)}) collective-permute-start(bf16[4,144,128]{2,1,0:T(8,128)(2,1)} %fusion.67), channel_id=1, source_target_pairs={{0,16},{8,24},{16,32},{24,40},{32,48},{40,56},{48,64},{56,72},{64,... | collective-permute-start | bytes 442376 | tf_op jit(solution)/shard_map/ppermute | solution.py:39
  17.7 3.3 %collective-permute-start = (bf16[4,144,128]{2,1,0:T(8,128)(2,1)}, bf16[4,144,128]{2,1,0:T(8,128)(2,1)}, u32[]{:S(2)}, u32[]{:S(2)}) collective-permute-start(bf16[4,144,128]{2,1,0:T(8,128)(2,1)} %fusion.67), channel_id=1, source_target_pairs={{0,8},{8,16},{16,24},{24,32},{32,40},{40,48},{48,56},{56,64},{64,7... | collective-permute-start | bytes 442376 | tf_op jit(solution)/shard_map/ppermute | solution.py:39
  21.9 1.5 collective-permute-done
  27.8 2.8 %collective-permute-start.2 = (bf16[4,144,128]{2,1,0:T(8,128)(2,1)S(1)}, bf16[4,144,128]{2,1,0:T(8,128)(2,1)S(1)}, u32[]{:S(2)}, u32[]{:S(2)}) collective-permute-start(bf16[4,144,128]{2,1,0:T(8,128)(2,1)S(1)} %fusion.68), channel_id=1, source_target_pairs={{0,16},{8,24},{16,32},{24,40},{32,48},{40,56},{48,64},{56,72},{64,... | collective-permute-start | bytes 442376 | tf_op jit(solution)/shard_map/ppermute | solution.py:39
  30.7 2.1 collective-permute-done.2
  36.1 1.2 fusion.93
  37.3 5.3 %collective-permute-start.3 = (bf16[4,144,128]{2,1,0:T(8,128)(2,1)S(1)}, bf16[4,144,128]{2,1,0:T(8,128)(2,1)S(1)}, u32[]{:S(2)}, u32[]{:S(2)}) collective-permute-start(bf16[4,144,128]{2,1,0:T(8,128)(2,1)S(1)} %fusion.69), channel_id=1, source_target_pairs={{0,32},{8,40},{16,48},{24,56},{32,64},{40,72},{48,80},{56,88},{64,... | collective-permute-start | bytes 442376 | tf_op jit(solution)/shard_map/ppermute | solution.py:39
  42.6 1.2 add_exponential_fusion.2
  48.1 1.3 fusion.66
  49.4 7.5 %collective-permute-start.4 = (bf16[4,144,128]{2,1,0:T(8,128)(2,1)S(1)}, bf16[4,144,128]{2,1,0:T(8,128)(2,1)S(1)}, u32[]{:S(2)}, u32[]{:S(2)}) collective-permute-start(bf16[4,144,128]{2,1,0:T(8,128)(2,1)S(1)} %fusion.70), channel_id=1, source_target_pairs={{0,64},{8,72},{16,80},{24,88},{32,96},{40,104},{48,112},{56,120},{... | collective-permute-start | bytes 442376 | tf_op jit(solution)/shard_map/ppermute | solution.py:39
  57.6 1.9 collective-permute-done.4
  62.9 1.4 fusion.92
  64.3 5.9 %collective-permute-start.5 = (bf16[4,144,128]{2,1,0:T(8,128)(2,1)S(1)}, bf16[4,144,128]{2,1,0:T(8,128)(2,1)S(1)}, u32[]{:S(2)}, u32[]{:S(2)}) collective-permute-start(bf16[4,144,128]{2,1,0:T(8,128)(2,1)S(1)} %fusion.71), channel_id=1, source_target_pairs={{0,128},{8,136},{16,144},{24,152},{32,160},{40,168},{48,176},{56,1... | collective-permute-start | bytes 442376 | tf_op jit(solution)/shard_map/ppermute | solution.py:39
  70.2 1.1 convolution_multiply_fusion
  72.3 1.7 fusion.59
  75.2 1.5 fusion.58
  76.9 2.3 copy.197
  79.3 2.1 fusion.13
  81.4 9.5 %all-to-all-start = ((bf16[8,128,384]{2,1,0:T(8,128)(2,1)}), bf16[8,128,384]{2,1,0:T(8,128)(2,1)}, u32[]{:S(2)}, u32[]{:S(2)}) async-start(bf16[8,128,384]{2,1,0:T(8,128)(2,1)} %fusion.13), calls=%async_computation | async-start | bytes 1572864 | tf_op jit(solution)/shard_map/all_to_all | solution.py:134
  90.9 17.7 %all-to-all-done = bf16[8,128,384]{2,1,0:T(8,128)(2,1)} async-done(((bf16[8,128,384]{2,1,0:T(8,128)(2,1)}), bf16[8,128,384]{2,1,0:T(8,128)(2,1)}, u32[]{:S(2)}, u32[]{:S(2)}) %all-to-all-start) | async-done | bytes 786464 | tf_op jit(solution)/shard_map/all_to_all | solution.py:134
  108.6 1.3 convert_reduce_fusion
  111.7 4.2 %all-to-all-start.1 = ((bf16[8,128,384]{2,1,0:T(8,128)(2,1)}), bf16[8,128,384]{2,1,0:T(8,128)(2,1)}, u32[]{:S(2)}, u32[]{:S(2)}) async-start(bf16[8,128,384]{2,1,0:T(8,128)(2,1)} %broadcast_in_dim.30), calls=%async_computation.1 | async-start | bytes 1572864 | tf_op jit(solution)/shard_map/all_to_all | solution.py:144
  119.3 1.9 reduce-window.6
  126.0 7.3 %all-to-all-done.1 = bf16[8,128,384]{2,1,0:T(8,128)(2,1)} async-done(((bf16[8,128,384]{2,1,0:T(8,128)(2,1)}), bf16[8,128,384]{2,1,0:T(8,128)(2,1)}, u32[]{:S(2)}, u32[]{:S(2)}) %all-to-all-start.1) | async-done | bytes 786464 | tf_op jit(solution)/shard_map/all_to_all | solution.py:144
  133.3 1.3 convert_bitcast_fusion
  134.7 1.9 fusion.4
  137.8 50.9 %all_to_all.20 = bf16[32,16,3072]{2,1,0:T(8,128)(2,1)S(1)} all-to-all(bf16[32,16,3072]{2,1,0:T(8,128)(2,1)S(1)} %bitcast.212), channel_id=1, replica_groups=mesh['ctx'=32,'head'=8] {'ctx'}, dimensions={0} | all-to-all | bytes 6291456 | tf_op jit(solution)/shard_map/all_to_all | solution.py:166
  188.7 2.0 fusion.2
  190.8 2.1 fusion.10
  193.0 1.3 fusion.15
  194.3 1.3 fusion.17
  195.6 1.3 fusion.19
  197.0 1.4 fusion.21
  198.3 1.3 fusion.23
  199.7 1.4 fusion.25
  201.0 1.3 fusion.27
  202.4 1.4 fusion.29
  203.8 1.3 slice_bitcast_fusion
  205.0 35.3 %reduce-scatter.2.cloned.1.call-done = bf16[1,512,384]{2,1,0:T(8,128)(2,1)} async-done(((bf16[8,512,384]{2,1,0:T(8,128)(2,1)}), bf16[1,512,384]{2,1,0:T(8,128)(2,1)}) %reduce-scatter.2.cloned.1.call-update) | async-done | bytes 393232 | tf_op jit(solution)/shard_map/reduce_scatter | solution.py:187
  240.4 10.6 %all-to-all-start.3 = ((bf16[32,16,384]{2,1,0:T(8,128)(2,1)}), bf16[32,16,384]{2,1,0:T(8,128)(2,1)}, u32[]{:S(2)}, u32[]{:S(2)}) async-start(bf16[32,16,384]{2,1,0:T(8,128)(2,1)} %bitcast.220), calls=%async_computation.4 | async-start | bytes 786432 | tf_op jit(solution)/shard_map/all_to_all | solution.py:190
  251.0 3.1 %fusion.33 = f32[128,32]{0,1:T(8,128)S(1)} fusion(f32[3072,32]{0,1:T(8,128)} %param.33, f32[128,3072]{1,0:T(8,128)} %bitcast.210, f32[3072]{0:T(1024)S(1)} %copy-done.8, f32[128]{0:T(128)} %copy-done.16), kind=kOutput, calls=%fused_computation.48 | convolution fusion | flops 151392256 | bytes 1995264 | tf_op jit(solution)/shard_map/dot_general | solution.py:156
  254.1 7.1 %all-to-all-done.3 = bf16[32,16,384]{2,1,0:T(8,128)(2,1)} async-done(((bf16[32,16,384]{2,1,0:T(8,128)(2,1)}), bf16[32,16,384]{2,1,0:T(8,128)(2,1)}, u32[]{:S(2)}, u32[]{:S(2)}) %all-to-all-start.3) | async-done | bytes 393248 | tf_op jit(solution)/shard_map/all_to_all | solution.py:190
  261.2 1.3 fusion.31
  262.5 1.9 fusion.32
  (105 shorter events, 31.9 us)
Async XLA Ops:
  6.5 182.2 %copy-start = (bf16[1,3072,576]{1,2,0:T(8,128)(2,1)S(1)}, bf16[1,3072,576]{1,2,0:T(8,128)(2,1)}, u32[]{:S(2)}) copy-start(bf16[1,3072,576]{1,2,0:T(8,128)(2,1)} %param.34) | copy-start | bytes 10616836
  6.5 70.4 %all-gather.3.cloned.1.call-start = ((), (), s32[]{:S(2)}) async-start(), calls=%async_computation.6 | async-start | bytes 3244032 | tf_op jit(solution)/shard_map/all_gather | solution.py:125
  7.8 0.5 copy-start.12
  13.2 7.9 %collective-permute-start.1 = (bf16[4,144,128]{2,1,0:T(8,128)(2,1)}, bf16[4,144,128]{2,1,0:T(8,128)(2,1)}, u32[]{:S(2)}, u32[]{:S(2)}) collective-permute-start(bf16[4,144,128]{2,1,0:T(8,128)(2,1)} %fusion.67), channel_id=1, source_target_pairs={{0,16},{8,24},{16,32},{24,40},{32,48},{40,56},{48,64},{56,72},{64,... | collective-permute-start | bytes 442376 | tf_op jit(solution)/shard_map/ppermute | solution.py:39
  17.7 5.7 %collective-permute-start = (bf16[4,144,128]{2,1,0:T(8,128)(2,1)}, bf16[4,144,128]{2,1,0:T(8,128)(2,1)}, u32[]{:S(2)}, u32[]{:S(2)}) collective-permute-start(bf16[4,144,128]{2,1,0:T(8,128)(2,1)} %fusion.67), channel_id=1, source_target_pairs={{0,8},{8,16},{16,24},{24,32},{32,40},{40,48},{48,56},{56,64},{64,7... | collective-permute-start | bytes 442376 | tf_op jit(solution)/shard_map/ppermute | solution.py:39
  24.8 0.5 copy-start.13
  27.8 4.9 %collective-permute-start.2 = (bf16[4,144,128]{2,1,0:T(8,128)(2,1)S(1)}, bf16[4,144,128]{2,1,0:T(8,128)(2,1)S(1)}, u32[]{:S(2)}, u32[]{:S(2)}) collective-permute-start(bf16[4,144,128]{2,1,0:T(8,128)(2,1)S(1)} %fusion.68), channel_id=1, source_target_pairs={{0,16},{8,24},{16,32},{24,40},{32,48},{40,56},{48,64},{56,72},{64,... | collective-permute-start | bytes 442376 | tf_op jit(solution)/shard_map/ppermute | solution.py:39
  32.8 0.6 copy-start.2
  33.5 0.6 copy-start.14
  34.2 0.6 copy-start.18
  37.3 7.4 %collective-permute-start.3 = (bf16[4,144,128]{2,1,0:T(8,128)(2,1)S(1)}, bf16[4,144,128]{2,1,0:T(8,128)(2,1)S(1)}, u32[]{:S(2)}, u32[]{:S(2)}) collective-permute-start(bf16[4,144,128]{2,1,0:T(8,128)(2,1)S(1)} %fusion.69), channel_id=1, source_target_pairs={{0,32},{8,40},{16,48},{24,56},{32,64},{40,72},{48,80},{56,88},{64,... | collective-permute-start | bytes 442376 | tf_op jit(solution)/shard_map/ppermute | solution.py:39
  44.7 0.7 copy-start.5
  45.5 0.7 copy-start.15
  46.2 0.6 copy-start.17
  49.4 10.0 %collective-permute-start.4 = (bf16[4,144,128]{2,1,0:T(8,128)(2,1)S(1)}, bf16[4,144,128]{2,1,0:T(8,128)(2,1)S(1)}, u32[]{:S(2)}, u32[]{:S(2)}) collective-permute-start(bf16[4,144,128]{2,1,0:T(8,128)(2,1)S(1)} %fusion.70), channel_id=1, source_target_pairs={{0,64},{8,72},{16,80},{24,88},{32,96},{40,104},{48,112},{56,120},{... | collective-permute-start | bytes 442376 | tf_op jit(solution)/shard_map/ppermute | solution.py:39
  59.4 0.7 copy-start.7
  60.2 0.7 copy-start.11
  62.2 11.9 %copy-start.3 = (bf16[128,512]{1,0:T(8,128)(2,1)S(1)}, bf16[128,512]{1,0:T(8,128)(2,1)}, u32[]{:S(2)}) copy-start(bf16[128,512]{1,0:T(8,128)(2,1)} %param.27) | copy-start | bytes 393220
  64.3 8.0 %collective-permute-start.5 = (bf16[4,144,128]{2,1,0:T(8,128)(2,1)S(1)}, bf16[4,144,128]{2,1,0:T(8,128)(2,1)S(1)}, u32[]{:S(2)}, u32[]{:S(2)}) collective-permute-start(bf16[4,144,128]{2,1,0:T(8,128)(2,1)S(1)} %fusion.71), channel_id=1, source_target_pairs={{0,128},{8,136},{16,144},{24,152},{32,160},{40,168},{48,176},{56,1... | collective-permute-start | bytes 442376 | tf_op jit(solution)/shard_map/ppermute | solution.py:39
  76.9 2.3 copy-start.4
  81.4 34.6 %copy-start.9 = (s32[128,2]{0,1:T(2,128)S(1)}, s32[128,2]{0,1:T(2,128)}, u32[]{:S(2)}) copy-start(s32[128,2]{0,1:T(2,128)} %param.37) | copy-start | bytes 3076
  81.4 27.2 %all-to-all-start = ((bf16[8,128,384]{2,1,0:T(8,128)(2,1)}), bf16[8,128,384]{2,1,0:T(8,128)(2,1)}, u32[]{:S(2)}, u32[]{:S(2)}) async-start(bf16[8,128,384]{2,1,0:T(8,128)(2,1)} %fusion.13), calls=%async_computation | async-start | bytes 1572864 | tf_op jit(solution)/shard_map/all_to_all | solution.py:134
  111.7 21.6 %all-to-all-start.1 = ((bf16[8,128,384]{2,1,0:T(8,128)(2,1)}), bf16[8,128,384]{2,1,0:T(8,128)(2,1)}, u32[]{:S(2)}, u32[]{:S(2)}) async-start(bf16[8,128,384]{2,1,0:T(8,128)(2,1)} %broadcast_in_dim.30), calls=%async_computation.1 | async-start | bytes 1572864 | tf_op jit(solution)/shard_map/all_to_all | solution.py:144
  116.0 124.4 %reduce-scatter.2.cloned.1.call-start = ((), (), s32[]{:S(2)}) async-start(), calls=%async_computation.5 | async-start | bytes 3538944 | tf_op jit(solution)/shard_map/reduce_scatter | solution.py:187
  124.7 0.6 copy-start.10
  126.0 10.7 %copy-start.8 = (f32[3072]{0:T(1024)S(1)}, f32[3072]{0:T(1024)}, u32[]{:S(2)}) copy-start(f32[3072]{0:T(1024)} %param.32) | copy-start | bytes 36868
  133.3 3.4 %copy-start.6 = (pred[512,128]{1,0:T(8,128)(4,1)S(1)}, pred[512,128]{1,0:T(8,128)(4,1)}, u32[]{:S(2)}) copy-start(pred[512,128]{1,0:T(8,128)(4,1)} %fusion.39) | copy-start | bytes 196612
  134.7 54.0 %copy-start.1 = (f32[8,16,8,384]{3,2,0,1:T(8,128)}, f32[8,16,8,384]{3,2,0,1:T(8,128)S(1)}, u32[]{:S(2)}) copy-start(f32[8,16,8,384]{3,2,0,1:T(8,128)S(1)} %copy.175) | copy-start | bytes 4718596
  136.7 1.1 copy-start.16
  188.7 2.1 copy-start.19
  190.8 2.2 copy-start.20
  240.4 20.9 %all-to-all-start.3 = ((bf16[32,16,384]{2,1,0:T(8,128)(2,1)}), bf16[32,16,384]{2,1,0:T(8,128)(2,1)}, u32[]{:S(2)}, u32[]{:S(2)}) async-start(bf16[32,16,384]{2,1,0:T(8,128)(2,1)} %bitcast.220), calls=%async_computation.4 | async-start | bytes 786432 | tf_op jit(solution)/shard_map/all_to_all | solution.py:190
Sparse Core Ops, SparseCore 0:
  21.2 55.6 all-gather.2
  203.9 36.4 reduce-scatter.1

commit v12 on v11

--- a/solution.py
+++ b/solution.py
@@ -122,17 +122,24 @@
     )
     ctx_size = lax.axis_size("ctx")
     head_count = lax.axis_size("head")
-    weight_blocks = lax.all_gather(out_weight, "ctx")
+    weight_blocks = lax.all_gather(out_weight, "ctx", axis=1, tiled=True)
     model_width = residual.shape[1]
     experts_total = router.shape[1]
     capacity = 2 * token_count * TOP // experts_total
     slice_width = model_width // head_count
     slice_start = lax.axis_index("head") * slice_width
-    partial_out = jnp.einsum(
-        "tk,ckd->tcd", heads_normed, weight_blocks, preferred_element_type=jnp.float32
-    ).reshape(token_count, head_count, slice_width)
+    partial_out = jnp.stack(
+        [
+            jnp.dot(
+                heads_normed,
+                weight_blocks[:, group * slice_width : (group + 1) * slice_width],
+                preferred_element_type=jnp.float32,
+            )
+            for group in range(head_count)
+        ]
+    )
     pieces = lax.all_to_all(
-        partial_out.astype(jnp.bfloat16).transpose(1, 0, 2),
+        partial_out.astype(jnp.bfloat16),
         "head",
         split_axis=0,
         concat_axis=0,

time: 273 us -> 284 us (1.040)
  matrix products: 29.6 us -> 43.4 us
    dot_general x1 -> x8, matrix products: 2.06 us -> 15.9 us  [body(): jnp.dot(heads_normed, weight_blocks[:, group * slice_width:(group + 1) *...]
  transfers between devices with their start and end apart: 11 -> 11, of which waited for: 10 -> 9; matrix products, arithmetic and copies ran while one was open for 14% -> 13% of each run, Pallas kernels for 0% -> 0%
where the time goes in v12:
time: 284 us; the launch traced here: 283 us
  waiting for transfers between devices  76 us (27%)
  starting transfers between devices  53 us (19%)
  blocking collectives  50.5 us (18%)
  matrix products  43.4 us (15%)
  other arithmetic  28.4 us (10%)
  local copies, waits for them, and re-layouts  17.4 us (6%)
  between operations  13.8 us (5%)
    all_to_all x1, blocking collectives, body(): lax.all_to_all(packed.reshape(experts_total, capacity, width_here), 'ctx'...  50.5 us
    reduce_scatter x1, waiting for transfers between devices, body(): lax.psum_scatter(partial_down.astype(jnp.bfloat16), 'head', scatter_dimen...  35.9 us
    ppermute x6, starting transfers between devices, shifted(): return unpack(lax.ppermute(pack(value), axis, pairs))  28.9 us
    all_to_all x1, waiting for transfers between devices, body(): lax.all_to_all(partial_out.astype(jnp.bfloat16), 'head', split_axis=0, co...  17.3 us
    dot_general x8, matrix products, body(): jnp.dot(heads_normed, weight_blocks[:, group * slice_width:(group + 1) *...  15.9 us
    dot_general x8, matrix products, body(): jnp.dot(hidden, w_down[0][:, group * slice_width:(group + 1) * slice_widt...  10.8 us
    all_to_all x1, starting transfers between devices, body(): lax.all_to_all(summed.reshape(experts_total, capacity, slice_width), 'ctx...  10.7 us
    all_to_all x1, starting transfers between devices, body(): lax.all_to_all(partial_out.astype(jnp.bfloat16), 'head', split_axis=0, co...  9.18 us
  transfers between devices with their start and end apart: 11, of which 9 were waited for; matrix products, arithmetic and copies ran while one was open for 13% of the time, Pallas kernels for 0%

profile of v12, /device:TPU:1, one launch (start us, length us, event | category | flops | bytes accessed | tf_op | source)
XLA Modules:
  0.0 282.5 jit_solution(14351675712318383603)
XLA Ops:
  9.6 1.7 copy.144
  13.2 4.6 %collective-permute-start.1 = (bf16[4,144,128]{2,1,0:T(8,128)(2,1)}, bf16[4,144,128]{2,1,0:T(8,128)(2,1)}, u32[]{:S(2)}, u32[]{:S(2)}) collective-permute-start(bf16[4,144,128]{2,1,0:T(8,128)(2,1)} %fusion.90), channel_id=1, source_target_pairs={{0,16},{8,24},{16,32},{24,40},{32,48},{40,56},{48,64},{56,72},{64,... | collective-permute-start | bytes 442376 | tf_op jit(solution)/shard_map/ppermute | solution.py:39
  17.7 3.3 %collective-permute-start = (bf16[4,144,128]{2,1,0:T(8,128)(2,1)}, bf16[4,144,128]{2,1,0:T(8,128)(2,1)}, u32[]{:S(2)}, u32[]{:S(2)}) collective-permute-start(bf16[4,144,128]{2,1,0:T(8,128)(2,1)} %fusion.90), channel_id=1, source_target_pairs={{0,8},{8,16},{16,24},{24,32},{32,40},{40,48},{48,56},{56,64},{64,7... | collective-permute-start | bytes 442376 | tf_op jit(solution)/shard_map/ppermute | solution.py:39
  21.9 1.5 collective-permute-done
  27.8 2.8 %collective-permute-start.2 = (bf16[4,144,128]{2,1,0:T(8,128)(2,1)S(1)}, bf16[4,144,128]{2,1,0:T(8,128)(2,1)S(1)}, u32[]{:S(2)}, u32[]{:S(2)}) collective-permute-start(bf16[4,144,128]{2,1,0:T(8,128)(2,1)S(1)} %fusion.91), channel_id=1, source_target_pairs={{0,16},{8,24},{16,32},{24,40},{32,48},{40,56},{48,64},{56,72},{64,... | collective-permute-start | bytes 442376 | tf_op jit(solution)/shard_map/ppermute | solution.py:39
  30.7 2.1 collective-permute-done.2
  37.3 5.3 %collective-permute-start.3 = (bf16[4,144,128]{2,1,0:T(8,128)(2,1)S(1)}, bf16[4,144,128]{2,1,0:T(8,128)(2,1)S(1)}, u32[]{:S(2)}, u32[]{:S(2)}) collective-permute-start(bf16[4,144,128]{2,1,0:T(8,128)(2,1)S(1)} %fusion.92), channel_id=1, source_target_pairs={{0,32},{8,40},{16,48},{24,56},{32,64},{40,72},{48,80},{56,88},{64,... | collective-permute-start | bytes 442376 | tf_op jit(solution)/shard_map/ppermute | solution.py:39
  48.4 1.3 fusion.89
  49.6 7.5 %collective-permute-start.4 = (bf16[4,144,128]{2,1,0:T(8,128)(2,1)S(1)}, bf16[4,144,128]{2,1,0:T(8,128)(2,1)S(1)}, u32[]{:S(2)}, u32[]{:S(2)}) collective-permute-start(bf16[4,144,128]{2,1,0:T(8,128)(2,1)S(1)} %fusion.93), channel_id=1, source_target_pairs={{0,64},{8,72},{16,80},{24,88},{32,96},{40,104},{48,112},{56,120},{... | collective-permute-start | bytes 442376 | tf_op jit(solution)/shard_map/ppermute | solution.py:39
  57.8 3.0 %collective-permute-done.4 = bf16[4,144,128]{2,1,0:T(8,128)(2,1)S(1)} collective-permute-done((bf16[4,144,128]{2,1,0:T(8,128)(2,1)S(1)}, bf16[4,144,128]{2,1,0:T(8,128)(2,1)S(1)}, u32[]{:S(2)}, u32[]{:S(2)}) %collective-permute-start.4) | collective-permute-done | bytes 147488 | tf_op jit(solution)/shard_map/ppermute | solution.py:39
  64.3 1.4 fusion.115
  65.7 5.3 %collective-permute-start.5 = (bf16[4,144,128]{2,1,0:T(8,128)(2,1)S(1)}, bf16[4,144,128]{2,1,0:T(8,128)(2,1)S(1)}, u32[]{:S(2)}, u32[]{:S(2)}) collective-permute-start(bf16[4,144,128]{2,1,0:T(8,128)(2,1)S(1)} %fusion.94), channel_id=1, source_target_pairs={{0,128},{8,136},{16,144},{24,152},{32,160},{40,168},{48,176},{56,1... | collective-permute-start | bytes 442376 | tf_op jit(solution)/shard_map/ppermute | solution.py:39
  73.1 1.7 fusion.82
  76.0 1.5 fusion.81
  77.5 2.0 fusion.33
  79.5 2.0 fusion.35
  81.5 2.0 fusion.37
  83.5 2.0 fusion.39
  85.5 2.0 fusion.41
  87.5 1.9 fusion.43
  89.5 1.9 fusion.45
  91.4 1.9 fusion.47
  93.4 9.2 %all-to-all-start = ((bf16[8,128,384]{2,1,0:T(8,128)(2,1)}), bf16[8,128,384]{2,1,0:T(8,128)(2,1)}, u32[]{:S(2)}, u32[]{:S(2)}) async-start(bf16[8,128,384]{2,1,0:T(8,128)(2,1)} %fusion.47), calls=%async_computation | async-start | bytes 1572864 | tf_op jit(solution)/shard_map/all_to_all | solution.py:141
  102.5 17.3 %all-to-all-done = bf16[8,128,384]{2,1,0:T(8,128)(2,1)} async-done(((bf16[8,128,384]{2,1,0:T(8,128)(2,1)}), bf16[8,128,384]{2,1,0:T(8,128)(2,1)}, u32[]{:S(2)}, u32[]{:S(2)}) %all-to-all-start) | async-done | bytes 786464 | tf_op jit(solution)/shard_map/all_to_all | solution.py:141
  119.9 1.3 convert_reduce_fusion
  123.0 4.2 %all-to-all-start.1 = ((bf16[8,128,384]{2,1,0:T(8,128)(2,1)}), bf16[8,128,384]{2,1,0:T(8,128)(2,1)}, u32[]{:S(2)}, u32[]{:S(2)}) async-start(bf16[8,128,384]{2,1,0:T(8,128)(2,1)} %broadcast_in_dim.30), calls=%async_computation.1 | async-start | bytes 1572864 | tf_op jit(solution)/shard_map/all_to_all | solution.py:151
  130.6 1.9 reduce-window.6
  137.3 7.0 %all-to-all-done.1 = bf16[8,128,384]{2,1,0:T(8,128)(2,1)} async-done(((bf16[8,128,384]{2,1,0:T(8,128)(2,1)}), bf16[8,128,384]{2,1,0:T(8,128)(2,1)}, u32[]{:S(2)}, u32[]{:S(2)}) %all-to-all-start.1) | async-done | bytes 786464 | tf_op jit(solution)/shard_map/all_to_all | solution.py:151
  144.3 1.3 convert_bitcast_fusion
  145.8 1.9 fusion.4
  148.8 50.5 %all_to_all.20 = bf16[32,16,3072]{2,1,0:T(8,128)(2,1)S(1)} all-to-all(bf16[32,16,3072]{2,1,0:T(8,128)(2,1)S(1)} %bitcast.239), channel_id=1, replica_groups=mesh['ctx'=32,'head'=8] {'ctx'}, dimensions={0} | all-to-all | bytes 6291456 | tf_op jit(solution)/shard_map/all_to_all | solution.py:173
  199.3 2.0 fusion.2
  201.4 2.1 fusion.10
  203.5 1.3 fusion.14
  204.9 1.3 fusion.16
  206.2 1.3 fusion.18
  207.5 1.4 fusion.20
  208.9 1.3 fusion.22
  210.2 1.4 fusion.24
  211.6 1.3 fusion.26
  212.9 1.4 fusion.28
  214.3 1.3 slice_bitcast_fusion
  215.6 35.9 %reduce-scatter.2.cloned.1.call-done = bf16[1,512,384]{2,1,0:T(8,128)(2,1)} async-done(((bf16[8,512,384]{2,1,0:T(8,128)(2,1)}), bf16[1,512,384]{2,1,0:T(8,128)(2,1)}) %reduce-scatter.2.cloned.1.call-update) | async-done | bytes 393232 | tf_op jit(solution)/shard_map/reduce_scatter | solution.py:194
  251.5 10.7 %all-to-all-start.3 = ((bf16[32,16,384]{2,1,0:T(8,128)(2,1)}), bf16[32,16,384]{2,1,0:T(8,128)(2,1)}, u32[]{:S(2)}, u32[]{:S(2)}) async-start(bf16[32,16,384]{2,1,0:T(8,128)(2,1)} %bitcast.244), calls=%async_computation.4 | async-start | bytes 786432 | tf_op jit(solution)/shard_map/all_to_all | solution.py:197
  262.2 3.1 %fusion.48 = f32[128,32]{0,1:T(8,128)S(1)} fusion(f32[3072,32]{0,1:T(8,128)} %param.33, f32[128,3072]{1,0:T(8,128)} %bitcast.237, f32[3072]{0:T(1024)S(1)} %copy-done.8, f32[128]{0:T(128)} %copy-done.16), kind=kOutput, calls=%fused_computation.69 | convolution fusion | flops 151392256 | bytes 1995264 | tf_op jit(solution)/shard_map/dot_general | solution.py:163
  265.4 7.1 %all-to-all-done.3 = bf16[32,16,384]{2,1,0:T(8,128)(2,1)} async-done(((bf16[32,16,384]{2,1,0:T(8,128)(2,1)}), bf16[32,16,384]{2,1,0:T(8,128)(2,1)}, u32[]{:S(2)}, u32[]{:S(2)}) %all-to-all-start.3) | async-done | bytes 393248 | tf_op jit(solution)/shard_map/all_to_all | solution.py:197
  272.4 1.3 fusion.30
  273.8 1.9 fusion.31
  (111 shorter events, 39.1 us)
Async XLA Ops:
  6.5 192.8 %copy-start = (bf16[1,3072,576]{1,2,0:T(8,128)(2,1)S(1)}, bf16[1,3072,576]{1,2,0:T(8,128)(2,1)}, u32[]{:S(2)}) copy-start(bf16[1,3072,576]{1,2,0:T(8,128)(2,1)} %param.34) | copy-start | bytes 10616836
  6.5 71.0 %all-gather.2.cloned.1.call-start = ((), (), s32[]{:S(2)}) async-start(), calls=%async_computation.5 | async-start | bytes 3244032 | tf_op jit(solution)/shard_map/all_gather | solution.py:125
  7.8 0.5 copy-start.12
  13.2 7.9 %collective-permute-start.1 = (bf16[4,144,128]{2,1,0:T(8,128)(2,1)}, bf16[4,144,128]{2,1,0:T(8,128)(2,1)}, u32[]{:S(2)}, u32[]{:S(2)}) collective-permute-start(bf16[4,144,128]{2,1,0:T(8,128)(2,1)} %fusion.90), channel_id=1, source_target_pairs={{0,16},{8,24},{16,32},{24,40},{32,48},{40,56},{48,64},{56,72},{64,... | collective-permute-start | bytes 442376 | tf_op jit(solution)/shard_map/ppermute | solution.py:39
  17.7 5.7 %collective-permute-start = (bf16[4,144,128]{2,1,0:T(8,128)(2,1)}, bf16[4,144,128]{2,1,0:T(8,128)(2,1)}, u32[]{:S(2)}, u32[]{:S(2)}) collective-permute-start(bf16[4,144,128]{2,1,0:T(8,128)(2,1)} %fusion.90), channel_id=1, source_target_pairs={{0,8},{8,16},{16,24},{24,32},{32,40},{40,48},{48,56},{56,64},{64,7... | collective-permute-start | bytes 442376 | tf_op jit(solution)/shard_map/ppermute | solution.py:39
  24.8 0.5 copy-start.13
  27.8 4.9 %collective-permute-start.2 = (bf16[4,144,128]{2,1,0:T(8,128)(2,1)S(1)}, bf16[4,144,128]{2,1,0:T(8,128)(2,1)S(1)}, u32[]{:S(2)}, u32[]{:S(2)}) collective-permute-start(bf16[4,144,128]{2,1,0:T(8,128)(2,1)S(1)} %fusion.91), channel_id=1, source_target_pairs={{0,16},{8,24},{16,32},{24,40},{32,48},{40,56},{48,64},{56,72},{64,... | collective-permute-start | bytes 442376 | tf_op jit(solution)/shard_map/ppermute | solution.py:39
  32.8 0.6 copy-start.2
  33.5 0.6 copy-start.14
  34.2 0.6 copy-start.18
  37.3 7.7 %collective-permute-start.3 = (bf16[4,144,128]{2,1,0:T(8,128)(2,1)S(1)}, bf16[4,144,128]{2,1,0:T(8,128)(2,1)S(1)}, u32[]{:S(2)}, u32[]{:S(2)}) collective-permute-start(bf16[4,144,128]{2,1,0:T(8,128)(2,1)S(1)} %fusion.92), channel_id=1, source_target_pairs={{0,32},{8,40},{16,48},{24,56},{32,64},{40,72},{48,80},{56,88},{64,... | collective-permute-start | bytes 442376 | tf_op jit(solution)/shard_map/ppermute | solution.py:39
  45.0 0.7 copy-start.4
  45.7 0.7 copy-start.15
  46.4 0.6 copy-start.17
  49.6 11.1 %collective-permute-start.4 = (bf16[4,144,128]{2,1,0:T(8,128)(2,1)S(1)}, bf16[4,144,128]{2,1,0:T(8,128)(2,1)S(1)}, u32[]{:S(2)}, u32[]{:S(2)}) collective-permute-start(bf16[4,144,128]{2,1,0:T(8,128)(2,1)S(1)} %fusion.93), channel_id=1, source_target_pairs={{0,64},{8,72},{16,80},{24,88},{32,96},{40,104},{48,112},{56,120},{... | collective-permute-start | bytes 442376 | tf_op jit(solution)/shard_map/ppermute | solution.py:39
  60.8 0.7 copy-start.7
  61.6 0.7 copy-start.11
  63.6 11.3 %copy-start.3 = (bf16[128,512]{1,0:T(8,128)(2,1)S(1)}, bf16[128,512]{1,0:T(8,128)(2,1)}, u32[]{:S(2)}) copy-start(bf16[128,512]{1,0:T(8,128)(2,1)} %param.27) | copy-start | bytes 393220
  65.7 7.4 %collective-permute-start.5 = (bf16[4,144,128]{2,1,0:T(8,128)(2,1)S(1)}, bf16[4,144,128]{2,1,0:T(8,128)(2,1)S(1)}, u32[]{:S(2)}, u32[]{:S(2)}) collective-permute-start(bf16[4,144,128]{2,1,0:T(8,128)(2,1)S(1)} %fusion.94), channel_id=1, source_target_pairs={{0,128},{8,136},{16,144},{24,152},{32,160},{40,168},{48,176},{56,1... | collective-permute-start | bytes 442376 | tf_op jit(solution)/shard_map/ppermute | solution.py:39
  77.5 10.0 %copy-start.6 = (bf16[128,4,128]{0,2,1:T(8,128)(2,1)S(1)}, bf16[128,4,128]{0,2,1:T(8,128)(2,1)}, u32[]{:S(2)}) copy-start(bf16[128,4,128]{0,2,1:T(8,128)(2,1)} %fusion.81) | copy-start | bytes 393220
  91.4 35.9 %copy-start.9 = (s32[128,2]{0,1:T(2,128)S(1)}, s32[128,2]{0,1:T(2,128)}, u32[]{:S(2)}) copy-start(s32[128,2]{0,1:T(2,128)} %param.37) | copy-start | bytes 3076
  93.4 26.5 %all-to-all-start = ((bf16[8,128,384]{2,1,0:T(8,128)(2,1)}), bf16[8,128,384]{2,1,0:T(8,128)(2,1)}, u32[]{:S(2)}, u32[]{:S(2)}) async-start(bf16[8,128,384]{2,1,0:T(8,128)(2,1)} %fusion.47), calls=%async_computation | async-start | bytes 1572864 | tf_op jit(solution)/shard_map/all_to_all | solution.py:141
  123.0 21.3 %all-to-all-start.1 = ((bf16[8,128,384]{2,1,0:T(8,128)(2,1)}), bf16[8,128,384]{2,1,0:T(8,128)(2,1)}, u32[]{:S(2)}, u32[]{:S(2)}) async-start(bf16[8,128,384]{2,1,0:T(8,128)(2,1)} %broadcast_in_dim.30), calls=%async_computation.1 | async-start | bytes 1572864 | tf_op jit(solution)/shard_map/all_to_all | solution.py:151
  127.2 124.3 %reduce-scatter.2.cloned.1.call-start = ((), (), s32[]{:S(2)}) async-start(), calls=%async_computation.6 | async-start | bytes 3538944 | tf_op jit(solution)/shard_map/reduce_scatter | solution.py:194
  136.0 0.6 copy-start.10
  137.3 10.4 %copy-start.8 = (f32[3072]{0:T(1024)S(1)}, f32[3072]{0:T(1024)}, u32[]{:S(2)}) copy-start(f32[3072]{0:T(1024)} %param.32) | copy-start | bytes 36868
  144.3 3.4 %copy-start.5 = (pred[512,128]{1,0:T(8,128)(4,1)S(1)}, pred[512,128]{1,0:T(8,128)(4,1)}, u32[]{:S(2)}) copy-start(pred[512,128]{1,0:T(8,128)(4,1)} %fusion.54) | copy-start | bytes 196612
  145.8 53.5 %copy-start.1 = (f32[8,16,8,384]{3,2,0,1:T(8,128)}, f32[8,16,8,384]{3,2,0,1:T(8,128)S(1)}, u32[]{:S(2)}) copy-start(f32[8,16,8,384]{3,2,0,1:T(8,128)S(1)} %copy.160) | copy-start | bytes 4718596
  147.7 1.1 copy-start.16
  199.3 2.1 copy-start.19
  201.4 2.2 copy-start.20
  251.5 20.9 %all-to-all-start.3 = ((bf16[32,16,384]{2,1,0:T(8,128)(2,1)}), bf16[32,16,384]{2,1,0:T(8,128)(2,1)}, u32[]{:S(2)}, u32[]{:S(2)}) async-start(bf16[32,16,384]{2,1,0:T(8,128)(2,1)} %bitcast.244), calls=%async_computation.4 | async-start | bytes 786432 | tf_op jit(solution)/shard_map/all_to_all | solution.py:197
Sparse Core Ops, SparseCore 0:
  21.2 53.2 all-gather.1
  214.4 37.0 reduce-scatter.1
